TPU v7x, 128 devices: a whole 4x4x4 slice. The times are simulated.
128 devices in a mesh: seq: 32 (over z_hi, x, y), vocab: 4 (over z_lo, core).
Axes of the slice: x: 4, y: 4, z: 4 (z_hi: 2, z_lo: 2; z = z_hi * 2 + z_lo), core: 2. Of those that a mesh axis runs over, the one named last changes fastest.
Arguments:
- policy_hidden: bfloat16 [8192, 2560], P('seq'), may hold values from -45 to 45
- reference_hidden: bfloat16 [8192, 2560], P('seq'), may hold values from -45 to 45
- targets: int32 [8192], P('seq'), may hold values from 0 to 2559
- lengths: int32 [4], replicated, may hold values from 1 to 4096, 8192 in all
- block_source: int32 [64], P('seq'), may hold values from 0 to 63, each once
- rollout_prompt: int32 [4], replicated, may hold values from 0 to 3, each once
- rollout_slot: int32 [4], replicated, may hold values from 0 to 3, each once
- policy_input_gain: float32 [2560], replicated, may hold values from 0.3 to 3
- policy_query_weight: bfloat16 [2560, 2048], P(None, 'vocab'), may hold values from -0.125 to 0.125
- policy_key_weight: bfloat16 [2560, 512], P(None, 'vocab'), may hold values from -0.125 to 0.125
- policy_value_weight: bfloat16 [2560, 512], P(None, 'vocab'), may hold values from -0.125 to 0.125
- policy_query_gain: float32 [128], replicated, may hold values from 0.5 to 9, as said below
- policy_key_gain: float32 [128], replicated, may hold values from 0.5 to 9, as said below
- policy_out_weight: bfloat16 [2048, 2560], P('vocab'), may hold values from -0.5 to 0.5
- policy_final_gain: float32 [2560], replicated, may hold values from 1.5 to 60, as said below
- policy_head: bfloat16 [2560, 2560], P(None, 'vocab'), may hold values from -0.125 to 0.125
- policy_prompt_keys: bfloat16 [4, 256, 512], P(None, 'seq', 'vocab'), may hold values from -6 to 6
- policy_prompt_values: bfloat16 [4, 256, 512], P(None, 'seq', 'vocab'), may hold values from -6 to 6
- reference_input_gain: float32 [2560], replicated, may hold values from 0.3 to 3
- reference_query_weight: bfloat16 [2560, 2048], P(None, 'vocab'), may hold values from -0.125 to 0.125
- reference_key_weight: bfloat16 [2560, 512], P(None, 'vocab'), may hold values from -0.125 to 0.125
- reference_value_weight: bfloat16 [2560, 512], P(None, 'vocab'), may hold values from -0.125 to 0.125
- reference_query_gain: float32 [128], replicated, may hold values from 0.5 to 9, as said below
- reference_key_gain: float32 [128], replicated, may hold values from 0.5 to 9, as said below
- reference_out_weight: bfloat16 [2048, 2560], P('vocab'), may hold values from -0.5 to 0.5
- reference_final_gain: float32 [2560], replicated, may hold values from 1.5 to 60, as said below
- reference_head: bfloat16 [2560, 2560], P(None, 'vocab'), may hold values from -0.125 to 0.125
- reference_prompt_keys: bfloat16 [4, 256, 512], P(None, 'seq', 'vocab'), may hold values from -6 to 6
- reference_prompt_values: bfloat16 [4, 256, 512], P(None, 'seq', 'vocab'), may hold values from -6 to 6
Outputs:
- token_diff: float32 [8192], P('seq')
- rollout_mean: float32 [4], replicated
Inputs may be any that keep to these rules, and one draw needn't show every extreme that they name: `policy_query_gain`: positive. `policy_key_gain`: positive. `reference_query_gain`: positive. `reference_key_gain`: positive. `policy_final_gain`: positive. `reference_final_gain`: positive.
All inputs are finite; a program needn't handle non-finite values.
Results may differ from a plain program's by a relative error of at most 0.04.
The roundings to bfloat16 on the way count: a program that leaves them out, or rounds other values in their place, can miss the bound.
Values may be sent and summed in bfloat16 or wider, within the bound.
No kernel may reach another device: no remote copies, remote signals or barrier semaphores. Data moves between devices by JAX's collectives and lax.ppermute only.
A program may use at most 128 MiB of HBM per device.

v0:
```python
import jax
import jax.numpy as jnp
from jax import lax
from jax.sharding import PartitionSpec as P

HD = 128
BLOCK = 128


EPSILON = 1e-06
ROPE_BASE = 1000000.0
NEGATIVE_FILL = -1e30


def rms_scale(values, gain_row):
    values = values.astype(jnp.float32)
    return (
        values * lax.rsqrt(jnp.mean(values * values, axis=-1, keepdims=True) + EPSILON) * gain_row
    )


def rotate(values, positions):
    half_width = values.shape[-1] // 2
    frequency = ROPE_BASE ** (-2.0 * jnp.arange(half_width, dtype=jnp.float32) / values.shape[-1])
    angles = positions.astype(jnp.float32)[:, None] * frequency[None, :]
    cosine = jnp.cos(angles)
    sine_part = jnp.sin(angles)
    cosine = jnp.concatenate([cosine, cosine], axis=-1)[:, None, :]
    sine_part = jnp.concatenate([sine_part, sine_part], axis=-1)[:, None, :]
    turned = jnp.concatenate([-values[..., half_width:], values[..., :half_width]], axis=-1)
    return values * cosine + turned * sine_part


def lookup(member, lookup_table):
    return jnp.sum(jnp.where(member, lookup_table[None, :], 0), axis=1)


def project(
    hidden,
    input_gain,
    query_weight,
    key_weight,
    value_weight,
    query_gain,
    key_gain,
    prompt_keys,
    prompt_values,
    positions,
    rope_offset,
):
    tok_rows = hidden.shape[0]
    kv_local = key_weight.shape[1] // HD
    normed = rms_scale(hidden, input_gain).astype(jnp.bfloat16)
    query_rows = jnp.dot(normed, query_weight, preferred_element_type=jnp.float32).reshape(
        tok_rows, -1, HD
    )
    query_rows = rotate(rms_scale(query_rows, query_gain), positions + rope_offset).astype(
        jnp.bfloat16
    )
    key_rows = jnp.dot(normed, key_weight, preferred_element_type=jnp.float32).reshape(
        tok_rows, kv_local, HD
    )
    key_rows = (
        rotate(rms_scale(key_rows, key_gain), positions + rope_offset)
        .astype(jnp.bfloat16)
        .reshape(tok_rows, kv_local * HD)
    )
    value_rows = jnp.dot(normed, value_weight, preferred_element_type=jnp.float32).astype(
        jnp.bfloat16
    )
    key_block = jnp.concatenate([key_rows, prompt_keys.reshape(-1, kv_local * HD)], axis=0)
    value_block = jnp.concatenate([value_rows, prompt_values.reshape(-1, kv_local * HD)], axis=0)
    stacked = jnp.concatenate([key_block, value_block], axis=1)
    return (query_rows.reshape(tok_rows, kv_local, -1, HD), stacked)


def empty_state(query_rows):
    tok_rows, kv_local, group_size = (query_rows.shape[0], query_rows.shape[1], query_rows.shape[2])
    running_max = jnp.full((kv_local, group_size, tok_rows), NEGATIVE_FILL, jnp.float32)
    weight_sum = jnp.zeros((kv_local, group_size, tok_rows), jnp.float32)
    accumulated = jnp.zeros((tok_rows, kv_local, group_size, HD), jnp.float32)
    return (running_max, weight_sum, accumulated)


def update_state(model_state, query_rows, stacked, visible):
    running_max, weight_sum, accumulated = model_state
    half_columns = stacked.shape[1] // 2
    kv_local = query_rows.shape[1]
    key_part = stacked[:, :half_columns].reshape(-1, kv_local, HD)
    value_part = stacked[:, half_columns:].reshape(-1, kv_local, HD)
    scores = jnp.einsum(
        "qkgd,skd->kgqs", query_rows, key_part, preferred_element_type=jnp.float32
    ) * HD ** (-0.5)
    masked = jnp.where(visible[None, None], scores, NEGATIVE_FILL)
    new_max = jnp.maximum(running_max, jnp.max(masked, axis=-1))
    weights = jnp.where(visible[None, None], jnp.exp(scores - new_max[..., None]), 0.0)
    factor = jnp.exp(running_max - new_max)
    new_sum = weight_sum * factor + jnp.sum(weights, axis=-1)
    product = jnp.einsum(
        "kgqs,skd->qkgd",
        weights.astype(jnp.bfloat16),
        value_part,
        preferred_element_type=jnp.float32,
    )
    new_accumulated = accumulated * jnp.transpose(factor, (2, 0, 1))[..., None] + product
    return (new_max, new_sum, new_accumulated)


def attend(states, queries, pieces, query_tag, query_position, query_prompt):
    stacked_list = pieces[:-2]
    key_tag = pieces[-2]
    key_position = pieces[-1]
    visible = (key_tag[None, :] == query_tag[:, None]) & (
        key_position[None, :] <= query_position[:, None]
    ) | (key_tag[None, :] == -1 - query_prompt[:, None])

    def compute(current):
        updated = []
        for model_state, query_rows, stacked in zip(current, queries, stacked_list):
            updated.append(update_state(model_state, query_rows, stacked, visible))
        return tuple(updated)

    def unchanged(current):
        return current

    return lax.cond(jnp.any(visible), compute, unchanged, states)


def make_fold(queries, query_tag, query_position, query_prompt, shard_rows):

    def fold_pieces(states, pieces, start_row):
        rows_here = pieces[0].shape[0]
        shard_count = rows_here // shard_rows
        split_pieces = tuple(
            (
                member_piece.reshape((shard_count, shard_rows) + member_piece.shape[1:])
                for member_piece in pieces
            )
        )

        def scan_step(carry_states, piece_item):
            return (
                attend(carry_states, queries, piece_item, query_tag, query_position, query_prompt),
                None,
            )

        return lax.scan(scan_step, states, split_pieces)[0]

    return fold_pieces


def finish(model_state, out_weight):
    running_max, weight_sum, accumulated = model_state
    attended = accumulated / jnp.transpose(weight_sum, (2, 0, 1))[..., None]
    attended = attended.reshape(accumulated.shape[0], -1).astype(jnp.bfloat16)
    return jnp.dot(attended, out_weight, preferred_element_type=jnp.float32)


def head_terms(final_rows, head_weight, targets, vocab_start):
    logits = jnp.dot(final_rows, head_weight, preferred_element_type=jnp.float32)
    local_max = jnp.max(logits, axis=-1)
    word_ids = vocab_start + jnp.arange(logits.shape[1], dtype=jnp.int32)
    target_logit = jnp.sum(jnp.where(word_ids[None, :] == targets[:, None], logits, 0.0), axis=-1)
    return (logits, local_max, target_logit)


def local(
    policy_hidden,
    reference_hidden,
    targets,
    lengths,
    block_source,
    rollout_prompt,
    rollout_slot,
    policy_input_gain,
    policy_query_weight,
    policy_key_weight,
    policy_value_weight,
    policy_query_gain,
    policy_key_gain,
    policy_out_weight,
    policy_final_gain,
    policy_head,
    policy_prompt_keys,
    policy_prompt_values,
    reference_input_gain,
    reference_query_weight,
    reference_key_weight,
    reference_value_weight,
    reference_query_gain,
    reference_key_gain,
    reference_out_weight,
    reference_final_gain,
    reference_head,
    reference_prompt_keys,
    reference_prompt_values,
):
    tok_rows = policy_hidden.shape[0]
    roll_ids = jnp.arange(lengths.shape[0], dtype=jnp.int32)
    slot_ids = jnp.arange(tok_rows, dtype=jnp.int32)
    packed = jnp.repeat(block_source, BLOCK) * BLOCK + slot_ids % BLOCK
    end_points = jnp.cumsum(lengths)
    rollout = jnp.sum((packed[:, None] >= end_points[None, :]).astype(jnp.int32), axis=1)
    member = rollout[:, None] == roll_ids[None, :]
    position = packed - lookup(member, end_points - lengths)
    query_prompt = lookup(member, rollout_prompt)
    slot_of = lookup(member, rollout_slot)
    length_of = lookup(member, lengths)
    prompt_count = policy_prompt_keys.shape[0]
    prefix_local = policy_prompt_keys.shape[1]
    prompt_rows = prompt_count * prefix_local
    rope_offset = prefix_local * lax.axis_size("seq")
    prompt_ids = jnp.arange(prompt_rows, dtype=jnp.int32) // prefix_local
    key_tag = jnp.concatenate([rollout, -1 - prompt_ids])
    key_position = jnp.concatenate([position, jnp.full((prompt_rows,), -1, jnp.int32)])
    shard_rows = tok_rows + prompt_rows
    policy_query, policy_stack = project(
        policy_hidden,
        policy_input_gain,
        policy_query_weight,
        policy_key_weight,
        policy_value_weight,
        policy_query_gain,
        policy_key_gain,
        policy_prompt_keys,
        policy_prompt_values,
        position,
        rope_offset,
    )
    reference_query, reference_stack = project(
        reference_hidden,
        reference_input_gain,
        reference_query_weight,
        reference_key_weight,
        reference_value_weight,
        reference_query_gain,
        reference_key_gain,
        reference_prompt_keys,
        reference_prompt_values,
        position,
        rope_offset,
    )
    fold_policy = make_fold((policy_query,), rollout, position, query_prompt, shard_rows)
    (policy_state,) = fold_policy(
        (empty_state(policy_query),),
        (
            lax.all_gather(policy_stack, "seq", axis=0, tiled=True),
            lax.all_gather(key_tag, "seq", axis=0, tiled=True),
            lax.all_gather(key_position, "seq", axis=0, tiled=True),
        ),
        jnp.int32(0),
    )
    fold_reference = make_fold((reference_query,), rollout, position, query_prompt, shard_rows)
    (reference_state,) = fold_reference(
        (empty_state(reference_query),),
        (
            lax.all_gather(reference_stack, "seq", axis=0, tiled=True),
            lax.all_gather(key_tag, "seq", axis=0, tiled=True),
            lax.all_gather(key_position, "seq", axis=0, tiled=True),
        ),
        jnp.int32(0),
    )
    policy_part = finish(policy_state, policy_out_weight)
    reference_part = finish(reference_state, reference_out_weight)
    policy_mixed, reference_mixed = (
        lax.psum(policy_part.astype(jnp.bfloat16), "vocab").astype(jnp.float32),
        lax.psum(reference_part.astype(jnp.bfloat16), "vocab").astype(jnp.float32),
    )
    policy_final = rms_scale(
        policy_hidden.astype(jnp.float32) + policy_mixed, policy_final_gain
    ).astype(jnp.bfloat16)
    reference_final = rms_scale(
        reference_hidden.astype(jnp.float32) + reference_mixed, reference_final_gain
    ).astype(jnp.bfloat16)
    vocab_start = lax.axis_index("vocab") * policy_head.shape[1]
    policy_logits, policy_max, policy_target = head_terms(
        policy_final, policy_head, targets, vocab_start
    )
    reference_logits, reference_max, reference_target = head_terms(
        reference_final, reference_head, targets, vocab_start
    )
    policy_top, reference_top = lax.pmax((policy_max, reference_max), "vocab")
    policy_local = jnp.sum(jnp.exp(policy_logits - policy_top[:, None]), axis=-1)
    reference_local = jnp.sum(jnp.exp(reference_logits - reference_top[:, None]), axis=-1)
    totals = lax.psum((policy_local, reference_local, policy_target, reference_target), "vocab")
    policy_score = totals[2] - (policy_top + jnp.log(totals[0]))
    reference_score = totals[3] - (reference_top + jnp.log(totals[1]))
    token_diff = policy_score - reference_score
    per_token = token_diff / length_of.astype(jnp.float32)
    partial_sums = jnp.sum(
        jnp.where(slot_of[:, None] == roll_ids[None, :], per_token[:, None], 0.0), axis=0
    )
    rollout_mean = lax.psum(partial_sums, "seq")
    return (token_diff, rollout_mean)


def solution(mesh):
    return jax.shard_map(
        local,
        mesh=mesh,
        in_specs=(
            P("seq", None),
            P("seq", None),
            P("seq"),
            P(),
            P("seq"),
            P(),
            P(),
            P(),
            P(None, "vocab"),
            P(None, "vocab"),
            P(None, "vocab"),
            P(),
            P(),
            P("vocab", None),
            P(),
            P(None, "vocab"),
            P(None, "seq", "vocab"),
            P(None, "seq", "vocab"),
            P(),
            P(None, "vocab"),
            P(None, "vocab"),
            P(None, "vocab"),
            P(),
            P(),
            P("vocab", None),
            P(),
            P(None, "vocab"),
            P(None, "seq", "vocab"),
            P(None, "seq", "vocab"),
        ),
        out_specs=(P("seq"), P()),
        check_vma=False,
    )
```

profile of v0, /device:TPU:0, one launch (start us, length us, event | category | flops | bytes accessed | tf_op | source)
XLA Modules:
  0.0 949.9 jit_solution(1144065349795593373)
XLA Ops:
  35.2 3.8 fusion.65
  43.1 3.9 fusion.60
  65.6 265.0 %all-reduce.10.cloned.1.call-done = (s32[9216]{0:T(1024)}, s32[9216]{0:T(1024)}) async-done(((s32[9216]{0:T(1024)}, s32[9216]{0:T(1024)}), (s32[9216]{0:T(1024)}, s32[9216]{0:T(1024)})) %all-reduce.10.cloned.1.call-update) | async-done | bytes 73744
  332.3 85.3 %all-gather.3.cloned.1.call-done = bf16[9216,256]{1,0:T(8,128)(2,1)} async-done(((bf16[288,256]{1,0:T(8,128)(2,1)}), bf16[9216,256]{1,0:T(8,128)(2,1)}) %all-gather.3.cloned.1.call-update) | async-done | bytes 4718608 | tf_op jit(solution)/shard_map/all_gather | solution.py:247
  418.4 166.9 %while.28 = (s32[]{:T(128)}, f32[1,4,256]{2,1,0:T(4,128)S(1)}, f32[1,4,256]{2,1,0:T(4,128)S(1)}, f32[256,1,4,128]{0,3,2,1:T(8,128)}, s32[32,288]{1,0:T(8,128)S(1...) while((s32[]{:T(128)}, f32[1,4,256]{2,1,0:T(4,128)S(1)}, ...), condition=%wide.region_13.14_spmd, body=%wide.region_7.13_spmd.sunk | while | flops 154356992 | bytes 9859115 | solution.py:147
  586.3 167.9 %while.29 = (s32[]{:T(128)}, f32[1,4,256]{2,1,0:T(4,128)S(1)}, f32[1,4,256]{2,1,0:T(4,128)S(1)}, f32[256,1,4,128]{0,3,2,1:T(8,128)}, s32[32,288]{1,0:T(8,128)S(1...) while((s32[]{:T(128)}, f32[1,4,256]{2,1,0:T(4,128)S(1)}, ...), condition=%wide.region_31.32_spmd, body=%wide.region_25.31_spmd.sunk | while | flops 154356992 | bytes 9859115 | solution.py:147
  598.2 3.7 conditional.5
  603.5 3.7 conditional.5
  608.7 3.7 conditional.5
  614.0 3.7 conditional.5
  624.5 3.7 conditional.5
  629.7 3.7 conditional.5
  634.9 3.7 conditional.5
  640.2 3.7 conditional.5
  650.7 3.7 conditional.5
  655.9 3.7 conditional.5
  661.2 3.7 conditional.5
  671.7 3.7 conditional.5
  676.9 3.7 conditional.5
  682.2 3.7 conditional.5
  687.4 3.7 conditional.5
  697.9 3.7 conditional.5
  703.1 3.7 conditional.5
  708.4 3.7 conditional.5
  713.6 3.7 conditional.5
  724.1 3.7 conditional.5
  729.4 3.7 conditional.5
  755.2 3.8 convolution_convert_fusion.1
  761.1 62.7 %all-reduce.12.cloned.1.call-done = (bf16[256,2560]{1,0:T(8,128)(2,1)}, bf16[256,2560]{1,0:T(8,128)(2,1)}) async-done(((bf16[256,2560]{1,0:T(8,128)(2,1)}, bf16[256,2560]{1,0:T(8,128)(2,1)}), (bf16[256,2560]{1,0:T(8,128)(2,1)}, bf16[256,2560]{1,0:T(8,128)(2,1)})) %all-reduce.12.cloned.1.call-update) | async-done | bytes 2621456 | tf_op jit(solution)/shard_map/psum | solution.py:267
  832.3 6.1 all-reduce.5
  840.2 5.7 all-reduce.4
  846.5 96.9 %psum.55 = f32[4]{0:T(128)} all-reduce(f32[4]{0:T(128)S(1)} %select_reduce_fusion.2), channel_id=1, replica_groups=mesh['seq'=32,'vocab'=4] {'seq'}, use_global_device_ids=true, to_apply=%region_43.44 | all-reduce | flops 4 | bytes 32 | tf_op jit(solution)/shard_map/psum | solution.py:293
  (1107 shorter events, 514.3 us)
Async XLA Ops:
  7.2 819.7 %copy-start = (bf16[2560,640]{1,0:T(8,128)(2,1)S(1)}, bf16[2560,640]{1,0:T(8,128)(2,1)}, u32[]{:S(2)}) copy-start(bf16[2560,640]{1,0:T(8,128)(2,1)} %param.63) | copy-start | bytes 9830404
  7.2 9.7 %copy-start.41 = (f32[2560]{0:T(1024)S(1)}, f32[2560]{0:T(1024)}, u32[]{:S(2)}) copy-start(f32[2560]{0:T(1024)} %param.44) | copy-start | bytes 30724
  7.2 323.4 %all-reduce.10.cloned.1.call-start = ((), (), s32[]{:S(2)}) async-start(), calls=%async_computation.2 | async-start | bytes 147456
  14.6 403.0 %all-gather.3.cloned.1.call-start = ((), (), s32[]{:S(2)}) async-start(), calls=%async_computation | async-start | bytes 4866048 | tf_op jit(solution)/shard_map/all_gather | solution.py:247
  16.9 5.9 copy-start.32
  16.9 2.7 copy-start.6
  22.8 2.7 copy-start.24
  22.8 3.4 copy-start.25
  29.1 6.1 copy-start.33
  32.4 552.9 %all-gather.5.cloned.1.call-start = ((), (), s32[]{:S(2)}) async-start(), calls=%async_computation.1 | async-start | bytes 4866048 | tf_op jit(solution)/shard_map/all_gather | solution.py:257
  33.3 790.5 %all-reduce.12.cloned.1.call-start = ((), (), s32[]{:S(2)}) async-start(), calls=%async_computation.3 | async-start | bytes 5242880 | tf_op jit(solution)/shard_map/psum | solution.py:267
  39.0 4.0 copy-start.35
  39.0 4.0 copy-start.43
  46.9 4.1 copy-start.17
  456.4 2.3 copy-start.4
  482.5 2.3 copy-start.4
  487.7 2.3 copy-start.4
  493.0 2.3 copy-start.4
  598.2 2.3 copy-start.1
  619.2 2.3 copy-start.1
  624.5 2.3 copy-start.1
  645.5 2.3 copy-start.1
  666.4 2.3 copy-start.1
  671.7 2.3 copy-start.1
  755.2 3.8 copy-start.3
  755.2 3.9 copy-start.11
  761.1 65.8 %copy-start.44 = (f32[2560]{0:T(1024)S(1)}, f32[2560]{0:T(1024)}, u32[]{:S(2)}) copy-start(f32[2560]{0:T(1024)} %param.62) | copy-start | bytes 30724
  823.8 2.4 copy-start.9
  823.8 2.5 copy-start.14
  830.2 8.2 copy-start.36
  832.3 13.5 %copy-start.26 = (s32[256]{0:T(256)S(1)}, s32[256]{0:T(256)}, u32[]{:S(2)}) copy-start(s32[256]{0:T(256)} %get-tuple-element.243) | copy-start | bytes 3076
  832.3 14.1 %copy-start.27 = (s32[256]{0:T(256)S(1)}, s32[256]{0:T(256)}, u32[]{:S(2)}) copy-start(s32[256]{0:T(256)} %get-tuple-element.242) | copy-start | bytes 3076
  (142 other events, 212.1 us)
Sparse Core Ops, SparseCore 0:
  14.7 315.8 all-reduce.9
  333.6 83.8 all-gather.2
  420.6 81.4 all-gather.4
  761.2 62.5 all-reduce.11
where the time goes:
time: 954 us; the launch traced here: 950 us
  waiting for transfers between devices  413 us (43%)
  matrix products  141 us (15%)
  local copies, waits for them, and re-layouts  127 us (13%)
  blocking collectives  109 us (11%)
  other arithmetic  98 us (10%)
  loops' own time  47.4 us (5%)
  between operations  14.9 us (2%)
    unnamed x5, waiting for transfers between devices  265 us
    psum x1, blocking collectives, local(): rollout_mean = lax.psum(partial_sums, 'seq')  96.9 us
    all_gather x1, waiting for transfers between devices, local(): lax.all_gather(policy_stack, 'seq', axis=0, tiled=True)  85.3 us
    dot_general x64, matrix products, update_state(): jnp.einsum('qkgd,skd->kgqs', query_rows, key_part, preferred_element_type...  83.1 us
    squeeze x64, local copies, waits for them, and re-layouts, fold_pieces(): return lax.scan(scan_step, states, split_pieces)[0]  62.9 us
    psum x1, waiting for transfers between devices, local(): lax.psum(reference_part.astype(jnp.bfloat16), 'vocab').astype(jnp.float32)  62.7 us
    reduce_or x64, other arithmetic, attend(): return lax.cond(jnp.any(visible), compute, unchanged, states)  51.5 us
    another operation x2, loops' own time, fold_pieces(): return lax.scan(scan_step, states, split_pieces)[0]  43 us
  transfers between devices with their start and end apart: 4, of which 3 were waited for; matrix products, arithmetic and copies ran while one was open for 19% of the time, Pallas kernels for 0%

commit v1 on v0

--- a/solution.py
+++ b/solution.py
@@ -211,8 +211,32 @@
     prompt_rows = prompt_count * prefix_local
     rope_offset = prefix_local * lax.axis_size("seq")
     prompt_ids = jnp.arange(prompt_rows, dtype=jnp.int32) // prefix_local
-    key_tag = jnp.concatenate([rollout, -1 - prompt_ids])
-    key_position = jnp.concatenate([position, jnp.full((prompt_rows,), -1, jnp.int32)])
+    seq_count = lax.axis_size("seq")
+    lead = lax.axis_index("vocab") == 0
+    source_slots = jnp.zeros((seq_count, block_source.shape[0]), jnp.int32)
+    source_slots = lax.dynamic_update_slice(
+        source_slots, jnp.where(lead, block_source, 0)[None, :], (lax.axis_index("seq"), 0)
+    )
+    all_source = lax.psum(source_slots, ("seq", "vocab")).reshape(-1)
+    all_ids = jnp.arange(tok_rows * seq_count, dtype=jnp.int32)
+    all_packed = jnp.repeat(all_source, BLOCK) * BLOCK + all_ids % BLOCK
+    all_rollout = jnp.sum((all_packed[:, None] >= end_points[None, :]).astype(jnp.int32), axis=1)
+    all_member = all_rollout[:, None] == roll_ids[None, :]
+    all_position = all_packed - lookup(all_member, end_points - lengths)
+    key_tag = jnp.concatenate(
+        [
+            all_rollout.reshape(seq_count, tok_rows),
+            jnp.broadcast_to(-1 - prompt_ids, (seq_count, prompt_rows)),
+        ],
+        axis=1,
+    ).reshape(-1)
+    key_position = jnp.concatenate(
+        [
+            all_position.reshape(seq_count, tok_rows),
+            jnp.full((seq_count, prompt_rows), -1, jnp.int32),
+        ],
+        axis=1,
+    ).reshape(-1)
     shard_rows = tok_rows + prompt_rows
     policy_query, policy_stack = project(
         policy_hidden,
@@ -245,8 +269,8 @@
         (empty_state(policy_query),),
         (
             lax.all_gather(policy_stack, "seq", axis=0, tiled=True),
-            lax.all_gather(key_tag, "seq", axis=0, tiled=True),
-            lax.all_gather(key_position, "seq", axis=0, tiled=True),
+            key_tag,
+            key_position,
         ),
         jnp.int32(0),
     )
@@ -255,8 +279,8 @@
         (empty_state(reference_query),),
         (
             lax.all_gather(reference_stack, "seq", axis=0, tiled=True),
-            lax.all_gather(key_tag, "seq", axis=0, tiled=True),
-            lax.all_gather(key_position, "seq", axis=0, tiled=True),
+            key_tag,
+            key_position,
         ),
         jnp.int32(0),
     )
@@ -290,7 +314,7 @@
     partial_sums = jnp.sum(
         jnp.where(slot_of[:, None] == roll_ids[None, :], per_token[:, None], 0.0), axis=0
     )
-    rollout_mean = lax.psum(partial_sums, "seq")
+    rollout_mean = lax.psum(jnp.where(lead, partial_sums, 0.0), ("seq", "vocab"))
     return (token_diff, rollout_mean)
 
 

time: 954 us -> 707 us (0.74)
  waiting for transfers between devices: 413 us -> 64.1 us
  local copies, waits for them, and re-layouts: 127 us -> 174 us
  blocking collectives: 109 us -> 156 us
    unnamed x5 -> x3, waiting for transfers between devices: 265 us -> 0.05 us
    all_gather x1, waiting for transfers between devices: 85.3 us -> 0.01 us  [local(): lax.all_gather(policy_stack, 'seq', axis=0, tiled=True)]
    psum x1 -> x2, blocking collectives: 96.9 us -> 145 us  [the longest x1 77.8 us: local(): all_source = lax.psum(source_slots, ('seq', 'vocab')).reshape(-1)]
    dynamic_slice x64, local copies, waits for them, and re-layouts: 1.71 us -> 47.9 us  [fold_pieces(): return lax.scan(scan_step, states, split_pieces)[0]]
  transfers between devices with their start and end apart: 4 -> 3, of which waited for: 3 -> 1; matrix products, arithmetic and copies ran while one was open for 19% -> 27% of each run, Pallas kernels for 0% -> 0%
where the time goes in v1:
time: 707 us; the launch traced here: 695 us
  local copies, waits for them, and re-layouts  174 us (25%)
  blocking collectives  156 us (22%)
  matrix products  141 us (20%)
  other arithmetic  101 us (14%)
  waiting for transfers between devices  64.1 us (9%)
  loops' own time  44.5 us (6%)
  between operations  14.3 us (2%)
    dot_general x64, matrix products, update_state(): jnp.einsum('qkgd,skd->kgqs', query_rows, key_part, preferred_element_type...  83.1 us
    psum x1, blocking collectives, local(): all_source = lax.psum(source_slots, ('seq', 'vocab')).reshape(-1)  77.8 us
    psum x1, blocking collectives, local(): lax.psum(jnp.where(lead, partial_sums, 0.0), ('seq', 'vocab'))  66.8 us
    psum x1, waiting for transfers between devices, local(): lax.psum(reference_part.astype(jnp.bfloat16), 'vocab').astype(jnp.float32)  64 us
    squeeze x64, local copies, waits for them, and re-layouts, fold_pieces(): return lax.scan(scan_step, states, split_pieces)[0]  63 us
    reduce_or x64, other arithmetic, attend(): return lax.cond(jnp.any(visible), compute, unchanged, states)  49.8 us
    dynamic_slice x64, local copies, waits for them, and re-layouts, fold_pieces(): return lax.scan(scan_step, states, split_pieces)[0]  47.9 us
    another operation x2, loops' own time, fold_pieces(): return lax.scan(scan_step, states, split_pieces)[0]  40.1 us
  transfers between devices with their start and end apart: 3, of which 1 were waited for; matrix products, arithmetic and copies ran while one was open for 27% of the time, Pallas kernels for 0%

profile of v1, /device:TPU:0, one launch (start us, length us, event | category | flops | bytes accessed | tf_op | source)
XLA Modules:
  0.0 694.8 jit_solution(18089096328701590887)
XLA Ops:
  32.7 3.8 fusion.73
  40.6 3.9 fusion.68
  50.4 77.8 %psum.56 = s32[32,2]{1,0:T(8,128)} all-reduce(s32[32,2]{1,0:T(8,128)} %dynamic_update_slice.3), channel_id=1, replica_groups=mesh['seq'=32,'vocab'=4] {'seq','vocab'}, use_global_device_ids=true, to_apply=%region_5.6 | all-reduce | flops 64 | bytes 512 | tf_op jit(solution)/shard_map/psum | solution.py:220
  150.6 185.5 %while.28 = (s32[]{:T(128)}, f32[1,4,256]{2,1,0:T(4,128)S(1)}, f32[1,4,256]{2,1,0:T(4,128)S(1)}, f32[256,1,4,128]{0,3,2,1:T(8,128)}, s32[32,288]{1,0:T(8,128)}, ...) while((s32[]{:T(128)}, f32[1,4,256]{2,1,0:T(4,128)S(1)}, ...), condition=%wide.region_16.17_spmd, body=%wide.region_10.16_spmd.sunk | while | flops 154356992 | bytes 9859115 | solution.py:147
  170.1 3.8 conditional.4
  337.0 190.8 %while.29 = (s32[]{:T(128)}, f32[1,4,256]{2,1,0:T(4,128)S(1)}, f32[1,4,256]{2,1,0:T(4,128)S(1)}, f32[256,1,4,128]{0,3,2,1:T(8,128)}, s32[32,288]{1,0:T(8,128)}, ...) while((s32[]{:T(128)}, f32[1,4,256]{2,1,0:T(4,128)S(1)}, ...), condition=%wide.region_34.35_spmd, body=%wide.region_28.34_spmd.sunk | while | flops 154356992 | bytes 9859115 | solution.py:147
  339.2 3.7 conditional.5
  345.2 3.7 conditional.5
  351.1 3.7 conditional.5
  357.1 3.7 conditional.5
  363.0 3.7 conditional.5
  369.0 3.7 conditional.5
  375.0 3.7 conditional.5
  380.9 3.7 conditional.5
  386.9 3.7 conditional.5
  392.9 3.7 conditional.5
  398.8 3.7 conditional.5
  404.8 3.7 conditional.5
  410.7 3.7 conditional.5
  416.7 3.7 conditional.5
  422.7 3.7 conditional.5
  428.6 3.7 conditional.5
  434.6 3.7 conditional.5
  452.5 3.7 conditional.5
  470.4 3.7 conditional.5
  494.2 3.7 conditional.5
  518.1 3.7 conditional.5
  528.9 3.8 convolution_convert_fusion.1
  534.8 64.0 %all-reduce.6.cloned.1.call-done = (bf16[256,2560]{1,0:T(8,128)(2,1)}, bf16[256,2560]{1,0:T(8,128)(2,1)}) async-done(((bf16[256,2560]{1,0:T(8,128)(2,1)}, bf16[256,2560]{1,0:T(8,128)(2,1)}), (bf16[256,2560]{1,0:T(8,128)(2,1)}, bf16[256,2560]{1,0:T(8,128)(2,1)})) %all-reduce.6.cloned.1.call-update) | async-done | bytes 2621456 | tf_op jit(solution)/shard_map/psum | solution.py:291
  607.2 6.1 all-reduce.2
  615.1 5.7 all-reduce.1
  621.5 66.8 %psum.63 = f32[4]{0:T(128)} all-reduce(f32[4]{0:T(128)S(1)} %broadcast_select_fusion), channel_id=1, replica_groups=mesh['seq'=32,'vocab'=4] {'seq','vocab'}, use_global_device_ids=true, to_apply=%region_46.47 | all-reduce | flops 4 | bytes 32 | tf_op jit(solution)/shard_map/psum | solution.py:317
  (1125 shorter events, 560.2 us)
Async XLA Ops:
  7.2 594.6 %copy-start = (bf16[2560,640]{1,0:T(8,128)(2,1)S(1)}, bf16[2560,640]{1,0:T(8,128)(2,1)}, u32[]{:S(2)}) copy-start(bf16[2560,640]{1,0:T(8,128)(2,1)} %param.63) | copy-start | bytes 9830404
  7.2 7.4 %copy-start.47 = (f32[2560]{0:T(1024)S(1)}, f32[2560]{0:T(1024)}, u32[]{:S(2)}) copy-start(f32[2560]{0:T(1024)} %param.44) | copy-start | bytes 30724
  7.2 142.6 %all-gather.3.cloned.1.call-start = ((), (), s32[]{:S(2)}) async-start(), calls=%async_computation | async-start | bytes 4866048 | tf_op jit(solution)/shard_map/all_gather | solution.py:271
  10.0 4.5 copy-start.37
  10.0 4.6 copy-start.8
  14.6 5.9 copy-start.38
  14.6 2.7 copy-start.6
  20.5 2.8 copy-start.27
  20.5 3.5 copy-start.28
  26.8 5.9 copy-start.39
  30.2 305.9 %all-gather.5.cloned.1.call-start = ((), (), s32[]{:S(2)}) async-start(), calls=%async_computation.1 | async-start | bytes 4866048 | tf_op jit(solution)/shard_map/all_gather | solution.py:281
  31.0 567.7 %all-reduce.6.cloned.1.call-start = ((), (), s32[]{:S(2)}) async-start(), calls=%async_computation.2 | async-start | bytes 5242880 | tf_op jit(solution)/shard_map/psum | solution.py:291
  36.5 4.0 copy-start.41
  36.5 4.0 copy-start.49
  44.4 88.6 %copy-start.36 = (s32[4]{0:T(128)S(1)}, s32[4]{0:T(128)}, u32[]{:S(2)}) copy-start(s32[4]{0:T(128)} %copy-done.35) | copy-start | bytes 52
  44.4 91.2 %copy-start.17 = (f32[256,128]{0,1:T(8,128)S(1)}, f32[256,128]{0,1:T(8,128)}, u32[]{:S(2)}) copy-start(f32[256,128]{0,1:T(8,128)} %get-tuple-element.344) | copy-start | bytes 393220
  142.0 4.0 copy-start.23
  152.7 2.3 copy-start.4
  158.5 2.3 copy-start.4
  170.1 2.4 copy-start.4
  193.3 2.3 copy-start.4
  216.5 2.3 copy-start.4
  222.3 2.3 copy-start.4
  245.5 2.3 copy-start.4
  528.9 3.8 copy-start.3
  528.9 3.9 copy-start.11
  534.7 67.1 %copy-start.50 = (f32[2560]{0:T(1024)S(1)}, f32[2560]{0:T(1024)}, u32[]{:S(2)}) copy-start(f32[2560]{0:T(1024)} %param.62) | copy-start | bytes 30724
  598.8 2.4 copy-start.9
  598.8 2.5 copy-start.14
  605.1 8.2 %copy-start.42 = (s32[256]{0:T(256)S(1)}, s32[256]{0:T(256)}, u32[]{:S(2)}) copy-start(s32[256]{0:T(256)} %param.39) | copy-start | bytes 3076
  607.2 13.5 %copy-start.29 = (s32[256]{0:T(256)S(1)}, s32[256]{0:T(256)}, u32[]{:S(2)}) copy-start(s32[256]{0:T(256)} %get-tuple-element.243) | copy-start | bytes 3076
  607.2 14.1 %copy-start.30 = (s32[256]{0:T(256)S(1)}, s32[256]{0:T(256)}, u32[]{:S(2)}) copy-start(s32[256]{0:T(256)} %get-tuple-element.242) | copy-start | bytes 3076
  (147 other events, 225.5 us)
Sparse Core Ops, SparseCore 0:
  30.3 87.6 all-gather.2
  121.1 81.3 all-gather.4
  534.9 63.8 all-reduce.5

commit v2 on v1

--- a/solution.py
+++ b/solution.py
@@ -2,6 +2,8 @@
 import jax.numpy as jnp
 from jax import lax
 from jax.sharding import PartitionSpec as P
+from jax.experimental import pallas as pl
+from jax.experimental.pallas import tpu as pltpu
 
 HD = 128
 BLOCK = 128
@@ -147,6 +149,83 @@
         return lax.scan(scan_step, states, split_pieces)[0]
 
     return fold_pieces
+
+
+Q_TILE = 512
+K_TILE = 1024
+CODE_STRIDE = 65536
+
+
+def flash_kernel(flags_ref, q_ref, kv_ref, kcode_ref, qlo_ref, qhi_ref, out_ref, m_sc, l_sc, acc_sc):
+    j = pl.program_id(1)
+
+    @pl.when(j == 0)
+    def _():
+        m_sc[...] = jnp.full(m_sc.shape, NEGATIVE_FILL, jnp.float32)
+        l_sc[...] = jnp.zeros(l_sc.shape, jnp.float32)
+        acc_sc[...] = jnp.zeros(acc_sc.shape, jnp.float32)
+
+    @pl.when(flags_ref[j] > 0)
+    def _():
+        kv = kv_ref[...]
+        scores = lax.dot_general(
+            q_ref[...], kv[:, :HD], (((1,), (1,)), ((), ())), preferred_element_type=jnp.float32
+        ) * HD ** (-0.5)
+        key_code = kcode_ref[...]
+        visible = (key_code >= qlo_ref[...]) & (key_code <= qhi_ref[...])
+        masked = jnp.where(visible, scores, NEGATIVE_FILL)
+        old_max = m_sc[...]
+        new_max = jnp.maximum(old_max, jnp.max(masked, axis=1, keepdims=True))
+        weights = jnp.where(visible, jnp.exp(scores - new_max), 0.0)
+        factor = jnp.exp(old_max - new_max)
+        l_sc[...] = l_sc[...] * factor + jnp.sum(weights, axis=1, keepdims=True)
+        acc_sc[...] = acc_sc[...] * factor + jnp.dot(
+            weights.astype(jnp.bfloat16), kv[:, HD:], preferred_element_type=jnp.float32
+        )
+        m_sc[...] = new_max
+
+    @pl.when(j == pl.num_programs(1) - 1)
+    def _():
+        out_ref[...] = (acc_sc[...] / l_sc[...]).astype(out_ref.dtype)
+
+
+def flash_attend(flags, queries, stacked, key_code, query_low, query_high):
+    q_rows = queries.shape[0]
+    k_rows = stacked.shape[0]
+    grid_spec = pltpu.PrefetchScalarGridSpec(
+        num_scalar_prefetch=1,
+        grid=(q_rows // Q_TILE, k_rows // K_TILE),
+        in_specs=[
+            pl.BlockSpec((Q_TILE, HD), lambda i, j, f: (i, 0)),
+            pl.BlockSpec((K_TILE, 2 * HD), lambda i, j, f: (j, 0)),
+            pl.BlockSpec((1, K_TILE), lambda i, j, f: (0, j)),
+            pl.BlockSpec((Q_TILE, 1), lambda i, j, f: (i, 0)),
+            pl.BlockSpec((Q_TILE, 1), lambda i, j, f: (i, 0)),
+        ],
+        out_specs=pl.BlockSpec((Q_TILE, HD), lambda i, j, f: (i, 0)),
+        scratch_shapes=[
+            pltpu.VMEM((Q_TILE, 1), jnp.float32),
+            pltpu.VMEM((Q_TILE, 1), jnp.float32),
+            pltpu.VMEM((Q_TILE, HD), jnp.float32),
+        ],
+    )
+    return pl.pallas_call(
+        flash_kernel,
+        grid_spec=grid_spec,
+        out_shape=jax.ShapeDtypeStruct((q_rows, HD), jnp.bfloat16),
+        compiler_params=pltpu.CompilerParams(dimension_semantics=("arbitrary", "arbitrary")),
+    )(flags, queries, stacked, key_code, query_low, query_high)
+
+
+def attend_model(query_rows, gathered, flags, key_code, query_low, query_high, out_weight):
+    tok_rows, kv_local, group_size = query_rows.shape[:3]
+    flat_query = jnp.transpose(query_rows, (1, 2, 0, 3)).reshape(-1, HD)
+    tiled_low = jnp.tile(query_low, kv_local * group_size)[:, None]
+    tiled_high = jnp.tile(query_high, kv_local * group_size)[:, None]
+    attended = flash_attend(flags, flat_query, gathered, key_code[None, :], tiled_low, tiled_high)
+    attended = jnp.transpose(attended.reshape(kv_local, group_size, tok_rows, HD), (2, 0, 1, 3))
+    attended = attended.reshape(tok_rows, -1)
+    return jnp.dot(attended, out_weight, preferred_element_type=jnp.float32)
 
 
 def finish(model_state, out_weight):
@@ -223,20 +302,18 @@
     all_rollout = jnp.sum((all_packed[:, None] >= end_points[None, :]).astype(jnp.int32), axis=1)
     all_member = all_rollout[:, None] == roll_ids[None, :]
     all_position = all_packed - lookup(all_member, end_points - lengths)
-    key_tag = jnp.concatenate(
+    owner = lookup(rollout_prompt[None, :] == jnp.arange(prompt_count, dtype=jnp.int32)[:, None], roll_ids)
+    key_code = jnp.concatenate(
         [
-            all_rollout.reshape(seq_count, tok_rows),
-            jnp.broadcast_to(-1 - prompt_ids, (seq_count, prompt_rows)),
+            (all_rollout * CODE_STRIDE + all_position).reshape(seq_count, tok_rows),
+            jnp.broadcast_to(owner[prompt_ids] * CODE_STRIDE - 1, (seq_count, prompt_rows)),
         ],
         axis=1,
     ).reshape(-1)
-    key_position = jnp.concatenate(
-        [
-            all_position.reshape(seq_count, tok_rows),
-            jnp.full((seq_count, prompt_rows), -1, jnp.int32),
-        ],
-        axis=1,
-    ).reshape(-1)
+    query_low = rollout * CODE_STRIDE - 1
+    query_high = rollout * CODE_STRIDE + position
+    seen = (key_code[None, :] >= query_low[:, None]) & (key_code[None, :] <= query_high[:, None])
+    flags = jnp.any(seen.reshape(tok_rows, -1, K_TILE), axis=(0, 2)).astype(jnp.int32)
     shard_rows = tok_rows + prompt_rows
     policy_query, policy_stack = project(
         policy_hidden,
@@ -264,28 +341,24 @@
         position,
         rope_offset,
     )
-    fold_policy = make_fold((policy_query,), rollout, position, query_prompt, shard_rows)
-    (policy_state,) = fold_policy(
-        (empty_state(policy_query),),
-        (
-            lax.all_gather(policy_stack, "seq", axis=0, tiled=True),
-            key_tag,
-            key_position,
-        ),
-        jnp.int32(0),
-    )
-    fold_reference = make_fold((reference_query,), rollout, position, query_prompt, shard_rows)
-    (reference_state,) = fold_reference(
-        (empty_state(reference_query),),
-        (
-            lax.all_gather(reference_stack, "seq", axis=0, tiled=True),
-            key_tag,
-            key_position,
-        ),
-        jnp.int32(0),
-    )
-    policy_part = finish(policy_state, policy_out_weight)
-    reference_part = finish(reference_state, reference_out_weight)
+    policy_part = attend_model(
+        policy_query,
+        lax.all_gather(policy_stack, "seq", axis=0, tiled=True),
+        flags,
+        key_code,
+        query_low,
+        query_high,
+        policy_out_weight,
+    )
+    reference_part = attend_model(
+        reference_query,
+        lax.all_gather(reference_stack, "seq", axis=0, tiled=True),
+        flags,
+        key_code,
+        query_low,
+        query_high,
+        reference_out_weight,
+    )
     policy_mixed, reference_mixed = (
         lax.psum(policy_part.astype(jnp.bfloat16), "vocab").astype(jnp.float32),
         lax.psum(reference_part.astype(jnp.bfloat16), "vocab").astype(jnp.float32),

time: 707 us -> 402 us (0.57); the launches traced: 695 us -> 400 us
  local copies, waits for them, and re-layouts: 174 us -> 24.7 us
  matrix products: 141 us -> 26.1 us
  Pallas kernels: 0 us -> 69.2 us
  other arithmetic: 101 us -> 38.2 us
  loops' own time: 44.5 us -> 0 us
  waiting for transfers between devices: 64.1 us -> 71.4 us
    dot_general x130 -> x2, matrix products: 124 us -> 5.77 us  [attend_model(): return jnp.dot(attended, out_weight, preferred_element_type=jnp.float32)]
    pallas_call x0 -> x2, Pallas kernels: none -> 69.2 us  [flash_attend(): pl.pallas_call(flash_kernel, grid_spec=grid_spec, out_shape=jax.ShapeDtyp...]
    squeeze x64 -> x0, local copies, waits for them, and re-layouts: 63 us -> none  [fold_pieces(): return lax.scan(scan_step, states, split_pieces)[0]]
    dynamic_slice x64 -> x0, local copies, waits for them, and re-layouts: 47.9 us -> none  [fold_pieces(): return lax.scan(scan_step, states, split_pieces)[0]]
    reduce_or x64 -> x1, other arithmetic: 49.8 us -> 2.67 us  [local(): jnp.any(seen.reshape(tok_rows, -1, K_TILE), axis=(0, 2)).astype(jnp.int32)]
    another operation x66 -> x0, loops' own time: 44.5 us -> none  [the longest x2 40.1 us: fold_pieces(): return lax.scan(scan_step, states, split_pieces)[0]]
    cond x320 -> x0, local copies, waits for them, and re-layouts: 36.7 us -> none
    reduce_sum x64 -> x0, other arithmetic: 14.8 us -> none  [update_state(): new_sum = weight_sum * factor + jnp.sum(weights, axis=-1)]
  transfers between devices with their start and end apart: 3 -> 3, of which waited for: 1 -> 2; matrix products, arithmetic and copies ran while one was open for 27% -> 13% of each run, Pallas kernels for 0% -> 9%
where the time goes in v2:
time: 402 us; the launch traced here: 400 us
  blocking collectives  156 us (39%)
  waiting for transfers between devices  71.4 us (18%)
  Pallas kernels  69.2 us (17%)
  other arithmetic  38.2 us (10%)
  matrix products  26.1 us (6%)
  local copies, waits for them, and re-layouts  24.7 us (6%)
  between operations  14.3 us (4%)
    psum x1, blocking collectives, local(): all_source = lax.psum(source_slots, ('seq', 'vocab')).reshape(-1)  77.8 us
    pallas_call x2, Pallas kernels, flash_attend(): pl.pallas_call(flash_kernel, grid_spec=grid_spec, out_shape=jax.ShapeDtyp...  69.2 us
    psum x1, blocking collectives, local(): lax.psum(jnp.where(lead, partial_sums, 0.0), ('seq', 'vocab'))  66.8 us
    psum x1, waiting for transfers between devices, local(): lax.psum(reference_part.astype(jnp.bfloat16), 'vocab').astype(jnp.float32)  62.7 us
    reduce_sum x6, other arithmetic, rms_scale(): jnp.mean(values * values, axis=-1, keepdims=True) + EPSILON  9.03 us
    all_gather x1, waiting for transfers between devices, local(): lax.all_gather(reference_stack, 'seq', axis=0, tiled=True)  8.74 us
    reshape x4, local copies, waits for them, and re-layouts, project(): jnp.dot(normed, query_weight, preferred_element_type=jnp.float32)  8.1 us
  transfers between devices with their start and end apart: 3, of which 2 were waited for; matrix products, arithmetic and copies ran while one was open for 13% of the time, Pallas kernels for 9%

profile of v2, /device:TPU:0, one launch (start us, length us, event | category | flops | bytes accessed | tf_op | source)
XLA Modules:
  0.0 400.1 jit_solution(16969203479057128692)
XLA Ops:
  12.8 1.7 fusion
  14.5 1.7 fusion.3
  17.0 3.3 multiply_reduce_fusion.4
  22.0 2.1 convolution_convert_fusion.3
  25.7 1.5 fusion.25
  28.0 2.1 convolution_convert_fusion.2
  31.6 3.9 fusion.51
  35.5 2.0 reshape.471
  37.5 2.0 reshape.470
  39.5 3.9 fusion.46
  43.4 2.1 reshape.478
  45.5 2.0 reshape.477
  48.2 77.8 %psum.56 = s32[32,2]{1,0:T(8,128)} all-reduce(s32[32,2]{1,0:T(8,128)S(1)} %dynamic_update_slice.3), channel_id=1, replica_groups=mesh['seq'=32,'vocab'=4] {'seq','vocab'}, use_global_device_ids=true, to_apply=%region_0.1 | all-reduce | flops 64 | bytes 512 | tf_op jit(solution)/shard_map/psum | solution.py:299
  136.2 2.4 fusion.42
  140.1 1.5 ge.45
  141.6 1.5 broadcast_in_dim_reshape.2.kcode_ref
  143.3 1.5 multiply_reduce_fusion.3
  149.9 2.7 and_reduce_fusion
  155.9 34.6 %shard_map.284 = bf16[1024,128]{1,0:T(8,128)(2,1)} custom-call(s32[9]{0:T(128)} %convert_element_type.91.flags_ref, bf16[1024,128]{1,0:T(8,128)(2,1)} %bitcast.84, bf16[9216,256]{1,0:T(8,128)(2,1)} %all-gather.3.cloned.1.call-done.kv_ref, s32[1,9216]{1,0:T(1,128)} %broadcast_in_dim_reshape.2.kcode_ref, s32[1024,1]{1,0:T(8,128)} %bitcast.80, s32[1024,1]{1,0:T(8,128)} %bitcast.82), custom_call_target="tpu_custom_call" | custom-call | tf_op jit(solution)/shard_map/pallas_call | solution.py:212
  191.5 8.7 %all-gather.5.cloned.1.call-done.kv_ref = bf16[9216,256]{1,0:T(8,128)(2,1)} async-done(((bf16[288,256]{1,0:T(8,128)(2,1)}), bf16[9216,256]{1,0:T(8,128)(2,1)}) %all-gather.5.cloned.1.call-update) | async-done | bytes 4718608 | tf_op jit(solution)/shard_map/all_gather | solution.py:355
  200.3 34.6 %shard_map.285 = bf16[1024,128]{1,0:T(8,128)(2,1)} custom-call(s32[9]{0:T(128)} %convert_element_type.91.flags_ref, bf16[1024,128]{1,0:T(8,128)(2,1)} %bitcast.85, bf16[9216,256]{1,0:T(8,128)(2,1)} %all-gather.5.cloned.1.call-done.kv_ref, s32[1,9216]{1,0:T(1,128)} %broadcast_in_dim_reshape.2.kcode_ref, s32[1024,1]{1,0:T(8,128)} %bitcast.81, s32[1024,1]{1,0:T(8,128)} %bitcast.83), custom_call_target="tpu_custom_call" | custom-call | tf_op jit(solution)/shard_map/pallas_call | solution.py:212
  234.9 1.8 copy.68
  236.7 3.8 convolution_convert_fusion.1
  240.5 2.0 convolution_convert_fusion
  242.5 62.7 %all-reduce.5.cloned.1.call-done = (bf16[256,2560]{1,0:T(8,128)(2,1)}, bf16[256,2560]{1,0:T(8,128)(2,1)}) async-done(((bf16[256,2560]{1,0:T(8,128)(2,1)}, bf16[256,2560]{1,0:T(8,128)(2,1)}), (bf16[256,2560]{1,0:T(8,128)(2,1)}, bf16[256,2560]{1,0:T(8,128)(2,1)})) %all-reduce.5.cloned.1.call-update) | async-done | bytes 2621456 | tf_op jit(solution)/shard_map/psum | solution.py:364
  305.1 2.4 multiply_reduce_fusion
  308.4 2.1 fusion.54
  310.6 2.1 fusion.55
  312.7 6.0 %all-reduce.1 = (f32[256]{0:T(256)S(1)}, f32[256]{0:T(256)S(1)}) all-reduce(f32[256]{0:T(256)S(1)} %get-tuple-element.48, f32[256]{0:T(256)S(1)} %get-tuple-element.50), channel_id=1, replica_groups=mesh['seq'=32,'vocab'=4] {'vocab'}, use_global_device_ids=true, to_apply=%region_27.28 | all-reduce | flops 512 | bytes 4096 | tf_op jit(solution)/shard_map/pmax | solution.py:379
  318.7 1.8 exponential_reduce_fusion.1
  320.4 5.7 %all-reduce = (f32[256]{0:T(256)S(1)}, f32[256]{0:T(256)S(1)}, f32[256]{0:T(256)S(1)}, f32[256]{0:T(256)S(1)}) all-reduce(f32[256]{0:T(256)S(1)} %get-tuple-element.31, f32[256]{0:T(256)S(1)} %get-tuple-element.32, f32[256]{0:T(256)S(1)} %get-tuple-element.3, f32[256]{0:T(256)S(1)} %get-tuple-element.2), channel_id=1, replica_groups=mesh['seq'=32,'vocab'=4] {'vocab'}, use_global_device_ids=true, to_apply=%region_25.26 | all-reduce | flops 1024 | bytes 8192 | tf_op jit(solution)/shard_map/psum | solution.py:382
  326.8 66.8 %psum.63 = f32[4]{0:T(128)} all-reduce(f32[4]{0:T(128)S(1)} %broadcast_select_fusion), channel_id=1, replica_groups=mesh['seq'=32,'vocab'=4] {'seq','vocab'}, use_global_device_ids=true, to_apply=%region_33.34 | all-reduce | flops 4 | bytes 32 | tf_op jit(solution)/shard_map/psum | solution.py:390
  (152 shorter events, 35.3 us)
Async XLA Ops:
  7.2 301.0 %copy-start = (bf16[2560,640]{1,0:T(8,128)(2,1)S(1)}, bf16[2560,640]{1,0:T(8,128)(2,1)}, u32[]{:S(2)}) copy-start(bf16[2560,640]{1,0:T(8,128)(2,1)} %param.55) | copy-start | bytes 9830404
  7.2 9.0 %copy-start.38 = (f32[2560]{0:T(1024)S(1)}, f32[2560]{0:T(1024)}, u32[]{:S(2)}) copy-start(f32[2560]{0:T(1024)} %param.36) | copy-start | bytes 30724
  7.2 148.7 %all-gather.3.cloned.1.call-start = ((), (), s32[]{:S(2)}) async-start(), calls=%async_computation | async-start | bytes 4866048 | tf_op jit(solution)/shard_map/all_gather | solution.py:346
  9.9 7.0 %copy-start.30 = (s32[4,1]{0,1:T(1,128)}, s32[4,1]{0,1:T(1,128)S(1)}, u32[]{:S(2)}) copy-start(s32[4,1]{0,1:T(1,128)S(1)} %reduce-window.8) | copy-start | bytes 52
  9.9 6.2 %copy-start.2 = (bf16[256,2560]{1,0:T(8,128)(2,1)S(1)}, bf16[256,2560]{1,0:T(8,128)(2,1)}, u32[]{:S(2)}) copy-start(bf16[256,2560]{1,0:T(8,128)(2,1)} %param.29) | copy-start | bytes 3932164
  9.9 6.3 %copy-start.37 = (bf16[2560,128]{1,0:T(8,128)(2,1)S(1)}, bf16[2560,128]{1,0:T(8,128)(2,1)}, u32[]{:S(2)}) copy-start(bf16[2560,128]{1,0:T(8,128)(2,1)} %param.38) | copy-start | bytes 1966084
  14.5 2.5 copy-start.34
  17.0 8.3 %copy-start.27 = (f32[128]{0:T(128)S(1)}, f32[128]{0:T(128)}, u32[]{:S(2)}) copy-start(f32[128]{0:T(128)} %param.41) | copy-start | bytes 1540
  20.4 5.0 %copy-start.26 = (f32[128]{0:T(128)S(1)}, f32[128]{0:T(128)}, u32[]{:S(2)}) copy-start(f32[128]{0:T(128)} %param.52) | copy-start | bytes 1540
  22.0 5.2 %copy-start.21 = (bf16[4,8,128]{2,1,0:T(8,128)(2,1)S(1)}, bf16[4,8,128]{2,1,0:T(8,128)(2,1)}, u32[]{:S(2)}) copy-start(bf16[4,8,128]{2,1,0:T(8,128)(2,1)} %param.46) | copy-start | bytes 24580
  22.0 5.2 %copy-start.22 = (bf16[4,8,128]{2,1,0:T(8,128)(2,1)S(1)}, bf16[4,8,128]{2,1,0:T(8,128)(2,1)}, u32[]{:S(2)}) copy-start(bf16[4,8,128]{2,1,0:T(8,128)(2,1)} %param.45) | copy-start | bytes 24580
  25.7 4.4 %copy-start.23 = (bf16[4,8,128]{2,1,0:T(8,128)(2,1)S(1)}, bf16[4,8,128]{2,1,0:T(8,128)(2,1)}, u32[]{:S(2)}) copy-start(bf16[4,8,128]{2,1,0:T(8,128)(2,1)} %param.57) | copy-start | bytes 24580
  27.2 2.9 copy-start.18
  28.0 172.3 %all-gather.5.cloned.1.call-start = ((), (), s32[]{:S(2)}) async-start(), calls=%async_computation.1 | async-start | bytes 4866048 | tf_op jit(solution)/shard_map/all_gather | solution.py:355
  31.5 8.0 %copy-start.33 = (f32[256]{0:T(256)S(1)}, f32[256]{0:T(256)}, u32[]{:S(2)}) copy-start(f32[256]{0:T(256)} %copy-done.32) | copy-start | bytes 3076
  31.5 8.0 %copy-start.39 = (f32[2560]{0:T(1024)S(1)}, f32[2560]{0:T(1024)}, u32[]{:S(2)}) copy-start(f32[2560]{0:T(1024)} %param.47) | copy-start | bytes 30724
  31.5 273.6 %all-reduce.5.cloned.1.call-start = ((), (), s32[]{:S(2)}) async-start(), calls=%async_computation.2 | async-start | bytes 5242880 | tf_op jit(solution)/shard_map/psum | solution.py:364
  43.4 99.8 %copy-start.12 = (f32[256,64]{1,0:T(8,128)S(1)}, f32[256,64]{1,0:T(8,128)}, u32[]{:S(2)}) copy-start(f32[256,64]{1,0:T(8,128)} %copy-done.11) | copy-start | bytes 196612
  43.4 99.8 %copy-start.14 = (f32[256,64]{1,0:T(8,128)S(1)}, f32[256,64]{1,0:T(8,128)}, u32[]{:S(2)}) copy-start(f32[256,64]{1,0:T(8,128)} %copy-done.13) | copy-start | bytes 196612
  138.7 7.6 %copy-start.29 = (f32[128]{0:T(128)S(1)}, f32[128]{0:T(128)}, u32[]{:S(2)}) copy-start(f32[128]{0:T(128)} %param.40) | copy-start | bytes 1540
  138.7 7.9 %copy-start.28 = (f32[128]{0:T(128)S(1)}, f32[128]{0:T(128)}, u32[]{:S(2)}) copy-start(f32[128]{0:T(128)} %param.51) | copy-start | bytes 1540
  143.2 3.1 copy-start.4
  143.2 3.5 copy-start.5
  236.7 3.8 copy-start.6
  236.7 3.8 copy-start.15
  242.4 65.7 %copy-start.40 = (f32[2560]{0:T(1024)S(1)}, f32[2560]{0:T(1024)}, u32[]{:S(2)}) copy-start(f32[2560]{0:T(1024)} %param.54) | copy-start | bytes 30724
  305.1 2.5 copy-start.9
  305.1 3.0 copy-start.1
  305.1 3.3 copy-start.10
  310.6 8.1 %copy-start.35 = (s32[256]{0:T(256)S(1)}, s32[256]{0:T(256)}, u32[]{:S(2)}) copy-start(s32[256]{0:T(256)} %param.31) | copy-start | bytes 3076
  310.6 15.5 %copy-start.24 = (s32[256]{0:T(256)S(1)}, s32[256]{0:T(256)}, u32[]{:S(2)}) copy-start(s32[256]{0:T(256)} %get-tuple-element.7) | copy-start | bytes 3076
  310.6 16.1 %copy-start.25 = (s32[256]{0:T(256)S(1)}, s32[256]{0:T(256)}, u32[]{:S(2)}) copy-start(s32[256]{0:T(256)} %get-tuple-element.6) | copy-start | bytes 3076
  (13 other events, 22.3 us)
Sparse Core Ops, SparseCore 0:
  28.1 87.6 all-gather.2
  118.9 81.3 all-gather.4
  242.6 62.5 all-reduce.4

commit v3 on v2

--- a/solution.py
+++ b/solution.py
@@ -215,6 +215,11 @@
         out_shape=jax.ShapeDtypeStruct((q_rows, HD), jnp.bfloat16),
         compiler_params=pltpu.CompilerParams(dimension_semantics=("arbitrary", "arbitrary")),
     )(flags, queries, stacked, key_code, query_low, query_high)
+
+
+def tile_flags(key_code, query_low, query_high):
+    seen = (key_code[None, :] >= query_low[:, None]) & (key_code[None, :] <= query_high[:, None])
+    return jnp.any(seen.reshape(query_low.shape[0], -1, K_TILE), axis=(0, 2)).astype(jnp.int32)
 
 
 def attend_model(query_rows, gathered, flags, key_code, query_low, query_high, out_weight):
@@ -291,29 +296,6 @@
     rope_offset = prefix_local * lax.axis_size("seq")
     prompt_ids = jnp.arange(prompt_rows, dtype=jnp.int32) // prefix_local
     seq_count = lax.axis_size("seq")
-    lead = lax.axis_index("vocab") == 0
-    source_slots = jnp.zeros((seq_count, block_source.shape[0]), jnp.int32)
-    source_slots = lax.dynamic_update_slice(
-        source_slots, jnp.where(lead, block_source, 0)[None, :], (lax.axis_index("seq"), 0)
-    )
-    all_source = lax.psum(source_slots, ("seq", "vocab")).reshape(-1)
-    all_ids = jnp.arange(tok_rows * seq_count, dtype=jnp.int32)
-    all_packed = jnp.repeat(all_source, BLOCK) * BLOCK + all_ids % BLOCK
-    all_rollout = jnp.sum((all_packed[:, None] >= end_points[None, :]).astype(jnp.int32), axis=1)
-    all_member = all_rollout[:, None] == roll_ids[None, :]
-    all_position = all_packed - lookup(all_member, end_points - lengths)
-    owner = lookup(rollout_prompt[None, :] == jnp.arange(prompt_count, dtype=jnp.int32)[:, None], roll_ids)
-    key_code = jnp.concatenate(
-        [
-            (all_rollout * CODE_STRIDE + all_position).reshape(seq_count, tok_rows),
-            jnp.broadcast_to(owner[prompt_ids] * CODE_STRIDE - 1, (seq_count, prompt_rows)),
-        ],
-        axis=1,
-    ).reshape(-1)
-    query_low = rollout * CODE_STRIDE - 1
-    query_high = rollout * CODE_STRIDE + position
-    seen = (key_code[None, :] >= query_low[:, None]) & (key_code[None, :] <= query_high[:, None])
-    flags = jnp.any(seen.reshape(tok_rows, -1, K_TILE), axis=(0, 2)).astype(jnp.int32)
     shard_rows = tok_rows + prompt_rows
     policy_query, policy_stack = project(
         policy_hidden,
@@ -341,11 +323,38 @@
         position,
         rope_offset,
     )
+    pad_rows = prompt_rows
+    carrier = jnp.zeros((pad_rows, policy_stack.shape[1]), jnp.bfloat16)
+    carrier = carrier.at[0, : block_source.shape[0]].set(block_source.astype(jnp.bfloat16))
+    policy_gathered = lax.all_gather(
+        jnp.concatenate([policy_stack, carrier], axis=0), "seq", axis=0, tiled=True
+    )
+    policy_rows = policy_stack.shape[0] + pad_rows
+    all_source = (
+        policy_gathered.reshape(seq_count, policy_rows, -1)[:, policy_stack.shape[0], : block_source.shape[0]]
+        .astype(jnp.int32)
+        .reshape(-1)
+    )
+    all_ids = jnp.arange(tok_rows * seq_count, dtype=jnp.int32)
+    all_packed = jnp.repeat(all_source, BLOCK) * BLOCK + all_ids % BLOCK
+    all_rollout = jnp.sum((all_packed[:, None] >= end_points[None, :]).astype(jnp.int32), axis=1)
+    all_member = all_rollout[:, None] == roll_ids[None, :]
+    all_position = all_packed - lookup(all_member, end_points - lengths)
+    owner = lookup(rollout_prompt[None, :] == jnp.arange(prompt_count, dtype=jnp.int32)[:, None], roll_ids)
+    token_code = (all_rollout * CODE_STRIDE + all_position).reshape(seq_count, tok_rows)
+    prompt_code = jnp.broadcast_to(owner[prompt_ids] * CODE_STRIDE - 1, (seq_count, prompt_rows))
+    never_code = jnp.full((seq_count, pad_rows), -(1 << 30), jnp.int32)
+    key_code = jnp.concatenate([token_code, prompt_code], axis=1).reshape(-1)
+    policy_code = jnp.concatenate([token_code, prompt_code, never_code], axis=1).reshape(-1)
+    query_low = rollout * CODE_STRIDE - 1
+    query_high = rollout * CODE_STRIDE + position
+    flags = tile_flags(key_code, query_low, query_high)
+    policy_flags = tile_flags(policy_code, query_low, query_high)
     policy_part = attend_model(
         policy_query,
-        lax.all_gather(policy_stack, "seq", axis=0, tiled=True),
-        flags,
-        key_code,
+        policy_gathered,
+        policy_flags,
+        policy_code,
         query_low,
         query_high,
         policy_out_weight,
@@ -387,7 +396,13 @@
     partial_sums = jnp.sum(
         jnp.where(slot_of[:, None] == roll_ids[None, :], per_token[:, None], 0.0), axis=0
     )
-    rollout_mean = lax.psum(jnp.where(lead, partial_sums, 0.0), ("seq", "vocab"))
+    rollout_mean = partial_sums
+    stride = 1
+    while stride < seq_count:
+        rollout_mean = rollout_mean + lax.ppermute(
+            rollout_mean, "seq", [(i, i ^ stride) for i in range(seq_count)]
+        )
+        stride *= 2
     return (token_diff, rollout_mean)
 
 

time: 402 us -> 364 us (0.905)
  blocking collectives: 156 us -> 11.6 us
  waiting for transfers between devices: 71.4 us -> 161 us
  starting transfers between devices: 0.12 us -> 12.7 us
    psum x2 -> x0, blocking collectives: 145 us -> none  [the longest x1 77.8 us: local(): all_source = lax.psum(source_slots, ('seq', 'vocab')).reshape(-1)]
    all_gather x1, waiting for transfers between devices: 0.01 us -> 56.4 us  [local(): lax.all_gather(jnp.concatenate([policy_stack, carrier], axis=0), 'seq', a...]
    all_gather x1, waiting for transfers between devices: 8.74 us -> 31.8 us  [local(): lax.all_gather(reference_stack, 'seq', axis=0, tiled=True)]
    ppermute x0 -> x5, starting transfers between devices: none -> 12.6 us  [local(): lax.ppermute(rollout_mean, 'seq', [(i, i ^ stride) for i in range(seq_cou...]
    ppermute x0 -> x5, waiting for transfers between devices: none -> 9.85 us  [local(): lax.ppermute(rollout_mean, 'seq', [(i, i ^ stride) for i in range(seq_cou...]
  transfers between devices with their start and end apart: 3 -> 8, of which waited for: 2 -> 8; matrix products, arithmetic and copies ran while one was open for 13% -> 13% of each run, Pallas kernels for 9% -> 11%
where the time goes in v3:
time: 364 us; the launch traced here: 362 us
  waiting for transfers between devices  161 us (44%)
  Pallas kernels  72.7 us (20%)
  other arithmetic  40.9 us (11%)
  matrix products  28.2 us (8%)
  local copies, waits for them, and re-layouts  21.2 us (6%)
  between operations  14.2 us (4%)
  starting transfers between devices  12.7 us (3%)
  blocking collectives  11.6 us (3%)
    pallas_call x2, Pallas kernels, flash_attend(): pl.pallas_call(flash_kernel, grid_spec=grid_spec, out_shape=jax.ShapeDtyp...  72.7 us
    psum x1, waiting for transfers between devices, local(): lax.psum(reference_part.astype(jnp.bfloat16), 'vocab').astype(jnp.float32)  62.7 us
    all_gather x1, waiting for transfers between devices, local(): lax.all_gather(jnp.concatenate([policy_stack, carrier], axis=0), 'seq', a...  56.4 us
    all_gather x1, waiting for transfers between devices, local(): lax.all_gather(reference_stack, 'seq', axis=0, tiled=True)  31.8 us
    ppermute x5, starting transfers between devices, local(): lax.ppermute(rollout_mean, 'seq', [(i, i ^ stride) for i in range(seq_cou...  12.6 us
    ppermute x5, waiting for transfers between devices, local(): lax.ppermute(rollout_mean, 'seq', [(i, i ^ stride) for i in range(seq_cou...  9.85 us
    reduce_sum x6, other arithmetic, rms_scale(): jnp.mean(values * values, axis=-1, keepdims=True) + EPSILON  8.96 us
    reshape x4, local copies, waits for them, and re-layouts, project(): jnp.dot(normed, query_weight, preferred_element_type=jnp.float32)  8.09 us
  transfers between devices with their start and end apart: 8, of which 8 were waited for; matrix products, arithmetic and copies ran while one was open for 13% of the time, Pallas kernels for 11%

profile of v3, /device:TPU:0, one launch (start us, length us, event | category | flops | bytes accessed | tf_op | source)
XLA Modules:
  0.0 362.4 jit_solution(15789739969017044128)
XLA Ops:
  14.0 2.8 multiply_reduce_fusion.5
  19.3 3.4 multiply_reduce_fusion.4
  24.3 2.1 convolution_convert_fusion.3
  31.8 2.1 convolution_convert_fusion.2
  35.3 3.9 %fusion.50 = f32[256,512]{1,0:T(8,128)} fusion(bf16[2560,512]{1,0:T(8,128)(2,1)} %param.39, bf16[256,2560]{1,0:T(8,128)(2,1)} %param.31, f32[2560]{0:T(1024)} %param.38, f32[256]{0:T(256)S(1)} %copy-done.25), kind=kOutput, calls=%fused_computation.143 | convolution fusion | flops 673710080 | bytes 4467712 | tf_op jit(solution)/shard_map/dot_general | solution.py:56
  39.2 2.0 reshape.535
  41.2 2.0 reshape.534
  43.2 4.0 %fusion.48 = f32[256,512]{1,0:T(8,128)} fusion(bf16[2560,512]{1,0:T(8,128)(2,1)} %param.50, bf16[256,2560]{1,0:T(8,128)(2,1)} %param.32, f32[2560]{0:T(1024)} %param.49, f32[256]{0:T(256)S(1)} %copy-done.27), kind=kOutput, calls=%fused_computation.142 | convolution fusion | flops 673710080 | bytes 4467712 | tf_op jit(solution)/shard_map/dot_general | solution.py:56
  47.2 2.0 reshape.540
  49.3 2.0 reshape.539
  62.9 2.5 fusion.43
  65.4 56.4 %all-gather.3.cloned.1.call-done.kv_ref = bf16[10240,256]{1,0:T(8,128)(2,1)} async-done(((bf16[320,256]{1,0:T(8,128)(2,1)}), bf16[10240,256]{1,0:T(8,128)(2,1)}) %all-gather.3.cloned.1.call-update) | async-done | bytes 5242896 | tf_op jit(solution)/shard_map/all_gather | solution.py:329
  127.9 2.9 and_reduce_fusion
  131.4 38.1 %shard_map.284 = bf16[1024,128]{1,0:T(8,128)(2,1)} custom-call(s32[10]{0:T(128)} %convert_element_type.110.flags_ref, bf16[1024,128]{1,0:T(8,128)(2,1)} %bitcast.91, bf16[10240,256]{1,0:T(8,128)(2,1)} %all-gather.3.cloned.1.call-done.kv_ref, s32[1,10240]{1,0:T(1,128)} %broadcast_in_dim_reshape.4.kcode_ref, s32[1024,1]{1,0:T(8,128)} %bitcast.86, ...), custom_call_target="tpu_custom_call" | custom-call | tf_op jit(solution)/shard_map/pallas_call | solution.py:212
  170.6 3.5 and_reduce_fusion.1
  174.6 31.8 %all-gather.5.cloned.1.call-done.kv_ref = bf16[9216,256]{1,0:T(8,128)(2,1)} async-done(((bf16[288,256]{1,0:T(8,128)(2,1)}), bf16[9216,256]{1,0:T(8,128)(2,1)}) %all-gather.5.cloned.1.call-update) | async-done | bytes 4718608 | tf_op jit(solution)/shard_map/all_gather | solution.py:364
  206.4 34.6 %shard_map.285 = bf16[1024,128]{1,0:T(8,128)(2,1)} custom-call(s32[9]{0:T(128)} %convert_element_type.116.flags_ref, bf16[1024,128]{1,0:T(8,128)(2,1)} %bitcast.90, bf16[9216,256]{1,0:T(8,128)(2,1)} %all-gather.5.cloned.1.call-done.kv_ref, s32[1,9216]{1,0:T(1,128)} %broadcast_in_dim_reshape.5.kcode_ref, s32[1024,1]{1,0:T(8,128)} %bitcast.87, s32[1024,1]{1,0:T(8,128)} %bitcast.89), custom_call_target="tpu_custom_call" | custom-call | tf_op jit(solution)/shard_map/pallas_call | solution.py:212
  242.8 3.8 %convolution_convert_fusion.1 = bf16[256,2560]{1,0:T(8,128)(2,1)} fusion(bf16[256,512]{0,1:T(8,128)(2,1)S(1)} %bitcast.92, bf16[512,2560]{1,0:T(8,128)(2,1)} %param.44), kind=kOutput, calls=%fused_computation.9 | convolution fusion | flops 671744000 | bytes 4194304 | tf_op jit(solution)/shard_map/dot_general | solution.py:233
  246.6 2.0 convolution_convert_fusion
  248.6 62.7 %all-reduce.6.cloned.1.call-done = (bf16[256,2560]{1,0:T(8,128)(2,1)}, bf16[256,2560]{1,0:T(8,128)(2,1)}) async-done(((bf16[256,2560]{1,0:T(8,128)(2,1)}, bf16[256,2560]{1,0:T(8,128)(2,1)}), (bf16[256,2560]{1,0:T(8,128)(2,1)}, bf16[256,2560]{1,0:T(8,128)(2,1)})) %all-reduce.6.cloned.1.call-update) | async-done | bytes 2621456 | tf_op jit(solution)/shard_map/psum | solution.py:373
  311.3 2.4 multiply_reduce_fusion
  314.5 2.1 fusion.56
  316.7 2.1 fusion.57
  318.8 6.0 %all-reduce.2 = (f32[256]{0:T(256)S(1)}, f32[256]{0:T(256)S(1)}) all-reduce(f32[256]{0:T(256)S(1)} %get-tuple-element.62, f32[256]{0:T(256)S(1)} %get-tuple-element.64), channel_id=1, replica_groups=mesh['seq'=32,'vocab'=4] {'vocab'}, use_global_device_ids=true, to_apply=%region_27.28 | all-reduce | flops 512 | bytes 4096 | tf_op jit(solution)/shard_map/pmax | solution.py:388
  326.5 5.7 %all-reduce.1 = (f32[256]{0:T(256)S(1)}, f32[256]{0:T(256)S(1)}, f32[256]{0:T(256)S(1)}, f32[256]{0:T(256)S(1)}) all-reduce(f32[256]{0:T(256)S(1)} %get-tuple-element.43, f32[256]{0:T(256)S(1)} %get-tuple-element.44, f32[256]{0:T(256)S(1)} %get-tuple-element.15, ...), channel_id=1, replica_groups=mesh['seq'=32,'vocab'=4] {'vocab'}, use_global_device_ids=true, to_apply=%region_25.26 | all-reduce | flops 1024 | bytes 8192 | tf_op jit(solution)/shard_map/psum | solution.py:391
  334.5 2.0 collective-permute-done
  336.5 3.1 collective-permute-start.1
  339.6 2.0 collective-permute-done.1
  343.2 2.0 collective-permute-done.2
  345.2 3.1 collective-permute-start.3
  348.3 2.0 collective-permute-done.3
  350.3 3.2 collective-permute-start.4
  (155 shorter events, 48.0 us)
Async XLA Ops:
  7.2 307.1 %copy-start = (bf16[2560,640]{1,0:T(8,128)(2,1)S(1)}, bf16[2560,640]{1,0:T(8,128)(2,1)}, u32[]{:S(2)}) copy-start(bf16[2560,640]{1,0:T(8,128)(2,1)} %param.57) | copy-start | bytes 9830404
  7.2 114.6 %all-gather.3.cloned.1.call-start = ((), (), s32[]{:S(2)}) async-start(), calls=%async_computation | async-start | bytes 5406720 | tf_op jit(solution)/shard_map/all_gather | solution.py:329
  10.2 6.6 %copy-start.22 = (s32[4,1]{0,1:T(1,128)}, s32[4,1]{0,1:T(1,128)S(1)}, u32[]{:S(2)}) copy-start(s32[4,1]{0,1:T(1,128)S(1)} %reduce-window.8) | copy-start | bytes 52
  19.2 3.4 copy-start.26
  24.3 6.6 %copy-start.16 = (bf16[4,8,128]{2,1,0:T(8,128)(2,1)S(1)}, bf16[4,8,128]{2,1,0:T(8,128)(2,1)}, u32[]{:S(2)}) copy-start(bf16[4,8,128]{2,1,0:T(8,128)(2,1)} %param.48) | copy-start | bytes 24580
  24.3 6.7 %copy-start.17 = (bf16[4,8,128]{2,1,0:T(8,128)(2,1)S(1)}, bf16[4,8,128]{2,1,0:T(8,128)(2,1)}, u32[]{:S(2)}) copy-start(bf16[4,8,128]{2,1,0:T(8,128)(2,1)} %param.47) | copy-start | bytes 24580
  24.3 6.7 %copy-start.29 = (bf16[1,2]{1,0:T(2,128)(2,1)S(1)}, bf16[1,2]{1,0:T(2,128)(2,1)}, u32[]{:S(2)}) copy-start(bf16[1,2]{1,0:T(2,128)(2,1)} %get-tuple-element.52) | copy-start | bytes 16
  27.6 3.3 copy-start.10
  27.7 3.3 copy-start.12
  29.4 6.0 %copy-start.25 = (f32[256]{0:T(256)S(1)}, f32[256]{0:T(256)}, u32[]{:S(2)}) copy-start(f32[256]{0:T(256)} %copy-done.24) | copy-start | bytes 3076
  31.7 174.7 %all-gather.5.cloned.1.call-start = ((), (), s32[]{:S(2)}) async-start(), calls=%async_computation.1 | async-start | bytes 4866048 | tf_op jit(solution)/shard_map/all_gather | solution.py:364
  35.3 8.0 %copy-start.27 = (f32[256]{0:T(256)S(1)}, f32[256]{0:T(256)}, u32[]{:S(2)}) copy-start(f32[256]{0:T(256)} %copy-done.26) | copy-start | bytes 3076
  35.3 276.0 %all-reduce.6.cloned.1.call-start = ((), (), s32[]{:S(2)}) async-start(), calls=%async_computation.2 | async-start | bytes 5242880 | tf_op jit(solution)/shard_map/psum | solution.py:373
  43.2 8.7 %copy-start.11 = (f32[256,64]{1,0:T(8,128)S(1)}, f32[256,64]{1,0:T(8,128)}, u32[]{:S(2)}) copy-start(f32[256,64]{1,0:T(8,128)} %copy-done.10) | copy-start | bytes 196612
  43.2 8.7 %copy-start.13 = (f32[256,64]{1,0:T(8,128)S(1)}, f32[256,64]{1,0:T(8,128)}, u32[]{:S(2)}) copy-start(f32[256,64]{1,0:T(8,128)} %copy-done.12) | copy-start | bytes 196612
  47.2 7.7 %copy-start.20 = (f32[128]{0:T(128)S(1)}, f32[128]{0:T(128)}, u32[]{:S(2)}) copy-start(f32[128]{0:T(128)} %param.53) | copy-start | bytes 1540
  47.2 8.1 %copy-start.21 = (f32[128]{0:T(128)S(1)}, f32[128]{0:T(128)}, u32[]{:S(2)}) copy-start(f32[128]{0:T(128)} %param.42) | copy-start | bytes 1540
  51.3 3.7 %copy-start.4 = (f32[256,4,128]{2,1,0:T(4,128)S(1)}, f32[256,4,128]{2,1,0:T(4,128)}, u32[]{:S(2)}) copy-start(f32[256,4,128]{2,1,0:T(4,128)} %reshape.540) | copy-start | bytes 1572868
  51.3 4.1 %copy-start.3 = (f32[256,4,128]{2,1,0:T(4,128)S(1)}, f32[256,4,128]{2,1,0:T(4,128)}, u32[]{:S(2)}) copy-start(f32[256,4,128]{2,1,0:T(4,128)} %reshape.535) | copy-start | bytes 1572868
  242.8 3.8 %copy-start.5 = (bf16[512,2560]{1,0:T(8,128)(2,1)S(1)}, bf16[512,2560]{1,0:T(8,128)(2,1)}, u32[]{:S(2)}) copy-start(bf16[512,2560]{1,0:T(8,128)(2,1)} %param.55) | copy-start | bytes 7864324
  242.8 3.8 %copy-start.14 = (bf16[1,4,256,128]{2,3,1,0:T(8,128)(2,1)S(1)}, bf16[1,4,256,128]{2,3,1,0:T(8,128)(2,1)}, u32[]{:S(2)}) copy-start(bf16[1,4,256,128]{2,3,1,0:T(8,128)(2,1)} %copy.80) | copy-start | bytes 786436
  248.5 65.7 %copy-start.31 = (f32[2560]{0:T(1024)S(1)}, f32[2560]{0:T(1024)}, u32[]{:S(2)}) copy-start(f32[2560]{0:T(1024)} %param.56) | copy-start | bytes 30724
  311.3 3.0 copy-start.1
  311.3 3.3 copy-start.9
  316.7 8.1 %copy-start.28 = (s32[256]{0:T(256)S(1)}, s32[256]{0:T(256)}, u32[]{:S(2)}) copy-start(s32[256]{0:T(256)} %param.33) | copy-start | bytes 3076
  316.7 15.5 %copy-start.18 = (s32[256]{0:T(256)S(1)}, s32[256]{0:T(256)}, u32[]{:S(2)}) copy-start(s32[256]{0:T(256)} %get-tuple-element.19) | copy-start | bytes 3076
  316.7 16.1 %copy-start.19 = (s32[256]{0:T(256)S(1)}, s32[256]{0:T(256)}, u32[]{:S(2)}) copy-start(s32[256]{0:T(256)} %get-tuple-element.18) | copy-start | bytes 3076
  332.9 3.6 %collective-permute-start = (f32[4]{0:T(128)S(1)}, f32[4]{0:T(128)S(1)}, u32[]{:S(2)}, u32[]{:S(2)}) collective-permute-start(f32[4]{0:T(128)S(1)} %select_reduce_fusion.1), channel_id=1, source_target_pairs={{0,4},{4,0},{8,12},{12,8},{16,20},{20,16},{24,28},{28,24},{32,36},... | collective-permute-start | bytes 56 | tf_op jit(solution)/shard_map/ppermute | solution.py:402
  336.5 5.1 %collective-permute-start.1 = (f32[4]{0:T(128)S(1)}, f32[4]{0:T(128)S(1)}, u32[]{:S(2)}, u32[]{:S(2)}) collective-permute-start(f32[4]{0:T(128)S(1)} %add.293), channel_id=1, source_target_pairs={{0,8},{4,12},{8,0},{12,4},{16,24},{20,28},{24,16},{28,20},{32,40},... | collective-permute-start | bytes 56 | tf_op jit(solution)/shard_map/ppermute | solution.py:402
  341.6 3.6 collective-permute-start.2
  345.2 5.1 %collective-permute-start.3 = (f32[4]{0:T(128)S(1)}, f32[4]{0:T(128)S(1)}, u32[]{:S(2)}, u32[]{:S(2)}) collective-permute-start(f32[4]{0:T(128)S(1)} %add.295), channel_id=1, source_target_pairs={{0,32},{4,36},{8,40},{12,44},{16,48},{20,52},{24,56},{28,60},{32,0... | collective-permute-start | bytes 56 | tf_op jit(solution)/shard_map/ppermute | solution.py:402
  350.3 5.1 %collective-permute-start.4 = (f32[4]{0:T(128)S(1)}, f32[4]{0:T(128)S(1)}, u32[]{:S(2)}, u32[]{:S(2)}) collective-permute-start(f32[4]{0:T(128)S(1)} %add.296), channel_id=1, source_target_pairs={{0,64},{4,68},{8,72},{12,76},{16,80},{20,84},{24,88},{28,92},{32,9... | collective-permute-start | bytes 56 | tf_op jit(solution)/shard_map/ppermute | solution.py:402
  (9 other events, 18.6 us)
Sparse Core Ops, SparseCore 0:
  31.8 89.9 all-gather.2
  124.9 81.4 all-gather.4
  248.7 62.5 all-reduce.5

commit v4 on v3

--- a/solution.py
+++ b/solution.py
@@ -368,10 +368,10 @@
         query_high,
         reference_out_weight,
     )
-    policy_mixed, reference_mixed = (
-        lax.psum(policy_part.astype(jnp.bfloat16), "vocab").astype(jnp.float32),
-        lax.psum(reference_part.astype(jnp.bfloat16), "vocab").astype(jnp.float32),
-    )
+    policy_summed = lax.psum(policy_part.astype(jnp.bfloat16), "vocab")
+    policy_summed, reference_part = lax.optimization_barrier((policy_summed, reference_part))
+    policy_mixed = policy_summed.astype(jnp.float32)
+    reference_mixed = lax.psum(reference_part.astype(jnp.bfloat16), "vocab").astype(jnp.float32)
     policy_final = rms_scale(
         policy_hidden.astype(jnp.float32) + policy_mixed, policy_final_gain
     ).astype(jnp.bfloat16)

time: 364 us -> 350 us (0.962)
  waiting for transfers between devices: 161 us -> 127 us
  other arithmetic: 40.9 us -> 51.1 us
  local copies, waits for them, and re-layouts: 21.2 us -> 28.9 us
    all_gather x1, waiting for transfers between devices: 31.8 us -> 12.5 us  [local(): lax.all_gather(reference_stack, 'seq', axis=0, tiled=True)]
    psum x1, waiting for transfers between devices: 62.7 us -> 43.3 us  [local(): lax.psum(reference_part.astype(jnp.bfloat16), 'vocab').astype(jnp.float32)]
    psum x0 -> x1, waiting for transfers between devices: none -> 4.53 us  [local(): policy_summed = lax.psum(policy_part.astype(jnp.bfloat16), 'vocab')]
  transfers between devices with their start and end apart: 8 -> 9, of which waited for: 8 -> 9; matrix products, arithmetic and copies ran while one was open for 13% -> 22% of each run, Pallas kernels for 11% -> 21%
where the time goes in v4:
time: 350 us; the launch traced here: 348 us
  waiting for transfers between devices  127 us (36%)
  Pallas kernels  72.6 us (21%)
  other arithmetic  51.1 us (15%)
  matrix products  29.8 us (9%)
  local copies, waits for them, and re-layouts  28.9 us (8%)
  between operations  14.2 us (4%)
  starting transfers between devices  13.1 us (4%)
  blocking collectives  11.5 us (3%)
    pallas_call x2, Pallas kernels, flash_attend(): pl.pallas_call(flash_kernel, grid_spec=grid_spec, out_shape=jax.ShapeDtyp...  72.6 us
    all_gather x1, waiting for transfers between devices, local(): lax.all_gather(jnp.concatenate([policy_stack, carrier], axis=0), 'seq', a...  56.4 us
    psum x1, waiting for transfers between devices, local(): lax.psum(reference_part.astype(jnp.bfloat16), 'vocab').astype(jnp.float32)  43.3 us
    ppermute x5, starting transfers between devices, local(): lax.ppermute(rollout_mean, 'seq', [(i, i ^ stride) for i in range(seq_cou...  12.5 us
    all_gather x1, waiting for transfers between devices, local(): lax.all_gather(reference_stack, 'seq', axis=0, tiled=True)  12.5 us
    reduce_sum x6, other arithmetic, rms_scale(): jnp.mean(values * values, axis=-1, keepdims=True) + EPSILON  10.8 us
    ppermute x5, waiting for transfers between devices, local(): lax.ppermute(rollout_mean, 'seq', [(i, i ^ stride) for i in range(seq_cou...  9.9 us
    reshape x4, local copies, waits for them, and re-layouts, project(): jnp.dot(normed, query_weight, preferred_element_type=jnp.float32)  8.09 us
  transfers between devices with their start and end apart: 9, of which 9 were waited for; matrix products, arithmetic and copies ran while one was open for 22% of the time, Pallas kernels for 21%

profile of v4, /device:TPU:0, one launch (start us, length us, event | category | flops | bytes accessed | tf_op | source)
XLA Modules:
  0.0 348.0 jit_solution(17343041275645159754)
XLA Ops:
  16.1 2.8 convolution_convert_fusion.2
  18.9 2.6 multiply_reduce_fusion.5
  31.4 2.1 convolution_convert_fusion.1
  35.2 3.9 %fusion.48 = f32[256,512]{1,0:T(8,128)} fusion(bf16[2560,512]{1,0:T(8,128)(2,1)} %param.50, bf16[256,2560]{1,0:T(8,128)(2,1)} %param.32, f32[2560]{0:T(1024)} %param.49, f32[256]{0:T(256)} %copy-done.29), kind=kOutput, calls=%fused_computation.141 | convolution fusion | flops 673710080 | bytes 4467712 | tf_op jit(solution)/shard_map/dot_general | solution.py:56
  39.0 2.0 reshape.540
  41.1 2.0 reshape.539
  43.1 4.0 %fusion.50 = f32[256,512]{1,0:T(8,128)} fusion(bf16[2560,512]{1,0:T(8,128)(2,1)} %param.39, bf16[256,2560]{1,0:T(8,128)(2,1)} %param.31, f32[2560]{0:T(1024)} %param.38, f32[256]{0:T(256)S(1)} %copy-done.28), kind=kOutput, calls=%fused_computation.142 | convolution fusion | flops 673710080 | bytes 4467712 | tf_op jit(solution)/shard_map/dot_general | solution.py:56
  47.1 2.0 reshape.535
  49.1 2.0 reshape.534
  62.0 3.1 fusion.43
  65.1 56.4 %all-gather.3.cloned.1.call-done.kv_ref = bf16[10240,256]{1,0:T(8,128)(2,1)} async-done(((bf16[320,256]{1,0:T(8,128)(2,1)}), bf16[10240,256]{1,0:T(8,128)(2,1)}) %all-gather.3.cloned.1.call-update) | async-done | bytes 5242896 | tf_op jit(solution)/shard_map/all_gather | solution.py:329
  139.2 3.7 %and_reduce_fusion = pred[10]{0:T(512)(128)(4,1)S(1)} fusion(s32[10,1024]{1,0:T(8,128)} %ge.64, s32[256]{0:T(256)} %copy-done.19, s32[256]{0:T(256)} %copy-done.20), kind=kLoop, calls=%fused_computation | loop fusion | flops 10485750 | bytes 43018 | tf_op jit(solution)/shard_map/reduce_or | solution.py:222
  143.4 38.1 %shard_map.284 = bf16[1024,128]{1,0:T(8,128)(2,1)} custom-call(s32[10]{0:T(128)} %convert_element_type.110.flags_ref, bf16[1024,128]{1,0:T(8,128)(2,1)} %bitcast.90, bf16[10240,256]{1,0:T(8,128)(2,1)} %all-gather.3.cloned.1.call-done.kv_ref, s32[1,10240]{1,0:T(1,128)} %broadcast_in_dim_reshape.4.kcode_ref, s32[1024,1]{1,0:T(8,128)} %bitcast.86, ...), custom_call_target="tpu_custom_call" | custom-call | tf_op jit(solution)/shard_map/pallas_call | solution.py:212
  183.3 3.8 %convolution_convert_fusion = bf16[256,2560]{1,0:T(8,128)(2,1)} fusion(bf16[256,512]{0,1:T(8,128)(2,1)} %bitcast.94, bf16[512,2560]{1,0:T(8,128)(2,1)} %param.44), kind=kOutput, calls=%fused_computation.8 | convolution fusion | flops 671744000 | bytes 4194304 | tf_op jit(solution)/shard_map/dot_general | solution.py:233
  189.7 3.3 and_reduce_fusion.1
  193.6 12.5 %all-gather.5.cloned.1.call-done.kv_ref = bf16[9216,256]{1,0:T(8,128)(2,1)} async-done(((bf16[288,256]{1,0:T(8,128)(2,1)}), bf16[9216,256]{1,0:T(8,128)(2,1)}) %all-gather.5.cloned.1.call-update) | async-done | bytes 4718608 | tf_op jit(solution)/shard_map/all_gather | solution.py:364
  206.0 34.6 %shard_map.285 = bf16[1024,128]{1,0:T(8,128)(2,1)} custom-call(s32[9]{0:T(128)} %convert_element_type.113.flags_ref, bf16[1024,128]{1,0:T(8,128)(2,1)} %bitcast.91, bf16[9216,256]{1,0:T(8,128)(2,1)} %all-gather.5.cloned.1.call-done.kv_ref, s32[1,9216]{1,0:T(1,128)} %broadcast_in_dim_reshape.5.kcode_ref, s32[1024,1]{1,0:T(8,128)} %bitcast.87, s32[1024,1]{1,0:T(8,128)} %bitcast.89), custom_call_target="tpu_custom_call" | custom-call | tf_op jit(solution)/shard_map/pallas_call | solution.py:212
  241.7 3.7 %fusion.58 = bf16[256,2560]{1,0:T(8,128)(2,1)} fusion(bf16[256,512]{0,1:T(8,128)(2,1)S(1)} %bitcast.95, bf16[512,2560]{1,0:T(8,128)(2,1)} %param.55), kind=kOutput, calls=%fused_computation.147 | convolution fusion | flops 671088640 | bytes 4194304 | tf_op jit(solution)/shard_map/dot_general | solution.py:233
  245.4 4.5 %all-reduce.6.cloned.1.call-done = bf16[256,2560]{1,0:T(8,128)(2,1)} async-done(((bf16[256,2560]{1,0:T(8,128)(2,1)}), bf16[256,2560]{1,0:T(8,128)(2,1)}) %all-reduce.6.cloned.1.call-update) | async-done | bytes 1310736 | tf_op jit(solution)/shard_map/psum | solution.py:371
  250.0 2.4 multiply_reduce_fusion.1
  252.5 2.1 fusion.57
  254.6 43.3 %all-reduce.8.cloned.1.call-done = bf16[256,2560]{1,0:T(8,128)(2,1)} async-done(((bf16[256,2560]{1,0:T(8,128)(2,1)}), bf16[256,2560]{1,0:T(8,128)(2,1)}) %all-reduce.8.cloned.1.call-update) | async-done | bytes 1310736 | tf_op jit(solution)/shard_map/psum | solution.py:374
  297.9 2.4 multiply_reduce_fusion
  300.4 4.1 %fusion.56 = (f32[256]{0:T(256)S(1)}, f32[256,640]{1,0:T(8,128)}) fusion(bf16[2560,640]{1,0:T(8,128)(2,1)} %param.57, bf16[256,2560]{1,0:T(8,128)(2,1)S(1)} %copy-done.10, bf16[256,2560]{1,0:T(8,128)(2,1)S(1)} %copy-done.4, f32[2560]{0:T(1024)S(1)} %copy-done.36, f32[256]{0:T(256)S(1)} %add_rsqrt_fusion.2), kind=kOutput, calls=%fused_computation.145 | convolution fusion | flops 842956544 | bytes 6565888 | tf_op jit(solution)/shard_map/dot_general | solution.py:244
  304.5 5.9 %all-reduce.2 = (f32[256]{0:T(256)S(1)}, f32[256]{0:T(256)S(1)}) all-reduce(f32[256]{0:T(256)S(1)} %get-tuple-element.64, f32[256]{0:T(256)S(1)} %get-tuple-element.66), channel_id=1, replica_groups=mesh['seq'=32,'vocab'=4] {'vocab'}, use_global_device_ids=true, to_apply=%region_27.28 | all-reduce | flops 512 | bytes 4096 | tf_op jit(solution)/shard_map/pmax | solution.py:388
  312.2 5.7 %all-reduce.1 = (f32[256]{0:T(256)S(1)}, f32[256]{0:T(256)S(1)}, f32[256]{0:T(256)S(1)}, f32[256]{0:T(256)S(1)}) all-reduce(f32[256]{0:T(256)S(1)} %get-tuple-element.45, f32[256]{0:T(256)S(1)} %get-tuple-element.46, f32[256]{0:T(256)S(1)} %get-tuple-element.19, ...), channel_id=1, replica_groups=mesh['seq'=32,'vocab'=4] {'vocab'}, use_global_device_ids=true, to_apply=%region_25.26 | all-reduce | flops 1024 | bytes 8192 | tf_op jit(solution)/shard_map/psum | solution.py:391
  320.2 2.0 collective-permute-done
  322.2 3.1 collective-permute-start.1
  328.8 2.0 collective-permute-done.2
  330.8 3.1 collective-permute-start.3
  333.9 2.0 collective-permute-done.3
  335.9 3.2 collective-permute-start.4
  (166 shorter events, 65.4 us)
Async XLA Ops:
  7.2 245.2 %copy-start = (bf16[2560,640]{1,0:T(8,128)(2,1)S(1)}, bf16[2560,640]{1,0:T(8,128)(2,1)}, u32[]{:S(2)}) copy-start(bf16[2560,640]{1,0:T(8,128)(2,1)} %param.46) | copy-start | bytes 9830404
  7.2 8.0 %copy-start.34 = (f32[2560]{0:T(1024)S(1)}, f32[2560]{0:T(1024)}, u32[]{:S(2)}) copy-start(f32[2560]{0:T(1024)} %param.49) | copy-start | bytes 30724
  7.2 114.3 %all-gather.3.cloned.1.call-start = ((), (), s32[]{:S(2)}) async-start(), calls=%async_computation | async-start | bytes 5406720 | tf_op jit(solution)/shard_map/all_gather | solution.py:329
  10.5 12.7 %copy-start.26 = (s32[4,1]{0,1:T(1,128)}, s32[4,1]{0,1:T(1,128)S(1)}, u32[]{:S(2)}) copy-start(s32[4,1]{0,1:T(1,128)S(1)} %reduce-window.8) | copy-start | bytes 52
  10.5 4.7 %copy-start.3 = (bf16[256,2560]{1,0:T(8,128)(2,1)S(1)}, bf16[256,2560]{1,0:T(8,128)(2,1)}, u32[]{:S(2)}) copy-start(bf16[256,2560]{1,0:T(8,128)(2,1)} %param.32) | copy-start | bytes 3932164
  10.5 4.7 %copy-start.32 = (bf16[2560,128]{1,0:T(8,128)(2,1)S(1)}, bf16[2560,128]{1,0:T(8,128)(2,1)}, u32[]{:S(2)}) copy-start(bf16[2560,128]{1,0:T(8,128)(2,1)} %param.51) | copy-start | bytes 1966084
  11.3 12.7 %copy-start.27 = (s32[4]{0:T(128)}, s32[4]{0:T(128)S(1)}, u32[]{:S(2)}) copy-start(s32[4]{0:T(128)S(1)} %bitcast_subtract_fusion) | copy-start | bytes 52
  16.1 10.0 %copy-start.23 = (f32[128]{0:T(128)S(1)}, f32[128]{0:T(128)}, u32[]{:S(2)}) copy-start(f32[128]{0:T(128)} %param.54) | copy-start | bytes 1540
  22.5 7.4 %copy-start.18 = (bf16[256,128]{1,0:T(8,128)(2,1)S(1)}, bf16[256,128]{1,0:T(8,128)(2,1)}, u32[]{:S(2)}) copy-start(bf16[256,128]{1,0:T(8,128)(2,1)} %convolution_convert_fusion.2) | copy-start | bytes 196612
  26.1 32.3 %copy-start.19 = (s32[256]{0:T(256)}, s32[256]{0:T(256)S(1)}, u32[]{:S(2)}) copy-start(s32[256]{0:T(256)S(1)} %get-tuple-element.47) | copy-start | bytes 3076
  26.1 32.3 %copy-start.20 = (s32[256]{0:T(256)}, s32[256]{0:T(256)S(1)}, u32[]{:S(2)}) copy-start(s32[256]{0:T(256)S(1)} %get-tuple-element.51) | copy-start | bytes 3076
  29.9 3.6 %copy-start.17 = (bf16[256,128]{1,0:T(8,128)(2,1)S(1)}, bf16[256,128]{1,0:T(8,128)(2,1)}, u32[]{:S(2)}) copy-start(bf16[256,128]{1,0:T(8,128)(2,1)} %get-tuple-element.37) | copy-start | bytes 196612
  31.4 174.7 %all-gather.5.cloned.1.call-start = ((), (), s32[]{:S(2)}) async-start(), calls=%async_computation.2 | async-start | bytes 4866048 | tf_op jit(solution)/shard_map/all_gather | solution.py:364
  34.9 8.2 %copy-start.28 = (f32[256]{0:T(256)S(1)}, f32[256]{0:T(256)}, u32[]{:S(2)}) copy-start(f32[256]{0:T(256)} %add_rsqrt_fusion.7) | copy-start | bytes 3076
  34.9 215.0 %all-reduce.6.cloned.1.call-start = ((), (), s32[]{:S(2)}) async-start(), calls=%async_computation.1 | async-start | bytes 2621440 | tf_op jit(solution)/shard_map/psum | solution.py:371
  43.1 8.7 %copy-start.12 = (f32[256,64]{1,0:T(8,128)S(1)}, f32[256,64]{1,0:T(8,128)}, u32[]{:S(2)}) copy-start(f32[256,64]{1,0:T(8,128)} %copy-done.11) | copy-start | bytes 196612
  43.1 8.7 %copy-start.14 = (f32[256,64]{1,0:T(8,128)S(1)}, f32[256,64]{1,0:T(8,128)}, u32[]{:S(2)}) copy-start(f32[256,64]{1,0:T(8,128)} %copy-done.13) | copy-start | bytes 196612
  47.1 7.7 %copy-start.24 = (f32[128]{0:T(128)S(1)}, f32[128]{0:T(128)}, u32[]{:S(2)}) copy-start(f32[128]{0:T(128)} %param.53) | copy-start | bytes 1540
  47.1 8.1 %copy-start.25 = (f32[128]{0:T(128)S(1)}, f32[128]{0:T(128)}, u32[]{:S(2)}) copy-start(f32[128]{0:T(128)} %param.42) | copy-start | bytes 1540
  51.1 3.7 %copy-start.5 = (f32[256,4,128]{2,1,0:T(4,128)S(1)}, f32[256,4,128]{2,1,0:T(4,128)}, u32[]{:S(2)}) copy-start(f32[256,4,128]{2,1,0:T(4,128)} %reshape.540) | copy-start | bytes 1572868
  51.1 4.1 %copy-start.6 = (f32[256,4,128]{2,1,0:T(4,128)S(1)}, f32[256,4,128]{2,1,0:T(4,128)}, u32[]{:S(2)}) copy-start(f32[256,4,128]{2,1,0:T(4,128)} %reshape.535) | copy-start | bytes 1572868
  187.1 110.8 %all-reduce.8.cloned.1.call-start = ((), (), s32[]{:S(2)}) async-start(), calls=%async_computation.3 | async-start | bytes 2621440 | tf_op jit(solution)/shard_map/psum | solution.py:374
  245.4 7.0 %copy-start.35 = (f32[2560]{0:T(1024)S(1)}, f32[2560]{0:T(1024)}, u32[]{:S(2)}) copy-start(f32[2560]{0:T(1024)} %param.45) | copy-start | bytes 30724
  252.5 47.8 %copy-start.36 = (f32[2560]{0:T(1024)S(1)}, f32[2560]{0:T(1024)}, u32[]{:S(2)}) copy-start(f32[2560]{0:T(1024)} %param.56) | copy-start | bytes 30724
  300.4 10.0 %copy-start.30 = (s32[256]{0:T(256)S(1)}, s32[256]{0:T(256)}, u32[]{:S(2)}) copy-start(s32[256]{0:T(256)} %param.33) | copy-start | bytes 3076
  300.4 17.4 %copy-start.21 = (s32[256]{0:T(256)S(1)}, s32[256]{0:T(256)}, u32[]{:S(2)}) copy-start(s32[256]{0:T(256)} %get-tuple-element.23) | copy-start | bytes 3076
  300.4 18.0 %copy-start.22 = (s32[256]{0:T(256)S(1)}, s32[256]{0:T(256)}, u32[]{:S(2)}) copy-start(s32[256]{0:T(256)} %get-tuple-element.22) | copy-start | bytes 3076
  318.5 3.6 %collective-permute-start = (f32[4]{0:T(128)S(1)}, f32[4]{0:T(128)S(1)}, u32[]{:S(2)}, u32[]{:S(2)}) collective-permute-start(f32[4]{0:T(128)S(1)} %select_reduce_fusion.1), channel_id=1, source_target_pairs={{0,4},{4,0},{8,12},{12,8},{16,20},{20,16},{24,28},{28,24},{32,36},... | collective-permute-start | bytes 56 | tf_op jit(solution)/shard_map/ppermute | solution.py:402
  322.2 5.1 %collective-permute-start.1 = (f32[4]{0:T(128)S(1)}, f32[4]{0:T(128)S(1)}, u32[]{:S(2)}, u32[]{:S(2)}) collective-permute-start(f32[4]{0:T(128)S(1)} %add.293), channel_id=1, source_target_pairs={{0,8},{4,12},{8,0},{12,4},{16,24},{20,28},{24,16},{28,20},{32,40},... | collective-permute-start | bytes 56 | tf_op jit(solution)/shard_map/ppermute | solution.py:402
  327.2 3.6 %collective-permute-start.2 = (f32[4]{0:T(128)S(1)}, f32[4]{0:T(128)S(1)}, u32[]{:S(2)}, u32[]{:S(2)}) collective-permute-start(f32[4]{0:T(128)S(1)} %add.294), channel_id=1, source_target_pairs={{0,16},{4,20},{8,24},{12,28},{16,0},{20,4},{24,8},{28,12},{32,48},... | collective-permute-start | bytes 56 | tf_op jit(solution)/shard_map/ppermute | solution.py:402
  330.8 5.1 %collective-permute-start.3 = (f32[4]{0:T(128)S(1)}, f32[4]{0:T(128)S(1)}, u32[]{:S(2)}, u32[]{:S(2)}) collective-permute-start(f32[4]{0:T(128)S(1)} %add.295), channel_id=1, source_target_pairs={{0,32},{4,36},{8,40},{12,44},{16,48},{20,52},{24,56},{28,60},{32,0... | collective-permute-start | bytes 56 | tf_op jit(solution)/shard_map/ppermute | solution.py:402
  335.9 5.1 %collective-permute-start.4 = (f32[4]{0:T(128)S(1)}, f32[4]{0:T(128)S(1)}, u32[]{:S(2)}, u32[]{:S(2)}) collective-permute-start(f32[4]{0:T(128)S(1)} %add.296), channel_id=1, source_target_pairs={{0,64},{4,68},{8,72},{12,76},{16,80},{20,84},{24,88},{28,92},{32,9... | collective-permute-start | bytes 56 | tf_op jit(solution)/shard_map/ppermute | solution.py:402
  (14 other events, 23.6 us)
Sparse Core Ops, SparseCore 0:
  31.5 89.9 all-gather.2
  124.5 81.4 all-gather.4
  208.6 41.3 all-reduce.5
  252.3 45.5 all-reduce.7

commit v5 on v4

--- a/solution.py
+++ b/solution.py
@@ -215,6 +215,20 @@
         out_shape=jax.ShapeDtypeStruct((q_rows, HD), jnp.bfloat16),
         compiler_params=pltpu.CompilerParams(dimension_semantics=("arbitrary", "arbitrary")),
     )(flags, queries, stacked, key_code, query_low, query_high)
+
+
+def doubling_gather(block, axis_name):
+    count = lax.axis_size(axis_name)
+    gathered = block
+    stride = 1
+    while stride < count:
+        received = lax.ppermute(gathered, axis_name, [(i, i ^ stride) for i in range(count)])
+        upper = (lax.axis_index(axis_name) // stride) % 2 == 1
+        gathered = jnp.concatenate(
+            [jnp.where(upper, received, gathered), jnp.where(upper, gathered, received)], axis=0
+        )
+        stride *= 2
+    return gathered
 
 
 def tile_flags(key_code, query_low, query_high):
@@ -361,7 +375,7 @@
     )
     reference_part = attend_model(
         reference_query,
-        lax.all_gather(reference_stack, "seq", axis=0, tiled=True),
+        doubling_gather(reference_stack, "seq"),
         flags,
         key_code,
         query_low,

time: 350 us -> 380 us (1.086)
  waiting for transfers between devices: 127 us -> 143 us
  starting transfers between devices: 13.1 us -> 25.7 us
  other arithmetic: 51.1 us -> 61.5 us
  local copies, waits for them, and re-layouts: 28.9 us -> 22.6 us
    ppermute x0 -> x5, waiting for transfers between devices: none -> 91.1 us  [doubling_gather(): lax.ppermute(gathered, axis_name, [(i, i ^ stride) for i in range(count)])]
    all_gather x1, waiting for transfers between devices: 56.4 us -> 0.01 us  [local(): lax.all_gather(jnp.concatenate([policy_stack, carrier], axis=0), 'seq', a...]
    ppermute x0 -> x5, starting transfers between devices: none -> 12.8 us  [doubling_gather(): lax.ppermute(gathered, axis_name, [(i, i ^ stride) for i in range(count)])]
    all_gather x1 -> x0, waiting for transfers between devices: 12.5 us -> none  [local(): lax.all_gather(reference_stack, 'seq', axis=0, tiled=True)]
    select_n x0 -> x5, other arithmetic: none -> 11 us  [doubling_gather(): jnp.where(upper, received, gathered)]
    concatenate x0 -> x5, other arithmetic: none -> 10.6 us  [doubling_gather(): jnp.concatenate([jnp.where(upper, received, gathered), jnp.where(upper, g...]
    psum x1, waiting for transfers between devices: 4.53 us -> 0.01 us  [local(): policy_summed = lax.psum(policy_part.astype(jnp.bfloat16), 'vocab')]
  transfers between devices with their start and end apart: 9 -> 13, of which waited for: 9 -> 11; matrix products, arithmetic and copies ran while one was open for 22% -> 17% of each run, Pallas kernels for 21% -> 9%
where the time goes in v5:
time: 380 us; the launch traced here: 379 us
  waiting for transfers between devices  143 us (38%)
  Pallas kernels  72.6 us (19%)
  other arithmetic  61.5 us (16%)
  matrix products  27.4 us (7%)
  starting transfers between devices  25.7 us (7%)
  local copies, waits for them, and re-layouts  22.6 us (6%)
  between operations  14.5 us (4%)
  blocking collectives  11.5 us (3%)
    ppermute x5, waiting for transfers between devices, doubling_gather(): lax.ppermute(gathered, axis_name, [(i, i ^ stride) for i in range(count)])  91.1 us
    pallas_call x2, Pallas kernels, flash_attend(): pl.pallas_call(flash_kernel, grid_spec=grid_spec, out_shape=jax.ShapeDtyp...  72.6 us
    psum x1, waiting for transfers between devices, local(): lax.psum(reference_part.astype(jnp.bfloat16), 'vocab').astype(jnp.float32)  41.7 us
    ppermute x5, starting transfers between devices, doubling_gather(): lax.ppermute(gathered, axis_name, [(i, i ^ stride) for i in range(count)])  12.8 us
    ppermute x5, starting transfers between devices, local(): lax.ppermute(rollout_mean, 'seq', [(i, i ^ stride) for i in range(seq_cou...  12.5 us
    select_n x5, other arithmetic, doubling_gather(): jnp.where(upper, received, gathered)  11 us
    concatenate x5, other arithmetic, doubling_gather(): jnp.concatenate([jnp.where(upper, received, gathered), jnp.where(upper, g...  10.6 us
    ppermute x5, waiting for transfers between devices, local(): lax.ppermute(rollout_mean, 'seq', [(i, i ^ stride) for i in range(seq_cou...  9.89 us
  transfers between devices with their start and end apart: 13, of which 11 were waited for; matrix products, arithmetic and copies ran while one was open for 17% of the time, Pallas kernels for 9%

profile of v5, /device:TPU:0, one launch (start us, length us, event | category | flops | bytes accessed | tf_op | source)
XLA Modules:
  0.0 378.7 jit_solution(10604775964799953644)
XLA Ops:
  16.1 2.8 convolution_convert_fusion.2
  19.0 2.6 multiply_reduce_fusion.5
  32.0 2.1 convolution_convert_fusion.1
  36.6 4.0 %collective-permute-done = bf16[288,256]{1,0:T(8,128)(2,1)} collective-permute-done((bf16[288,256]{1,0:T(8,128)(2,1)S(1)}, bf16[288,256]{1,0:T(8,128)(2,1)}, u32[]{:S(2)}, u32[]{:S(2)}) %collective-permute-start) | collective-permute-done | bytes 147488 | tf_op jit(solution)/shard_map/ppermute | solution.py:225
  43.0 3.3 collective-permute-start.1
  46.3 7.1 %collective-permute-done.1 = bf16[576,256]{1,0:T(8,128)(2,1)} collective-permute-done((bf16[576,256]{1,0:T(8,128)(2,1)}, bf16[576,256]{1,0:T(8,128)(2,1)}, u32[]{:S(2)}, u32[]{:S(2)}) %collective-permute-start.1) | collective-permute-done | bytes 294944 | tf_op jit(solution)/shard_map/ppermute | solution.py:225
  57.8 13.4 %collective-permute-done.2 = bf16[1152,256]{1,0:T(8,128)(2,1)} collective-permute-done((bf16[1152,256]{1,0:T(8,128)(2,1)}, bf16[1152,256]{1,0:T(8,128)(2,1)}, u32[]{:S(2)}, u32[]{:S(2)}) %collective-permute-start.2) | collective-permute-done | bytes 589856 | tf_op jit(solution)/shard_map/ppermute | solution.py:225
  74.6 3.1 collective-permute-start.3
  83.5 3.9 %fusion.50 = f32[256,512]{1,0:T(8,128)} fusion(bf16[2560,512]{1,0:T(8,128)(2,1)} %param.39, bf16[256,2560]{1,0:T(8,128)(2,1)} %param.31, f32[2560]{0:T(1024)S(1)} %copy-done.55, f32[256]{0:T(256)S(1)} %copy-done.45), kind=kOutput, calls=%fused_computation.157 | convolution fusion | flops 673710080 | bytes 4467712 | tf_op jit(solution)/shard_map/dot_general | solution.py:56
  93.5 9.5 %collective-permute-done.3 = bf16[2304,256]{1,0:T(8,128)(2,1)} collective-permute-done((bf16[2304,256]{1,0:T(8,128)(2,1)}, bf16[2304,256]{1,0:T(8,128)(2,1)}, u32[]{:S(2)}, u32[]{:S(2)}) %collective-permute-start.3) | collective-permute-done | bytes 1179680 | tf_op jit(solution)/shard_map/ppermute | solution.py:225
  103.0 2.0 broadcast_select_fusion.3
  106.7 3.0 collective-permute-start.4
  117.5 2.6 fusion.43
  120.2 57.1 %collective-permute-done.4 = bf16[4608,256]{1,0:T(8,128)(2,1)} collective-permute-done((bf16[4608,256]{1,0:T(8,128)(2,1)}, bf16[4608,256]{1,0:T(8,128)(2,1)}, u32[]{:S(2)}, u32[]{:S(2)}) %collective-permute-start.4) | collective-permute-done | bytes 2359328 | tf_op jit(solution)/shard_map/ppermute | solution.py:225
  177.3 5.4 %broadcast_select_fusion.1 = (bf16[4608,256]{1,0:T(8,128)(2,1)}, bf16[4608,256]{1,0:T(8,128)(2,1)}) fusion(bf16[4608,256]{1,0:T(8,128)(2,1)} %collective-permute-done.4, pred[]{:T(512)S(6)} %eq.109, bf16[2304,256]{1,0:T(8,128)(2,1)} %copy-done.2, bf16[2304,256]{1,0:T(8,128)(2,1)} %copy-done.1), kind=kLoop, calls=%fused_computation.22 | loop fusion | flops 7077888 | bytes 9437185 | tf_op jit(solution)/shard_map/jit(_where)/select_n | solution.py:228
  185.9 2.9 and_reduce_fusion
  189.4 38.1 %shard_map.284 = bf16[1024,128]{1,0:T(8,128)(2,1)} custom-call(s32[10]{0:T(128)} %convert_element_type.110.flags_ref, bf16[1024,128]{1,0:T(8,128)(2,1)} %bitcast.91, bf16[10240,256]{1,0:T(8,128)(2,1)} %all-gather.2.cloned.1.call-done.kv_ref, s32[1,10240]{1,0:T(1,128)} %broadcast_in_dim_reshape.4.kcode_ref, s32[1024,1]{1,0:T(8,128)} %bitcast.86, ...), custom_call_target="tpu_custom_call" | custom-call | tf_op jit(solution)/shard_map/pallas_call | solution.py:212
  228.6 3.7 convolution_convert_fusion
  232.6 6.3 %pad_maximum_fusion.kv_ref = bf16[9216,256]{1,0:T(8,128)(2,1)} fusion(bf16[4608,256]{1,0:T(8,128)(2,1)} %get-tuple-element.34, bf16[4608,256]{1,0:T(8,128)(2,1)} %get-tuple-element.33), kind=kLoop, calls=%fused_computation.2 | loop fusion | flops 9437184 | bytes 9437184 | tf_op jit(solution)/shard_map/concatenate | solution.py:227
  239.7 2.7 and_reduce_fusion.1
  242.9 34.5 %shard_map.285 = bf16[1024,128]{1,0:T(8,128)(2,1)} custom-call(s32[9]{0:T(128)} %convert_element_type.113.flags_ref, bf16[1024,128]{1,0:T(8,128)(2,1)} %bitcast.90, bf16[9216,256]{1,0:T(8,128)(2,1)} %pad_maximum_fusion.kv_ref, s32[1,9216]{1,0:T(1,128)} %broadcast_in_dim_reshape.5.kcode_ref, s32[1024,1]{1,0:T(8,128)} %bitcast.87, s32[1024,1]{1,0:T(8,128)} %bitcast.89), custom_call_target="tpu_custom_call" | custom-call | tf_op jit(solution)/shard_map/pallas_call | solution.py:212
  278.6 3.7 fusion.58
  282.3 2.4 multiply_reduce_fusion.1
  284.8 2.1 fusion.57
  286.9 41.7 %all-reduce.8.cloned.1.call-done = bf16[256,2560]{1,0:T(8,128)(2,1)} async-done(((bf16[256,2560]{1,0:T(8,128)(2,1)}), bf16[256,2560]{1,0:T(8,128)(2,1)}) %all-reduce.8.cloned.1.call-update) | async-done | bytes 1310736 | tf_op jit(solution)/shard_map/psum | solution.py:388
  328.6 2.4 multiply_reduce_fusion
  331.1 4.1 %fusion.56 = (f32[256]{0:T(256)S(1)}, f32[256,640]{1,0:T(8,128)}) fusion(bf16[2560,640]{1,0:T(8,128)(2,1)} %param.57, bf16[256,2560]{1,0:T(8,128)(2,1)S(1)} %copy-done.18, bf16[256,2560]{1,0:T(8,128)(2,1)S(1)} %copy-done.9, f32[2560]{0:T(1024)S(1)} %copy-done.57, f32[256]{0:T(256)S(1)} %add_rsqrt_fusion.2), kind=kOutput, calls=%fused_computation.160 | convolution fusion | flops 842956544 | bytes 6565888 | tf_op jit(solution)/shard_map/dot_general | solution.py:258
  335.2 5.9 %all-reduce.2 = (f32[256]{0:T(256)S(1)}, f32[256]{0:T(256)S(1)}) all-reduce(f32[256]{0:T(256)S(1)} %get-tuple-element.74, f32[256]{0:T(256)S(1)} %get-tuple-element.76), channel_id=1, replica_groups=mesh['seq'=32,'vocab'=4] {'vocab'}, use_global_device_ids=true, to_apply=%region_27.28 | all-reduce | flops 512 | bytes 4096 | tf_op jit(solution)/shard_map/pmax | solution.py:402
  342.9 5.7 %all-reduce.1 = (f32[256]{0:T(256)S(1)}, f32[256]{0:T(256)S(1)}, f32[256]{0:T(256)S(1)}, f32[256]{0:T(256)S(1)}) all-reduce(f32[256]{0:T(256)S(1)} %get-tuple-element.55, f32[256]{0:T(256)S(1)} %get-tuple-element.56, f32[256]{0:T(256)S(1)} %get-tuple-element.19, ...), channel_id=1, replica_groups=mesh['seq'=32,'vocab'=4] {'vocab'}, use_global_device_ids=true, to_apply=%region_25.26 | all-reduce | flops 1024 | bytes 8192 | tf_op jit(solution)/shard_map/psum | solution.py:405
  352.9 3.1 collective-permute-start.6
  361.5 3.1 collective-permute-start.8
  366.6 3.2 collective-permute-start.9
  (227 shorter events, 76.7 us)
Async XLA Ops:
  7.2 277.5 %copy-start = (bf16[2560,640]{1,0:T(8,128)(2,1)S(1)}, bf16[2560,640]{1,0:T(8,128)(2,1)}, u32[]{:S(2)}) copy-start(bf16[2560,640]{1,0:T(8,128)(2,1)} %param.46) | copy-start | bytes 9830404
  7.2 8.0 %copy-start.53 = (f32[2560]{0:T(1024)S(1)}, f32[2560]{0:T(1024)}, u32[]{:S(2)}) copy-start(f32[2560]{0:T(1024)} %param.49) | copy-start | bytes 30724
  7.2 175.5 %all-gather.2.cloned.1.call-start = ((), (), s32[]{:S(2)}) async-start(), calls=%async_computation | async-start | bytes 5406720 | tf_op jit(solution)/shard_map/all_gather | solution.py:343
  16.1 10.6 %copy-start.38 = (f32[128]{0:T(128)S(1)}, f32[128]{0:T(128)}, u32[]{:S(2)}) copy-start(f32[128]{0:T(128)} %param.54) | copy-start | bytes 1540
  19.0 11.6 %copy-start.33 = (bf16[4,8,128]{2,1,0:T(8,128)(2,1)S(1)}, bf16[4,8,128]{2,1,0:T(8,128)(2,1)}, u32[]{:S(2)}) copy-start(bf16[4,8,128]{2,1,0:T(8,128)(2,1)} %param.48) | copy-start | bytes 24580
  32.0 250.3 %all-reduce.6.cloned.1.call-start = ((), (), s32[]{:S(2)}) async-start(), calls=%async_computation.1 | async-start | bytes 2621440 | tf_op jit(solution)/shard_map/psum | solution.py:385
  34.9 5.7 %collective-permute-start = (bf16[288,256]{1,0:T(8,128)(2,1)S(1)}, bf16[288,256]{1,0:T(8,128)(2,1)}, u32[]{:S(2)}, u32[]{:S(2)}) collective-permute-start(bf16[288,256]{1,0:T(8,128)(2,1)S(1)} %maximum_maximum_fusion), channel_id=1, source_target_pairs={{0,4},{4,0},{8,12},{12,8},{16,20},{20,16},{24,28},{28,24},{32,36},... | collective-permute-start | bytes 442376 | tf_op jit(solution)/shard_map/ppermute | solution.py:225
  43.0 10.5 %collective-permute-start.1 = (bf16[576,256]{1,0:T(8,128)(2,1)}, bf16[576,256]{1,0:T(8,128)(2,1)}, u32[]{:S(2)}, u32[]{:S(2)}) collective-permute-start(bf16[576,256]{1,0:T(8,128)(2,1)} %pad_maximum_fusion.4), channel_id=1, source_target_pairs={{0,8},{4,12},{8,0},{12,4},{16,24},{20,28},{24,16},{28,20},{32,40},... | collective-permute-start | bytes 884744 | tf_op jit(solution)/shard_map/ppermute | solution.py:225
  56.1 21.6 %copy-start.47 = (f32[256]{0:T(256)S(1)}, f32[256]{0:T(256)}, u32[]{:S(2)}) copy-start(f32[256]{0:T(256)} %copy-done.46) | copy-start | bytes 3076
  56.1 21.6 %copy-start.54 = (f32[2560]{0:T(1024)S(1)}, f32[2560]{0:T(1024)}, u32[]{:S(2)}) copy-start(f32[2560]{0:T(1024)} %param.49) | copy-start | bytes 30724
  56.1 15.0 %collective-permute-start.2 = (bf16[1152,256]{1,0:T(8,128)(2,1)}, bf16[1152,256]{1,0:T(8,128)(2,1)}, u32[]{:S(2)}, u32[]{:S(2)}) collective-permute-start(bf16[1152,256]{1,0:T(8,128)(2,1)} %pad_maximum_fusion.3), channel_id=1, source_target_pairs={{0,16},{4,20},{8,24},{12,28},{16,0},{20,4},{24,8},{28,12},{32,48},... | collective-permute-start | bytes 1769480 | tf_op jit(solution)/shard_map/ppermute | solution.py:225
  57.8 19.9 %copy-start.8 = (bf16[256,2560]{1,0:T(8,128)(2,1)S(1)}, bf16[256,2560]{1,0:T(8,128)(2,1)}, u32[]{:S(2)}) copy-start(bf16[256,2560]{1,0:T(8,128)(2,1)} %param.32) | copy-start | bytes 3932164
  57.8 19.9 %copy-start.50 = (bf16[2560,512]{1,0:T(8,128)(2,1)S(1)}, bf16[2560,512]{1,0:T(8,128)(2,1)}, u32[]{:S(2)}) copy-start(bf16[2560,512]{1,0:T(8,128)(2,1)} %param.50) | copy-start | bytes 7864324
  74.6 8.9 %copy-start.45 = (f32[256]{0:T(256)S(1)}, f32[256]{0:T(256)}, u32[]{:S(2)}) copy-start(f32[256]{0:T(256)} %copy-done.44) | copy-start | bytes 3076
  74.6 8.9 %copy-start.55 = (f32[2560]{0:T(1024)S(1)}, f32[2560]{0:T(1024)}, u32[]{:S(2)}) copy-start(f32[2560]{0:T(1024)} %param.38) | copy-start | bytes 30724
  74.6 28.4 %collective-permute-start.3 = (bf16[2304,256]{1,0:T(8,128)(2,1)}, bf16[2304,256]{1,0:T(8,128)(2,1)}, u32[]{:S(2)}, u32[]{:S(2)}) collective-permute-start(bf16[2304,256]{1,0:T(8,128)(2,1)} %pad_maximum_fusion.2), channel_id=1, source_target_pairs={{0,32},{4,36},{8,40},{12,44},{16,48},{20,52},{24,56},{28,60},{32,0... | collective-permute-start | bytes 3538952 | tf_op jit(solution)/shard_map/ppermute | solution.py:225
  106.7 70.6 %collective-permute-start.4 = (bf16[4608,256]{1,0:T(8,128)(2,1)}, bf16[4608,256]{1,0:T(8,128)(2,1)}, u32[]{:S(2)}, u32[]{:S(2)}) collective-permute-start(bf16[4608,256]{1,0:T(8,128)(2,1)} %pad_maximum_fusion.1), channel_id=1, source_target_pairs={{0,64},{4,68},{8,72},{12,76},{16,80},{20,84},{24,88},{28,92},{32,9... | collective-permute-start | bytes 7077896 | tf_op jit(solution)/shard_map/ppermute | solution.py:225
  120.1 63.8 %copy-start.42 = (s32[4,1]{0,1:T(1,128)S(1)}, s32[4,1]{0,1:T(1,128)}, u32[]{:S(2)}) copy-start(s32[4,1]{0,1:T(1,128)} %copy-done.41) | copy-start | bytes 52
  120.1 64.0 %copy-start.43 = (s32[4]{0:T(128)S(1)}, s32[4]{0:T(128)}, u32[]{:S(2)}) copy-start(s32[4]{0:T(128)} %bitcast_subtract_fusion) | copy-start | bytes 52
  120.1 65.0 %copy-start.35 = (s32[320]{0:T(512)S(1)}, s32[320]{0:T(512)}, u32[]{:S(2)}) copy-start(s32[320]{0:T(512)} %pad.29.clone) | copy-start | bytes 3844
  120.2 65.8 %copy-start.28 = (s32[256]{0:T(256)S(1)}, s32[256]{0:T(256)}, u32[]{:S(2)}) copy-start(s32[256]{0:T(256)} %get-tuple-element.57) | copy-start | bytes 3076
  120.2 65.8 %copy-start.31 = (s32[256]{0:T(256)S(1)}, s32[256]{0:T(256)}, u32[]{:S(2)}) copy-start(s32[256]{0:T(256)} %get-tuple-element.61) | copy-start | bytes 3076
  232.3 96.3 %all-reduce.8.cloned.1.call-start = ((), (), s32[]{:S(2)}) async-start(), calls=%async_computation.2 | async-start | bytes 2621440 | tf_op jit(solution)/shard_map/psum | solution.py:388
  284.8 46.2 %copy-start.57 = (f32[2560]{0:T(1024)S(1)}, f32[2560]{0:T(1024)}, u32[]{:S(2)}) copy-start(f32[2560]{0:T(1024)} %param.56) | copy-start | bytes 30724
  331.1 10.0 %copy-start.48 = (s32[256]{0:T(256)S(1)}, s32[256]{0:T(256)}, u32[]{:S(2)}) copy-start(s32[256]{0:T(256)} %param.33) | copy-start | bytes 3076
  331.1 17.4 %copy-start.36 = (s32[256]{0:T(256)S(1)}, s32[256]{0:T(256)}, u32[]{:S(2)}) copy-start(s32[256]{0:T(256)} %get-tuple-element.23) | copy-start | bytes 3076
  331.1 18.0 %copy-start.37 = (s32[256]{0:T(256)S(1)}, s32[256]{0:T(256)}, u32[]{:S(2)}) copy-start(s32[256]{0:T(256)} %get-tuple-element.22) | copy-start | bytes 3076
  349.2 3.6 collective-permute-start.5
  352.9 5.1 %collective-permute-start.6 = (f32[4]{0:T(128)S(1)}, f32[4]{0:T(128)S(1)}, u32[]{:S(2)}, u32[]{:S(2)}) collective-permute-start(f32[4]{0:T(128)S(1)} %add.319), channel_id=1, source_target_pairs={{0,8},{4,12},{8,0},{12,4},{16,24},{20,28},{24,16},{28,20},{32,40},... | collective-permute-start | bytes 56 | tf_op jit(solution)/shard_map/ppermute | solution.py:416
  358.0 3.6 collective-permute-start.7
  361.5 5.1 %collective-permute-start.8 = (f32[4]{0:T(128)S(1)}, f32[4]{0:T(128)S(1)}, u32[]{:S(2)}, u32[]{:S(2)}) collective-permute-start(f32[4]{0:T(128)S(1)} %add.321), channel_id=1, source_target_pairs={{0,32},{4,36},{8,40},{12,44},{16,48},{20,52},{24,56},{28,60},{32,0... | collective-permute-start | bytes 56 | tf_op jit(solution)/shard_map/ppermute | solution.py:416
  366.6 5.1 %collective-permute-start.9 = (f32[4]{0:T(128)S(1)}, f32[4]{0:T(128)S(1)}, u32[]{:S(2)}, u32[]{:S(2)}) collective-permute-start(f32[4]{0:T(128)S(1)} %add.322), channel_id=1, source_target_pairs={{0,64},{4,68},{8,72},{12,76},{16,80},{20,84},{24,88},{28,92},{32,9... | collective-permute-start | bytes 56 | tf_op jit(solution)/shard_map/ppermute | solution.py:416
  (40 other events, 136.1 us)
Sparse Core Ops, SparseCore 0:
  32.1 134.0 all-gather.1
  232.4 46.2 all-reduce.5
  282.4 46.1 all-reduce.7

commit v6 on v4

--- a/solution.py
+++ b/solution.py
@@ -215,6 +215,16 @@
         out_shape=jax.ShapeDtypeStruct((q_rows, HD), jnp.bfloat16),
         compiler_params=pltpu.CompilerParams(dimension_semantics=("arbitrary", "arbitrary")),
     )(flags, queries, stacked, key_code, query_low, query_high)
+
+
+def exchange_sum(values, axis_name):
+    count = lax.axis_size(axis_name)
+    stride = 1
+    while stride < count:
+        received = lax.ppermute(values, axis_name, [(i, i ^ stride) for i in range(count)])
+        values = (values.astype(jnp.float32) + received.astype(jnp.float32)).astype(values.dtype)
+        stride *= 2
+    return values
 
 
 def tile_flags(key_code, query_low, query_high):
@@ -371,7 +381,7 @@
     policy_summed = lax.psum(policy_part.astype(jnp.bfloat16), "vocab")
     policy_summed, reference_part = lax.optimization_barrier((policy_summed, reference_part))
     policy_mixed = policy_summed.astype(jnp.float32)
-    reference_mixed = lax.psum(reference_part.astype(jnp.bfloat16), "vocab").astype(jnp.float32)
+    reference_mixed = exchange_sum(reference_part.astype(jnp.bfloat16), "vocab").astype(jnp.float32)
     policy_final = rms_scale(
         policy_hidden.astype(jnp.float32) + policy_mixed, policy_final_gain
     ).astype(jnp.bfloat16)

time: 350 us -> 339 us (0.969)
  waiting for transfers between devices: 127 us -> 113 us
    psum x1 -> x0, waiting for transfers between devices: 43.3 us -> none  [local(): lax.psum(reference_part.astype(jnp.bfloat16), 'vocab').astype(jnp.float32)]
    ppermute x0 -> x2, waiting for transfers between devices: none -> 29.4 us  [exchange_sum(): lax.ppermute(values, axis_name, [(i, i ^ stride) for i in range(count)])]
  transfers between devices with their start and end apart: 9 -> 10, of which waited for: 9 -> 10; matrix products, arithmetic and copies ran while one was open for 22% -> 22% of each run, Pallas kernels for 21% -> 22%
where the time goes in v6:
time: 339 us; the launch traced here: 337 us
  waiting for transfers between devices  113 us (33%)
  Pallas kernels  72.6 us (21%)
  other arithmetic  53.9 us (16%)
  matrix products  29.6 us (9%)
  local copies, waits for them, and re-layouts  28.9 us (9%)
  between operations  14.2 us (4%)
  starting transfers between devices  13 us (4%)
  blocking collectives  11.4 us (3%)
    pallas_call x2, Pallas kernels, flash_attend(): pl.pallas_call(flash_kernel, grid_spec=grid_spec, out_shape=jax.ShapeDtyp...  72.6 us
    all_gather x1, waiting for transfers between devices, local(): lax.all_gather(jnp.concatenate([policy_stack, carrier], axis=0), 'seq', a...  56.6 us
    ppermute x2, waiting for transfers between devices, exchange_sum(): lax.ppermute(values, axis_name, [(i, i ^ stride) for i in range(count)])  29.4 us
    all_gather x1, waiting for transfers between devices, local(): lax.all_gather(reference_stack, 'seq', axis=0, tiled=True)  12.7 us
    ppermute x5, starting transfers between devices, local(): lax.ppermute(rollout_mean, 'seq', [(i, i ^ stride) for i in range(seq_cou...  12.3 us
    reduce_sum x6, other arithmetic, rms_scale(): jnp.mean(values * values, axis=-1, keepdims=True) + EPSILON  10.8 us
    ppermute x5, waiting for transfers between devices, local(): lax.ppermute(rollout_mean, 'seq', [(i, i ^ stride) for i in range(seq_cou...  10.1 us
    reshape x4, local copies, waits for them, and re-layouts, project(): jnp.dot(normed, query_weight, preferred_element_type=jnp.float32)  8.09 us
  transfers between devices with their start and end apart: 10, of which 10 were waited for; matrix products, arithmetic and copies ran while one was open for 22% of the time, Pallas kernels for 22%

profile of v6, /device:TPU:0, one launch (start us, length us, event | category | flops | bytes accessed | tf_op | source)
XLA Modules:
  0.0 336.9 jit_solution(14150327335560582473)
XLA Ops:
  16.1 2.8 convolution_convert_fusion.2
  18.9 2.6 multiply_reduce_fusion.5
  31.4 2.1 convolution_convert_fusion.1
  35.0 3.9 %fusion.48 = f32[256,512]{1,0:T(8,128)} fusion(bf16[2560,512]{1,0:T(8,128)(2,1)} %param.50, bf16[256,2560]{1,0:T(8,128)(2,1)} %param.32, f32[2560]{0:T(1024)} %param.49, f32[256]{0:T(256)} %copy-done.28), kind=kOutput, calls=%fused_computation.143 | convolution fusion | flops 673710080 | bytes 4467712 | tf_op jit(solution)/shard_map/dot_general | solution.py:56
  38.9 2.0 reshape.540
  42.9 4.0 %fusion.50 = f32[256,512]{1,0:T(8,128)} fusion(bf16[2560,512]{1,0:T(8,128)(2,1)} %param.39, bf16[256,2560]{1,0:T(8,128)(2,1)} %param.31, f32[2560]{0:T(1024)} %param.38, f32[256]{0:T(256)S(1)} %copy-done.27), kind=kOutput, calls=%fused_computation.144 | convolution fusion | flops 673710080 | bytes 4467712 | tf_op jit(solution)/shard_map/dot_general | solution.py:56
  46.9 2.0 reshape.535
  48.9 2.0 reshape.534
  61.8 3.1 fusion.43
  64.9 56.6 %all-gather.3.cloned.1.call-done.kv_ref = bf16[10240,256]{1,0:T(8,128)(2,1)} async-done(((bf16[320,256]{1,0:T(8,128)(2,1)}), bf16[10240,256]{1,0:T(8,128)(2,1)}) %all-gather.3.cloned.1.call-update) | async-done | bytes 5242896 | tf_op jit(solution)/shard_map/all_gather | solution.py:339
  139.2 3.7 %and_reduce_fusion = pred[10]{0:T(512)(128)(4,1)S(1)} fusion(s32[10,1024]{1,0:T(8,128)} %ge.64, s32[256]{0:T(256)} %copy-done.18, s32[256]{0:T(256)} %copy-done.19), kind=kLoop, calls=%fused_computation | loop fusion | flops 10485750 | bytes 43018 | tf_op jit(solution)/shard_map/reduce_or | solution.py:232
  143.4 38.1 %shard_map.284 = bf16[1024,128]{1,0:T(8,128)(2,1)} custom-call(s32[10]{0:T(128)} %convert_element_type.128.flags_ref, bf16[1024,128]{1,0:T(8,128)(2,1)} %bitcast.90, bf16[10240,256]{1,0:T(8,128)(2,1)} %all-gather.3.cloned.1.call-done.kv_ref, s32[1,10240]{1,0:T(1,128)} %broadcast_in_dim_reshape.4.kcode_ref, s32[1024,1]{1,0:T(8,128)} %bitcast.86, ...), custom_call_target="tpu_custom_call" | custom-call | tf_op jit(solution)/shard_map/pallas_call | solution.py:212
  183.3 3.8 %convolution_convert_fusion = bf16[256,2560]{1,0:T(8,128)(2,1)} fusion(bf16[256,512]{0,1:T(8,128)(2,1)} %bitcast.94, bf16[512,2560]{1,0:T(8,128)(2,1)} %param.44), kind=kOutput, calls=%fused_computation.8 | convolution fusion | flops 671744000 | bytes 4194304 | tf_op jit(solution)/shard_map/dot_general | solution.py:243
  189.5 3.3 and_reduce_fusion.1
  193.3 12.7 %all-gather.5.cloned.1.call-done.kv_ref = bf16[9216,256]{1,0:T(8,128)(2,1)} async-done(((bf16[288,256]{1,0:T(8,128)(2,1)}), bf16[9216,256]{1,0:T(8,128)(2,1)}) %all-gather.5.cloned.1.call-update) | async-done | bytes 4718608 | tf_op jit(solution)/shard_map/all_gather | solution.py:374
  206.0 34.6 %shard_map.285 = bf16[1024,128]{1,0:T(8,128)(2,1)} custom-call(s32[9]{0:T(128)} %convert_element_type.131.flags_ref, bf16[1024,128]{1,0:T(8,128)(2,1)} %bitcast.91, bf16[9216,256]{1,0:T(8,128)(2,1)} %all-gather.5.cloned.1.call-done.kv_ref, s32[1,9216]{1,0:T(1,128)} %broadcast_in_dim_reshape.5.kcode_ref, s32[1024,1]{1,0:T(8,128)} %bitcast.87, s32[1024,1]{1,0:T(8,128)} %bitcast.89), custom_call_target="tpu_custom_call" | custom-call | tf_op jit(solution)/shard_map/pallas_call | solution.py:212
  241.7 3.7 %fusion.58 = bf16[256,2560]{1,0:T(8,128)(2,1)} fusion(bf16[256,512]{0,1:T(8,128)(2,1)S(1)} %bitcast.95, bf16[512,2560]{1,0:T(8,128)(2,1)} %param.55), kind=kOutput, calls=%fused_computation.149 | convolution fusion | flops 671088640 | bytes 4194304 | tf_op jit(solution)/shard_map/dot_general | solution.py:243
  245.4 4.5 %all-reduce.5.cloned.1.call-done = bf16[256,2560]{1,0:T(8,128)(2,1)} async-done(((bf16[256,2560]{1,0:T(8,128)(2,1)}), bf16[256,2560]{1,0:T(8,128)(2,1)}) %all-reduce.5.cloned.1.call-update) | async-done | bytes 1310736 | tf_op jit(solution)/shard_map/psum | solution.py:381
  250.2 3.0 collective-permute-done
  253.2 2.8 add_convert_fusion.1
  256.2 2.4 multiply_reduce_fusion.1
  258.7 2.1 fusion.57
  260.8 26.4 %collective-permute-done.1 = bf16[256,2560]{1,0:T(8,128)(2,1)} collective-permute-done((bf16[256,2560]{1,0:T(8,128)(2,1)}, bf16[256,2560]{1,0:T(8,128)(2,1)}, u32[]{:S(2)}, u32[]{:S(2)}) %collective-permute-start.1) | collective-permute-done | bytes 1310752 | tf_op jit(solution)/shard_map/ppermute | solution.py:224
  287.2 2.4 multiply_reduce_fusion
  289.6 3.9 %fusion.56 = (f32[256]{0:T(256)S(1)}, f32[256,640]{1,0:T(8,128)}) fusion(bf16[2560,640]{1,0:T(8,128)(2,1)S(1)} %copy-done.31, bf16[256,2560]{1,0:T(8,128)(2,1)S(1)} %copy-done.4, f32[2560]{0:T(1024)S(1)} %copy-done.36, f32[256]{0:T(256)S(1)} %add_rsqrt_fusion.2, bf16[256,2560]{1,0:T(8,128)(2,1)} %collective-permute-done.1, ...), kind=kOutput, calls=%fused_computation.147 | convolution fusion | flops 845577984 | bytes 7876608 | tf_op jit(solution)/shard_map/dot_general | solution.py:254
  293.6 5.7 %all-reduce.2 = (f32[256]{0:T(256)S(1)}, f32[256]{0:T(256)S(1)}) all-reduce(f32[256]{0:T(256)S(1)} %get-tuple-element.64, f32[256]{0:T(256)S(1)} %get-tuple-element.66), channel_id=1, replica_groups=mesh['seq'=32,'vocab'=4] {'vocab'}, use_global_device_ids=true, to_apply=%region_26.27 | all-reduce | flops 512 | bytes 4096 | tf_op jit(solution)/shard_map/pmax | solution.py:398
  301.1 5.7 %all-reduce.1 = (f32[256]{0:T(256)S(1)}, f32[256]{0:T(256)S(1)}, f32[256]{0:T(256)S(1)}, f32[256]{0:T(256)S(1)}) all-reduce(f32[256]{0:T(256)S(1)} %get-tuple-element.45, f32[256]{0:T(256)S(1)} %get-tuple-element.46, f32[256]{0:T(256)S(1)} %get-tuple-element.19, ...), channel_id=1, replica_groups=mesh['seq'=32,'vocab'=4] {'vocab'}, use_global_device_ids=true, to_apply=%region_24.25 | all-reduce | flops 1024 | bytes 8192 | tf_op jit(solution)/shard_map/psum | solution.py:401
  311.1 3.1 collective-permute-start.3
  317.7 2.0 collective-permute-done.4
  319.8 3.1 collective-permute-start.5
  324.8 3.0 collective-permute-start.6
  327.8 2.1 collective-permute-done.6
  (168 shorter events, 69.5 us)
Async XLA Ops:
  7.2 251.4 %copy-start = (bf16[2560,640]{1,0:T(8,128)(2,1)S(1)}, bf16[2560,640]{1,0:T(8,128)(2,1)}, u32[]{:S(2)}) copy-start(bf16[2560,640]{1,0:T(8,128)(2,1)} %param.46) | copy-start | bytes 9830404
  7.2 8.0 %copy-start.34 = (f32[2560]{0:T(1024)S(1)}, f32[2560]{0:T(1024)}, u32[]{:S(2)}) copy-start(f32[2560]{0:T(1024)} %param.49) | copy-start | bytes 30724
  7.2 114.3 %all-gather.3.cloned.1.call-start = ((), (), s32[]{:S(2)}) async-start(), calls=%async_computation | async-start | bytes 5406720 | tf_op jit(solution)/shard_map/all_gather | solution.py:339
  10.5 12.7 %copy-start.25 = (s32[4,1]{0,1:T(1,128)}, s32[4,1]{0,1:T(1,128)S(1)}, u32[]{:S(2)}) copy-start(s32[4,1]{0,1:T(1,128)S(1)} %reduce-window.8) | copy-start | bytes 52
  10.5 4.7 %copy-start.3 = (bf16[256,2560]{1,0:T(8,128)(2,1)S(1)}, bf16[256,2560]{1,0:T(8,128)(2,1)}, u32[]{:S(2)}) copy-start(bf16[256,2560]{1,0:T(8,128)(2,1)} %param.32) | copy-start | bytes 3932164
  10.5 4.7 %copy-start.32 = (bf16[2560,128]{1,0:T(8,128)(2,1)S(1)}, bf16[2560,128]{1,0:T(8,128)(2,1)}, u32[]{:S(2)}) copy-start(bf16[2560,128]{1,0:T(8,128)(2,1)} %param.51) | copy-start | bytes 1966084
  11.3 12.7 %copy-start.26 = (s32[4]{0:T(128)}, s32[4]{0:T(128)S(1)}, u32[]{:S(2)}) copy-start(s32[4]{0:T(128)S(1)} %bitcast_subtract_fusion) | copy-start | bytes 52
  16.1 10.0 %copy-start.22 = (f32[128]{0:T(128)S(1)}, f32[128]{0:T(128)}, u32[]{:S(2)}) copy-start(f32[128]{0:T(128)} %param.54) | copy-start | bytes 1540
  22.5 7.4 %copy-start.17 = (bf16[256,128]{1,0:T(8,128)(2,1)S(1)}, bf16[256,128]{1,0:T(8,128)(2,1)}, u32[]{:S(2)}) copy-start(bf16[256,128]{1,0:T(8,128)(2,1)} %convolution_convert_fusion.2) | copy-start | bytes 196612
  26.1 32.1 %copy-start.18 = (s32[256]{0:T(256)}, s32[256]{0:T(256)S(1)}, u32[]{:S(2)}) copy-start(s32[256]{0:T(256)S(1)} %get-tuple-element.47) | copy-start | bytes 3076
  26.1 32.1 %copy-start.19 = (s32[256]{0:T(256)}, s32[256]{0:T(256)S(1)}, u32[]{:S(2)}) copy-start(s32[256]{0:T(256)S(1)} %get-tuple-element.51) | copy-start | bytes 3076
  31.4 174.7 %all-gather.5.cloned.1.call-start = ((), (), s32[]{:S(2)}) async-start(), calls=%async_computation.2 | async-start | bytes 4866048 | tf_op jit(solution)/shard_map/all_gather | solution.py:374
  34.9 8.0 %copy-start.27 = (f32[256]{0:T(256)S(1)}, f32[256]{0:T(256)}, u32[]{:S(2)}) copy-start(f32[256]{0:T(256)} %add_rsqrt_fusion.7) | copy-start | bytes 3076
  34.9 215.0 %all-reduce.5.cloned.1.call-start = ((), (), s32[]{:S(2)}) async-start(), calls=%async_computation.1 | async-start | bytes 2621440 | tf_op jit(solution)/shard_map/psum | solution.py:381
  42.9 8.7 %copy-start.11 = (f32[256,64]{1,0:T(8,128)S(1)}, f32[256,64]{1,0:T(8,128)}, u32[]{:S(2)}) copy-start(f32[256,64]{1,0:T(8,128)} %copy-done.10) | copy-start | bytes 196612
  42.9 8.7 %copy-start.13 = (f32[256,64]{1,0:T(8,128)S(1)}, f32[256,64]{1,0:T(8,128)}, u32[]{:S(2)}) copy-start(f32[256,64]{1,0:T(8,128)} %copy-done.12) | copy-start | bytes 196612
  46.9 7.7 %copy-start.23 = (f32[128]{0:T(128)S(1)}, f32[128]{0:T(128)}, u32[]{:S(2)}) copy-start(f32[128]{0:T(128)} %param.53) | copy-start | bytes 1540
  46.9 8.1 %copy-start.24 = (f32[128]{0:T(128)S(1)}, f32[128]{0:T(128)}, u32[]{:S(2)}) copy-start(f32[128]{0:T(128)} %param.42) | copy-start | bytes 1540
  245.4 13.2 %copy-start.35 = (f32[2560]{0:T(1024)S(1)}, f32[2560]{0:T(1024)}, u32[]{:S(2)}) copy-start(f32[2560]{0:T(1024)} %param.45) | copy-start | bytes 30724
  249.9 3.2 collective-permute-start
  256.0 31.2 %collective-permute-start.1 = (bf16[256,2560]{1,0:T(8,128)(2,1)}, bf16[256,2560]{1,0:T(8,128)(2,1)}, u32[]{:S(2)}, u32[]{:S(2)}) collective-permute-start(bf16[256,2560]{1,0:T(8,128)(2,1)} %add_convert_fusion.1), channel_id=1, source_target_pairs={{0,2},{1,3},{2,0},{3,1},{4,6},{5,7},{6,4},{7,5},{8,10},{9,11},{10,... | collective-permute-start | bytes 3932168 | tf_op jit(solution)/shard_map/ppermute | solution.py:224
  258.7 28.5 %copy-start.4 = (bf16[256,2560]{1,0:T(8,128)(2,1)S(1)}, bf16[256,2560]{1,0:T(8,128)(2,1)}, u32[]{:S(2)}) copy-start(bf16[256,2560]{1,0:T(8,128)(2,1)} %param.32) | copy-start | bytes 3932164
  260.8 28.8 %copy-start.31 = (bf16[2560,640]{1,0:T(8,128)(2,1)S(1)}, bf16[2560,640]{1,0:T(8,128)(2,1)}, u32[]{:S(2)}) copy-start(bf16[2560,640]{1,0:T(8,128)(2,1)} %param.57) | copy-start | bytes 9830404
  260.8 28.8 %copy-start.36 = (f32[2560]{0:T(1024)S(1)}, f32[2560]{0:T(1024)}, u32[]{:S(2)}) copy-start(f32[2560]{0:T(1024)} %param.56) | copy-start | bytes 30724
  289.6 9.7 %copy-start.29 = (s32[256]{0:T(256)S(1)}, s32[256]{0:T(256)}, u32[]{:S(2)}) copy-start(s32[256]{0:T(256)} %param.33) | copy-start | bytes 3076
  289.6 17.1 %copy-start.20 = (s32[256]{0:T(256)S(1)}, s32[256]{0:T(256)}, u32[]{:S(2)}) copy-start(s32[256]{0:T(256)} %get-tuple-element.23) | copy-start | bytes 3076
  289.6 17.7 %copy-start.21 = (s32[256]{0:T(256)S(1)}, s32[256]{0:T(256)}, u32[]{:S(2)}) copy-start(s32[256]{0:T(256)} %get-tuple-element.22) | copy-start | bytes 3076
  307.5 3.6 %collective-permute-start.2 = (f32[4]{0:T(128)S(1)}, f32[4]{0:T(128)S(1)}, u32[]{:S(2)}, u32[]{:S(2)}) collective-permute-start(f32[4]{0:T(128)S(1)} %select_reduce_fusion.1), channel_id=1, source_target_pairs={{0,4},{4,0},{8,12},{12,8},{16,20},{20,16},{24,28},{28,24},{32,36},... | collective-permute-start | bytes 56 | tf_op jit(solution)/shard_map/ppermute | solution.py:412
  311.1 5.1 %collective-permute-start.3 = (f32[4]{0:T(128)S(1)}, f32[4]{0:T(128)S(1)}, u32[]{:S(2)}, u32[]{:S(2)}) collective-permute-start(f32[4]{0:T(128)S(1)} %add.299), channel_id=1, source_target_pairs={{0,8},{4,12},{8,0},{12,4},{16,24},{20,28},{24,16},{28,20},{32,40},... | collective-permute-start | bytes 56 | tf_op jit(solution)/shard_map/ppermute | solution.py:412
  316.2 3.6 %collective-permute-start.4 = (f32[4]{0:T(128)S(1)}, f32[4]{0:T(128)S(1)}, u32[]{:S(2)}, u32[]{:S(2)}) collective-permute-start(f32[4]{0:T(128)S(1)} %add.300), channel_id=1, source_target_pairs={{0,16},{4,20},{8,24},{12,28},{16,0},{20,4},{24,8},{28,12},{32,48},... | collective-permute-start | bytes 56 | tf_op jit(solution)/shard_map/ppermute | solution.py:412
  319.8 5.1 %collective-permute-start.5 = (f32[4]{0:T(128)S(1)}, f32[4]{0:T(128)S(1)}, u32[]{:S(2)}, u32[]{:S(2)}) collective-permute-start(f32[4]{0:T(128)S(1)} %add.301), channel_id=1, source_target_pairs={{0,32},{4,36},{8,40},{12,44},{16,48},{20,52},{24,56},{28,60},{32,0... | collective-permute-start | bytes 56 | tf_op jit(solution)/shard_map/ppermute | solution.py:412
  324.8 5.1 %collective-permute-start.6 = (f32[4]{0:T(128)S(1)}, f32[4]{0:T(128)S(1)}, u32[]{:S(2)}, u32[]{:S(2)}) collective-permute-start(f32[4]{0:T(128)S(1)} %add.302), channel_id=1, source_target_pairs={{0,64},{4,68},{8,72},{12,76},{16,80},{20,84},{24,88},{28,92},{32,9... | collective-permute-start | bytes 56 | tf_op jit(solution)/shard_map/ppermute | solution.py:412
  (15 other events, 30.1 us)
Sparse Core Ops, SparseCore 0:
  31.5 89.9 all-gather.2
  124.5 81.4 all-gather.4
  208.6 41.3 all-reduce.4

commit v7 on v6

--- a/solution.py
+++ b/solution.py
@@ -151,13 +151,14 @@
     return fold_pieces
 
 
-Q_TILE = 512
-K_TILE = 1024
+Q_TILE = 1024
+K_TILE = 512
 CODE_STRIDE = 65536
 
 
 def flash_kernel(flags_ref, q_ref, kv_ref, kcode_ref, qlo_ref, qhi_ref, out_ref, m_sc, l_sc, acc_sc):
     j = pl.program_id(1)
+    heads, tokens = m_sc.shape[0], m_sc.shape[1]
 
     @pl.when(j == 0)
     def _():
@@ -171,42 +172,48 @@
         scores = lax.dot_general(
             q_ref[...], kv[:, :HD], (((1,), (1,)), ((), ())), preferred_element_type=jnp.float32
         ) * HD ** (-0.5)
+        scores = scores.reshape(heads, tokens, scores.shape[1])
         key_code = kcode_ref[...]
-        visible = (key_code >= qlo_ref[...]) & (key_code <= qhi_ref[...])
+        visible = ((key_code >= qlo_ref[...]) & (key_code <= qhi_ref[...]))[None]
         masked = jnp.where(visible, scores, NEGATIVE_FILL)
         old_max = m_sc[...]
-        new_max = jnp.maximum(old_max, jnp.max(masked, axis=1, keepdims=True))
+        new_max = jnp.maximum(old_max, jnp.max(masked, axis=2, keepdims=True))
         weights = jnp.where(visible, jnp.exp(scores - new_max), 0.0)
         factor = jnp.exp(old_max - new_max)
-        l_sc[...] = l_sc[...] * factor + jnp.sum(weights, axis=1, keepdims=True)
-        acc_sc[...] = acc_sc[...] * factor + jnp.dot(
-            weights.astype(jnp.bfloat16), kv[:, HD:], preferred_element_type=jnp.float32
+        l_sc[...] = l_sc[...] * factor + jnp.sum(weights, axis=2, keepdims=True)
+        product = jnp.dot(
+            weights.reshape(heads * tokens, -1).astype(jnp.bfloat16),
+            kv[:, HD:],
+            preferred_element_type=jnp.float32,
         )
+        acc_sc[...] = acc_sc[...] * factor + product.reshape(heads, tokens, HD)
         m_sc[...] = new_max
 
     @pl.when(j == pl.num_programs(1) - 1)
     def _():
-        out_ref[...] = (acc_sc[...] / l_sc[...]).astype(out_ref.dtype)
+        out_ref[...] = (acc_sc[...] / l_sc[...]).reshape(heads * tokens, HD).astype(out_ref.dtype)
 
 
 def flash_attend(flags, queries, stacked, key_code, query_low, query_high):
     q_rows = queries.shape[0]
     k_rows = stacked.shape[0]
+    tokens = query_low.shape[0]
+    heads = q_rows // tokens
     grid_spec = pltpu.PrefetchScalarGridSpec(
         num_scalar_prefetch=1,
-        grid=(q_rows // Q_TILE, k_rows // K_TILE),
+        grid=(1, k_rows // K_TILE),
         in_specs=[
-            pl.BlockSpec((Q_TILE, HD), lambda i, j, f: (i, 0)),
+            pl.BlockSpec((q_rows, HD), lambda i, j, f: (0, 0)),
             pl.BlockSpec((K_TILE, 2 * HD), lambda i, j, f: (j, 0)),
             pl.BlockSpec((1, K_TILE), lambda i, j, f: (0, j)),
-            pl.BlockSpec((Q_TILE, 1), lambda i, j, f: (i, 0)),
-            pl.BlockSpec((Q_TILE, 1), lambda i, j, f: (i, 0)),
+            pl.BlockSpec((tokens, 1), lambda i, j, f: (0, 0)),
+            pl.BlockSpec((tokens, 1), lambda i, j, f: (0, 0)),
         ],
-        out_specs=pl.BlockSpec((Q_TILE, HD), lambda i, j, f: (i, 0)),
+        out_specs=pl.BlockSpec((q_rows, HD), lambda i, j, f: (0, 0)),
         scratch_shapes=[
-            pltpu.VMEM((Q_TILE, 1), jnp.float32),
-            pltpu.VMEM((Q_TILE, 1), jnp.float32),
-            pltpu.VMEM((Q_TILE, HD), jnp.float32),
+            pltpu.VMEM((heads, tokens, 1), jnp.float32),
+            pltpu.VMEM((heads, tokens, 1), jnp.float32),
+            pltpu.VMEM((heads, tokens, HD), jnp.float32),
         ],
     )
     return pl.pallas_call(
@@ -235,9 +242,9 @@
 def attend_model(query_rows, gathered, flags, key_code, query_low, query_high, out_weight):
     tok_rows, kv_local, group_size = query_rows.shape[:3]
     flat_query = jnp.transpose(query_rows, (1, 2, 0, 3)).reshape(-1, HD)
-    tiled_low = jnp.tile(query_low, kv_local * group_size)[:, None]
-    tiled_high = jnp.tile(query_high, kv_local * group_size)[:, None]
-    attended = flash_attend(flags, flat_query, gathered, key_code[None, :], tiled_low, tiled_high)
+    attended = flash_attend(
+        flags, flat_query, gathered, key_code[None, :], query_low[:, None], query_high[:, None]
+    )
     attended = jnp.transpose(attended.reshape(kv_local, group_size, tok_rows, HD), (2, 0, 1, 3))
     attended = attended.reshape(tok_rows, -1)
     return jnp.dot(attended, out_weight, preferred_element_type=jnp.float32)

time: 339 us -> 366 us (1.080)
  Pallas kernels: 72.6 us -> 116 us
  waiting for transfers between devices: 113 us -> 99.3 us
  starting transfers between devices: 13 us -> 7 us
    pallas_call x2, Pallas kernels: 72.6 us -> 116 us  [flash_attend(): pl.pallas_call(flash_kernel, grid_spec=grid_spec, out_shape=jax.ShapeDtyp...]
    all_gather x1, waiting for transfers between devices: 12.7 us -> 0.01 us  [local(): lax.all_gather(reference_stack, 'seq', axis=0, tiled=True)]
    ppermute x5, waiting for transfers between devices: 10.1 us -> 16.2 us  [local(): lax.ppermute(rollout_mean, 'seq', [(i, i ^ stride) for i in range(seq_cou...]
    ppermute x5, starting transfers between devices: 12.3 us -> 6.22 us  [local(): lax.ppermute(rollout_mean, 'seq', [(i, i ^ stride) for i in range(seq_cou...]
    psum x1, waiting for transfers between devices: 4.53 us -> 0.01 us  [local(): policy_summed = lax.psum(policy_part.astype(jnp.bfloat16), 'vocab')]
  transfers between devices with their start and end apart: 10 -> 10, of which waited for: 10 -> 8; matrix products, arithmetic and copies ran while one was open for 22% -> 21% of each run, Pallas kernels for 22% -> 32%
where the time goes in v7:
time: 366 us; the launch traced here: 364 us
  Pallas kernels  116 us (32%)
  waiting for transfers between devices  99.3 us (27%)
  other arithmetic  56.8 us (16%)
  local copies, waits for them, and re-layouts  29.8 us (8%)
  matrix products  29.6 us (8%)
  between operations  14.3 us (4%)
  blocking collectives  11.4 us (3%)
  starting transfers between devices  7 us (2%)
    pallas_call x2, Pallas kernels, flash_attend(): pl.pallas_call(flash_kernel, grid_spec=grid_spec, out_shape=jax.ShapeDtyp...  116 us
    all_gather x1, waiting for transfers between devices, local(): lax.all_gather(jnp.concatenate([policy_stack, carrier], axis=0), 'seq', a...  53.9 us
    ppermute x2, waiting for transfers between devices, exchange_sum(): lax.ppermute(values, axis_name, [(i, i ^ stride) for i in range(count)])  29.1 us
    ppermute x5, waiting for transfers between devices, local(): lax.ppermute(rollout_mean, 'seq', [(i, i ^ stride) for i in range(seq_cou...  16.2 us
    reduce_sum x6, other arithmetic, rms_scale(): jnp.mean(values * values, axis=-1, keepdims=True) + EPSILON  10.8 us
    reshape x4, local copies, waits for them, and re-layouts, project(): jnp.dot(normed, query_weight, preferred_element_type=jnp.float32)  8.09 us
    dot_general x2, matrix products, project(): jnp.dot(normed, query_weight, preferred_element_type=jnp.float32)  7.85 us
    dot_general x2, matrix products, attend_model(): return jnp.dot(attended, out_weight, preferred_element_type=jnp.float32)  7.48 us
  transfers between devices with their start and end apart: 10, of which 8 were waited for; matrix products, arithmetic and copies ran while one was open for 21% of the time, Pallas kernels for 32%

profile of v7, /device:TPU:0, one launch (start us, length us, event | category | flops | bytes accessed | tf_op | source)
XLA Modules:
  0.0 364.5 jit_solution(10449435017764549360)
XLA Ops:
  16.1 2.8 convolution_convert_fusion.2
  19.0 2.6 multiply_reduce_fusion.5
  32.7 2.1 convolution_convert_fusion.1
  36.2 3.9 %fusion.49 = f32[256,512]{1,0:T(8,128)} fusion(bf16[2560,512]{1,0:T(8,128)(2,1)} %param.50, bf16[256,2560]{1,0:T(8,128)(2,1)} %param.32, f32[2560]{0:T(1024)} %param.49, f32[256]{0:T(256)} %copy-done.28), kind=kOutput, calls=%fused_computation.146 | convolution fusion | flops 673710080 | bytes 4467712 | tf_op jit(solution)/shard_map/dot_general | solution.py:56
  40.1 2.0 reshape.555
  42.1 2.0 reshape.554
  44.1 4.0 %fusion.51 = f32[256,512]{1,0:T(8,128)} fusion(bf16[2560,512]{1,0:T(8,128)(2,1)} %param.39, bf16[256,2560]{1,0:T(8,128)(2,1)} %param.31, f32[2560]{0:T(1024)} %param.38, f32[256]{0:T(256)S(1)} %copy-done.27), kind=kOutput, calls=%fused_computation.147 | convolution fusion | flops 673710080 | bytes 4467712 | tf_op jit(solution)/shard_map/dot_general | solution.py:56
  48.1 2.0 reshape.550
  50.2 2.0 reshape.549
  64.0 3.1 fusion.44
  68.8 53.9 %all-gather.3.cloned.1.call-done.kv_ref = bf16[10240,256]{1,0:T(8,128)(2,1)} async-done(((bf16[320,256]{1,0:T(8,128)(2,1)}), bf16[10240,256]{1,0:T(8,128)(2,1)}) %all-gather.3.cloned.1.call-update) | async-done | bytes 5242896 | tf_op jit(solution)/shard_map/all_gather | solution.py:346
  140.4 3.7 %and_reduce_fusion = pred[20]{0:T(512)(128)(4,1)S(1)} fusion(s32[20,512]{1,0:T(8,128)} %ge.64, s32[256]{0:T(256)} %get-tuple-element.56, s32[256]{0:T(256)} %get-tuple-element.54), kind=kLoop, calls=%fused_computation | loop fusion | flops 10485740 | bytes 43028 | tf_op jit(solution)/shard_map/reduce_or | solution.py:239
  144.6 61.0 %shard_map.284 = bf16[1024,128]{1,0:T(8,128)(2,1)} custom-call(s32[20]{0:T(128)} %convert_element_type.128.flags_ref, bf16[1024,128]{1,0:T(8,128)(2,1)} %bitcast.79, bf16[10240,256]{1,0:T(8,128)(2,1)} %all-gather.3.cloned.1.call-done.kv_ref, s32[1,10240]{1,0:T(1,128)} %broadcast_in_dim_reshape.4.kcode_ref, s32[256,1]{1,0:T(8,128)} %get-tuple-element.44.qlo_ref, ...), custom_call_target="tpu_custom_call" | custom-call | tf_op jit(solution)/shard_map/pallas_call | solution.py:219
  207.4 3.8 %convolution_convert_fusion = bf16[256,2560]{1,0:T(8,128)(2,1)} fusion(bf16[256,512]{0,1:T(8,128)(2,1)} %bitcast.83, bf16[512,2560]{1,0:T(8,128)(2,1)} %param.44), kind=kOutput, calls=%fused_computation.8 | convolution fusion | flops 671744000 | bytes 4194304 | tf_op jit(solution)/shard_map/dot_general | solution.py:250
  213.5 3.3 and_reduce_fusion.1
  217.4 55.4 %shard_map.285 = bf16[1024,128]{1,0:T(8,128)(2,1)} custom-call(s32[18]{0:T(128)} %convert_element_type.131.flags_ref, bf16[1024,128]{1,0:T(8,128)(2,1)} %bitcast.80, bf16[9216,256]{1,0:T(8,128)(2,1)} %all-gather.5.cloned.1.call-done.kv_ref, s32[1,9216]{1,0:T(1,128)} %broadcast_in_dim_reshape.5.kcode_ref, s32[256,1]{1,0:T(8,128)} %get-tuple-element.44.qlo_ref, ...), custom_call_target="tpu_custom_call" | custom-call | tf_op jit(solution)/shard_map/pallas_call | solution.py:219
  273.8 3.7 %fusion.59 = bf16[256,2560]{1,0:T(8,128)(2,1)} fusion(bf16[256,512]{0,1:T(8,128)(2,1)S(1)} %bitcast.84, bf16[512,2560]{1,0:T(8,128)(2,1)} %param.55), kind=kOutput, calls=%fused_computation.152 | convolution fusion | flops 671088640 | bytes 4194304 | tf_op jit(solution)/shard_map/dot_general | solution.py:250
  277.5 3.2 collective-permute-done
  280.8 2.8 add_convert_fusion.1
  284.2 2.4 multiply_reduce_fusion.1
  286.7 2.1 fusion.58
  288.8 25.8 %collective-permute-done.1 = bf16[256,2560]{1,0:T(8,128)(2,1)} collective-permute-done((bf16[256,2560]{1,0:T(8,128)(2,1)}, bf16[256,2560]{1,0:T(8,128)(2,1)}, u32[]{:S(2)}, u32[]{:S(2)}) %collective-permute-start.1) | collective-permute-done | bytes 1310752 | tf_op jit(solution)/shard_map/ppermute | solution.py:231
  314.7 2.4 multiply_reduce_fusion
  317.1 4.0 %fusion.57 = (f32[256]{0:T(256)S(1)}, f32[256,640]{1,0:T(8,128)}) fusion(bf16[2560,640]{1,0:T(8,128)(2,1)S(1)} %copy-done.31, bf16[256,2560]{1,0:T(8,128)(2,1)S(1)} %copy-done.4, f32[2560]{0:T(1024)S(1)} %copy-done.36, f32[256]{0:T(256)S(1)} %add_rsqrt_fusion.2, bf16[256,2560]{1,0:T(8,128)(2,1)} %collective-permute-done.1, ...), kind=kOutput, calls=%fused_computation.150 | convolution fusion | flops 845577984 | bytes 7876608 | tf_op jit(solution)/shard_map/dot_general | solution.py:261
  321.1 5.6 %all-reduce.2 = (f32[256]{0:T(256)S(1)}, f32[256]{0:T(256)S(1)}) all-reduce(f32[256]{0:T(256)S(1)} %get-tuple-element.69, f32[256]{0:T(256)S(1)} %get-tuple-element.71), channel_id=1, replica_groups=mesh['seq'=32,'vocab'=4] {'vocab'}, use_global_device_ids=true, to_apply=%region_26.27 | all-reduce | flops 512 | bytes 4096 | tf_op jit(solution)/shard_map/pmax | solution.py:405
  328.5 5.8 %all-reduce.1 = (f32[256]{0:T(256)S(1)}, f32[256]{0:T(256)S(1)}, f32[256]{0:T(256)S(1)}, f32[256]{0:T(256)S(1)}) all-reduce(f32[256]{0:T(256)S(1)} %get-tuple-element.47, f32[256]{0:T(256)S(1)} %get-tuple-element.48, f32[256]{0:T(256)S(1)} %get-tuple-element.19, ...), channel_id=1, replica_groups=mesh['seq'=32,'vocab'=4] {'vocab'}, use_global_device_ids=true, to_apply=%region_24.25 | all-reduce | flops 1024 | bytes 8192 | tf_op jit(solution)/shard_map/psum | solution.py:408
  335.4 3.2 collective-permute-done.2
  340.4 3.3 collective-permute-done.3
  344.1 3.2 collective-permute-done.4
  349.0 3.3 collective-permute-done.5
  352.4 1.9 collective-permute-start.6
  354.3 3.1 collective-permute-done.6
  (169 shorter events, 66.6 us)
Async XLA Ops:
  7.2 279.4 %copy-start = (bf16[2560,640]{1,0:T(8,128)(2,1)S(1)}, bf16[2560,640]{1,0:T(8,128)(2,1)}, u32[]{:S(2)}) copy-start(bf16[2560,640]{1,0:T(8,128)(2,1)} %param.46) | copy-start | bytes 9830404
  7.2 8.1 %copy-start.34 = (f32[2560]{0:T(1024)S(1)}, f32[2560]{0:T(1024)}, u32[]{:S(2)}) copy-start(f32[2560]{0:T(1024)} %param.49) | copy-start | bytes 30724
  7.2 115.5 %all-gather.3.cloned.1.call-start = ((), (), s32[]{:S(2)}) async-start(), calls=%async_computation | async-start | bytes 5406720 | tf_op jit(solution)/shard_map/all_gather | solution.py:346
  10.5 12.8 %copy-start.25 = (s32[4,1]{0,1:T(1,128)}, s32[4,1]{0,1:T(1,128)S(1)}, u32[]{:S(2)}) copy-start(s32[4,1]{0,1:T(1,128)S(1)} %reduce-window.8) | copy-start | bytes 52
  10.5 4.7 %copy-start.3 = (bf16[256,2560]{1,0:T(8,128)(2,1)S(1)}, bf16[256,2560]{1,0:T(8,128)(2,1)}, u32[]{:S(2)}) copy-start(bf16[256,2560]{1,0:T(8,128)(2,1)} %param.32) | copy-start | bytes 3932164
  10.5 4.7 %copy-start.32 = (bf16[2560,128]{1,0:T(8,128)(2,1)S(1)}, bf16[2560,128]{1,0:T(8,128)(2,1)}, u32[]{:S(2)}) copy-start(bf16[2560,128]{1,0:T(8,128)(2,1)} %param.51) | copy-start | bytes 1966084
  19.0 12.2 %copy-start.18 = (bf16[4,8,128]{2,1,0:T(8,128)(2,1)S(1)}, bf16[4,8,128]{2,1,0:T(8,128)(2,1)}, u32[]{:S(2)}) copy-start(bf16[4,8,128]{2,1,0:T(8,128)(2,1)} %param.48) | copy-start | bytes 24580
  22.6 8.7 %copy-start.17 = (bf16[256,128]{1,0:T(8,128)(2,1)S(1)}, bf16[256,128]{1,0:T(8,128)(2,1)}, u32[]{:S(2)}) copy-start(bf16[256,128]{1,0:T(8,128)(2,1)} %convolution_convert_fusion.2) | copy-start | bytes 196612
  22.6 8.7 %copy-start.19 = (bf16[4,8,128]{2,1,0:T(8,128)(2,1)S(1)}, bf16[4,8,128]{2,1,0:T(8,128)(2,1)}, u32[]{:S(2)}) copy-start(bf16[4,8,128]{2,1,0:T(8,128)(2,1)} %param.47) | copy-start | bytes 24580
  32.6 184.8 %all-gather.5.cloned.1.call-start = ((), (), s32[]{:S(2)}) async-start(), calls=%async_computation.2 | async-start | bytes 4866048 | tf_op jit(solution)/shard_map/all_gather | solution.py:381
  36.2 8.0 %copy-start.27 = (f32[256]{0:T(256)S(1)}, f32[256]{0:T(256)}, u32[]{:S(2)}) copy-start(f32[256]{0:T(256)} %copy-done.26) | copy-start | bytes 3076
  36.2 241.4 %all-reduce.5.cloned.1.call-start = ((), (), s32[]{:S(2)}) async-start(), calls=%async_computation.1 | async-start | bytes 2621440 | tf_op jit(solution)/shard_map/psum | solution.py:388
  44.1 8.7 %copy-start.11 = (f32[256,64]{1,0:T(8,128)S(1)}, f32[256,64]{1,0:T(8,128)}, u32[]{:S(2)}) copy-start(f32[256,64]{1,0:T(8,128)} %copy-done.10) | copy-start | bytes 196612
  44.1 8.7 %copy-start.13 = (f32[256,64]{1,0:T(8,128)S(1)}, f32[256,64]{1,0:T(8,128)}, u32[]{:S(2)}) copy-start(f32[256,64]{1,0:T(8,128)} %copy-done.12) | copy-start | bytes 196612
  48.1 7.7 %copy-start.23 = (f32[128]{0:T(128)S(1)}, f32[128]{0:T(128)}, u32[]{:S(2)}) copy-start(f32[128]{0:T(128)} %param.53) | copy-start | bytes 1540
  48.1 8.1 %copy-start.24 = (f32[128]{0:T(128)S(1)}, f32[128]{0:T(128)}, u32[]{:S(2)}) copy-start(f32[128]{0:T(128)} %param.42) | copy-start | bytes 1540
  52.2 3.7 %copy-start.5 = (f32[256,4,128]{2,1,0:T(4,128)S(1)}, f32[256,4,128]{2,1,0:T(4,128)}, u32[]{:S(2)}) copy-start(f32[256,4,128]{2,1,0:T(4,128)} %reshape.555) | copy-start | bytes 1572868
  52.2 4.1 %copy-start.6 = (f32[256,4,128]{2,1,0:T(4,128)S(1)}, f32[256,4,128]{2,1,0:T(4,128)}, u32[]{:S(2)}) copy-start(f32[256,4,128]{2,1,0:T(4,128)} %reshape.550) | copy-start | bytes 1572868
  277.5 9.1 %copy-start.35 = (f32[2560]{0:T(1024)S(1)}, f32[2560]{0:T(1024)}, u32[]{:S(2)}) copy-start(f32[2560]{0:T(1024)} %param.45) | copy-start | bytes 30724
  277.5 3.2 collective-permute-start
  283.6 31.1 %collective-permute-start.1 = (bf16[256,2560]{1,0:T(8,128)(2,1)}, bf16[256,2560]{1,0:T(8,128)(2,1)}, u32[]{:S(2)}, u32[]{:S(2)}) collective-permute-start(bf16[256,2560]{1,0:T(8,128)(2,1)} %add_convert_fusion.1), channel_id=1, source_target_pairs={{0,2},{1,3},{2,0},{3,1},{4,6},{5,7},{6,4},{7,5},{8,10},{9,11},{10,... | collective-permute-start | bytes 3932168 | tf_op jit(solution)/shard_map/ppermute | solution.py:231
  286.7 28.0 %copy-start.4 = (bf16[256,2560]{1,0:T(8,128)(2,1)S(1)}, bf16[256,2560]{1,0:T(8,128)(2,1)}, u32[]{:S(2)}) copy-start(bf16[256,2560]{1,0:T(8,128)(2,1)} %param.32) | copy-start | bytes 3932164
  288.8 28.3 %copy-start.31 = (bf16[2560,640]{1,0:T(8,128)(2,1)S(1)}, bf16[2560,640]{1,0:T(8,128)(2,1)}, u32[]{:S(2)}) copy-start(bf16[2560,640]{1,0:T(8,128)(2,1)} %param.57) | copy-start | bytes 9830404
  288.8 28.3 %copy-start.36 = (f32[2560]{0:T(1024)S(1)}, f32[2560]{0:T(1024)}, u32[]{:S(2)}) copy-start(f32[2560]{0:T(1024)} %param.56) | copy-start | bytes 30724
  317.1 9.6 %copy-start.29 = (s32[256]{0:T(256)S(1)}, s32[256]{0:T(256)}, u32[]{:S(2)}) copy-start(s32[256]{0:T(256)} %param.33) | copy-start | bytes 3076
  317.1 17.2 %copy-start.21 = (s32[256]{0:T(256)S(1)}, s32[256]{0:T(256)}, u32[]{:S(2)}) copy-start(s32[256]{0:T(256)} %get-tuple-element.23) | copy-start | bytes 3076
  317.1 17.7 %copy-start.22 = (s32[256]{0:T(256)S(1)}, s32[256]{0:T(256)}, u32[]{:S(2)}) copy-start(s32[256]{0:T(256)} %get-tuple-element.22) | copy-start | bytes 3076
  335.0 3.6 collective-permute-start.2
  338.6 5.1 %collective-permute-start.3 = (f32[4]{0:T(128)S(1)}, f32[4]{0:T(128)S(1)}, u32[]{:S(2)}, u32[]{:S(2)}) collective-permute-start(f32[4]{0:T(128)S(1)} %add.308), channel_id=1, source_target_pairs={{0,8},{4,12},{8,0},{12,4},{16,24},{20,28},{24,16},{28,20},{32,40},... | collective-permute-start | bytes 56 | tf_op jit(solution)/shard_map/ppermute | solution.py:419
  343.7 3.6 collective-permute-start.4
  347.3 5.1 %collective-permute-start.5 = (f32[4]{0:T(128)S(1)}, f32[4]{0:T(128)S(1)}, u32[]{:S(2)}, u32[]{:S(2)}) collective-permute-start(f32[4]{0:T(128)S(1)} %add.310), channel_id=1, source_target_pairs={{0,32},{4,36},{8,40},{12,44},{16,48},{20,52},{24,56},{28,60},{32,0... | collective-permute-start | bytes 56 | tf_op jit(solution)/shard_map/ppermute | solution.py:419
  352.4 5.1 %collective-permute-start.6 = (f32[4]{0:T(128)S(1)}, f32[4]{0:T(128)S(1)}, u32[]{:S(2)}, u32[]{:S(2)}) collective-permute-start(f32[4]{0:T(128)S(1)} %add.311), channel_id=1, source_target_pairs={{0,64},{4,68},{8,72},{12,76},{16,80},{20,84},{24,88},{28,92},{32,9... | collective-permute-start | bytes 56 | tf_op jit(solution)/shard_map/ppermute | solution.py:419
  (15 other events, 27.3 us)
Sparse Core Ops, SparseCore 0:
  32.7 89.9 all-gather.2
  125.8 81.5 all-gather.4
  211.3 41.3 all-reduce.4

commit v8 on v6

--- a/solution.py
+++ b/solution.py
@@ -369,19 +369,26 @@
         query_high,
         policy_out_weight,
     )
-    reference_part = attend_model(
-        reference_query,
-        lax.all_gather(reference_stack, "seq", axis=0, tiled=True),
-        flags,
-        key_code,
-        query_low,
-        query_high,
-        reference_out_weight,
-    )
     policy_summed = lax.psum(policy_part.astype(jnp.bfloat16), "vocab")
-    policy_summed, reference_part = lax.optimization_barrier((policy_summed, reference_part))
     policy_mixed = policy_summed.astype(jnp.float32)
-    reference_mixed = exchange_sum(reference_part.astype(jnp.bfloat16), "vocab").astype(jnp.float32)
+    reference_gathered = lax.all_gather(reference_stack, "seq", axis=0, tiled=True)
+    _, reference_gathered = lax.optimization_barrier((policy_part, reference_gathered))
+    half = tok_rows // 2
+    reference_halves = []
+    for lo in (0, half):
+        half_low = query_low[lo : lo + half]
+        half_high = query_high[lo : lo + half]
+        half_part = attend_model(
+            reference_query[lo : lo + half],
+            reference_gathered,
+            tile_flags(key_code, half_low, half_high),
+            key_code,
+            half_low,
+            half_high,
+            reference_out_weight,
+        )
+        reference_halves.append(exchange_sum(half_part.astype(jnp.bfloat16), "vocab"))
+    reference_mixed = jnp.concatenate(reference_halves, axis=0).astype(jnp.float32)
     policy_final = rms_scale(
         policy_hidden.astype(jnp.float32) + policy_mixed, policy_final_gain
     ).astype(jnp.bfloat16)

time: 339 us -> 353 us (1.041)
  waiting for transfers between devices: 113 us -> 134 us
  starting transfers between devices: 13 us -> 8.37 us
  local copies, waits for them, and re-layouts: 28.9 us -> 24.4 us
    ppermute x2 -> x4, waiting for transfers between devices: 29.4 us -> 7.96 us  [exchange_sum(): lax.ppermute(values, axis_name, [(i, i ^ stride) for i in range(count)])]
    all_gather x1, waiting for transfers between devices: 12.7 us -> 32.7 us  [local(): lax.all_gather(reference_stack, 'seq', axis=0, tiled=True)]
    psum x1, waiting for transfers between devices: 4.53 us -> 24.4 us  [local(): policy_summed = lax.psum(policy_part.astype(jnp.bfloat16), 'vocab')]
    ppermute x5, waiting for transfers between devices: 10.1 us -> 17 us  [local(): lax.ppermute(rollout_mean, 'seq', [(i, i ^ stride) for i in range(seq_cou...]
    ppermute x5, starting transfers between devices: 12.3 us -> 5.45 us  [local(): lax.ppermute(rollout_mean, 'seq', [(i, i ^ stride) for i in range(seq_cou...]
    all_gather x1, waiting for transfers between devices: 56.6 us -> 52.3 us  [local(): lax.all_gather(jnp.concatenate([policy_stack, carrier], axis=0), 'seq', a...]
    pallas_call x2 -> x3, Pallas kernels: 72.6 us -> 75 us  [flash_attend(): pl.pallas_call(flash_kernel, grid_spec=grid_spec, out_shape=jax.ShapeDtyp...]
    reshape x4 -> x3, local copies, waits for them, and re-layouts: 8.09 us -> 6.05 us  [project(): jnp.dot(normed, query_weight, preferred_element_type=jnp.float32)]
  transfers between devices with their start and end apart: 10 -> 12, of which waited for: 10 -> 9; matrix products, arithmetic and copies ran while one was open for 22% -> 19% of each run, Pallas kernels for 22% -> 16%
where the time goes in v8:
time: 353 us; the launch traced here: 351 us
  waiting for transfers between devices  134 us (38%)
  Pallas kernels  75 us (21%)
  other arithmetic  53.9 us (15%)
  matrix products  29.6 us (8%)
  local copies, waits for them, and re-layouts  24.4 us (7%)
  between operations  14.3 us (4%)
  blocking collectives  11.4 us (3%)
  starting transfers between devices  8.37 us (2%)
    pallas_call x3, Pallas kernels, flash_attend(): pl.pallas_call(flash_kernel, grid_spec=grid_spec, out_shape=jax.ShapeDtyp...  75 us
    all_gather x1, waiting for transfers between devices, local(): lax.all_gather(jnp.concatenate([policy_stack, carrier], axis=0), 'seq', a...  52.3 us
    all_gather x1, waiting for transfers between devices, local(): lax.all_gather(reference_stack, 'seq', axis=0, tiled=True)  32.7 us
    psum x1, waiting for transfers between devices, local(): policy_summed = lax.psum(policy_part.astype(jnp.bfloat16), 'vocab')  24.4 us
    ppermute x5, waiting for transfers between devices, local(): lax.ppermute(rollout_mean, 'seq', [(i, i ^ stride) for i in range(seq_cou...  17 us
    dot_general x3, matrix products, attend_model(): return jnp.dot(attended, out_weight, preferred_element_type=jnp.float32)  9.07 us
    reduce_sum x6, other arithmetic, rms_scale(): jnp.mean(values * values, axis=-1, keepdims=True) + EPSILON  9.05 us
    ppermute x4, waiting for transfers between devices, exchange_sum(): lax.ppermute(values, axis_name, [(i, i ^ stride) for i in range(count)])  7.96 us
  transfers between devices with their start and end apart: 12, of which 9 were waited for; matrix products, arithmetic and copies ran while one was open for 19% of the time, Pallas kernels for 16%

profile of v8, /device:TPU:0, one launch (start us, length us, event | category | flops | bytes accessed | tf_op | source)
XLA Modules:
  0.0 351.2 jit_solution(15261269859614325950)
XLA Ops:
  17.4 2.7 convolution_convert_fusion.3
  20.1 2.5 multiply_reduce_fusion.5
  33.0 2.1 convolution_convert_fusion.2
  36.8 3.9 %fusion.49 = f32[256,512]{1,0:T(8,128)} fusion(bf16[2560,512]{1,0:T(8,128)(2,1)} %param.39, bf16[256,2560]{1,0:T(8,128)(2,1)} %param.31, f32[2560]{0:T(1024)} %param.38, f32[256]{0:T(256)} %add_rsqrt_fusion.7), kind=kOutput, calls=%fused_computation.149 | convolution fusion | flops 673710080 | bytes 4467712 | tf_op jit(solution)/shard_map/dot_general | solution.py:56
  40.6 2.0 reshape.522
  42.7 2.0 reshape.521
  53.3 3.9 %fusion.47 = f32[256,512]{1,0:T(8,128)} fusion(bf16[2560,512]{1,0:T(8,128)(2,1)} %param.50, bf16[256,2560]{1,0:T(8,128)(2,1)} %param.32, f32[2560]{0:T(1024)} %param.49, f32[256]{0:T(256)} %copy-done.25), kind=kOutput, calls=%fused_computation.148 | convolution fusion | flops 673710080 | bytes 4467712 | tf_op jit(solution)/shard_map/dot_general | solution.py:56
  57.2 2.0 reshape.526
  68.2 2.6 fusion.41
  70.8 52.3 %all-gather.3.cloned.1.call-done.kv_ref = bf16[10240,256]{1,0:T(8,128)(2,1)} async-done(((bf16[320,256]{1,0:T(8,128)(2,1)}), bf16[10240,256]{1,0:T(8,128)(2,1)}) %all-gather.3.cloned.1.call-update) | async-done | bytes 5242896 | tf_op jit(solution)/shard_map/all_gather | solution.py:339
  128.4 2.9 and_reduce_fusion
  131.9 38.3 %shard_map.284 = bf16[1024,128]{1,0:T(8,128)(2,1)} custom-call(s32[10]{0:T(128)} %convert_element_type.145.flags_ref, bf16[1024,128]{1,0:T(8,128)(2,1)} %bitcast.101, bf16[10240,256]{1,0:T(8,128)(2,1)} %all-gather.3.cloned.1.call-done.kv_ref, s32[1,10240]{1,0:T(1,128)} %broadcast_in_dim_reshape.4.kcode_ref, s32[1024,1]{1,0:T(8,128)} %bitcast.99, ...), custom_call_target="tpu_custom_call" | custom-call | tf_op jit(solution)/shard_map/pallas_call | solution.py:212
  171.3 3.7 %fusion.59 = bf16[256,2560]{1,0:T(8,128)(2,1)} fusion(bf16[256,512]{0,1:T(8,128)(2,1)S(1)} %bitcast.103, bf16[512,2560]{1,0:T(8,128)(2,1)} %param.44), kind=kOutput, calls=%fused_computation.156 | convolution fusion | flops 671088640 | bytes 4194304 | tf_op jit(solution)/shard_map/dot_general | solution.py:243
  174.9 32.7 %all-gather.5.cloned.1.call-done.kv_ref = bf16[9216,256]{1,0:T(8,128)(2,1)} async-done(((bf16[288,256]{1,0:T(8,128)(2,1)}), bf16[9216,256]{1,0:T(8,128)(2,1)}) %all-gather.5.cloned.1.call-update) | async-done | bytes 4718608 | tf_op jit(solution)/shard_map/all_gather | solution.py:374
  207.7 4.0 %and_reduce_fusion.2 = (pred[9]{0:T(512)(128)(4,1)}, pred[9]{0:T(512)(128)(4,1)S(1)}) fusion(s32[9,1024]{1,0:T(8,128)} %ge.80, s32[128]{0:T(128)S(1)} %get-tuple-element.74, s32[128]{0:T(128)S(1)} %copy-done.14, s32[128]{0:T(128)S(1)} %copy-done.18, s32[128]{0:T(128)S(1)} %copy-done.16), kind=kLoop, calls=%fused_computation.2 | loop fusion | flops 9437166 | bytes 38930 | tf_op jit(solution)/shard_map/reduce_or | solution.py:232
  212.2 18.3 %shard_map.286 = bf16[512,128]{1,0:T(8,128)(2,1)} custom-call(s32[9]{0:T(128)} %convert_element_type.163.flags_ref, bf16[512,128]{1,0:T(8,128)(2,1)} %bitcast.104, bf16[9216,256]{1,0:T(8,128)(2,1)} %all-gather.5.cloned.1.call-done.kv_ref, s32[1,9216]{1,0:T(1,128)} %broadcast_in_dim_reshape.5.kcode_ref, s32[512,1]{1,0:T(8,128)} %copy.109.qlo_ref, ...), custom_call_target="tpu_custom_call" | custom-call | tf_op jit(solution)/shard_map/pallas_call | solution.py:212
  231.6 3.1 convolution_convert_fusion
  237.7 18.3 %shard_map.285 = bf16[512,128]{1,0:T(8,128)(2,1)} custom-call(s32[9]{0:T(128)} %convert_element_type.151.flags_ref, bf16[512,128]{1,0:T(8,128)(2,1)} %bitcast.105, bf16[9216,256]{1,0:T(8,128)(2,1)} %all-gather.5.cloned.1.call-done.kv_ref, s32[1,9216]{1,0:T(1,128)} %broadcast_in_dim_reshape.5.kcode_ref, s32[512,1]{1,0:T(8,128)} %copy.105.qlo_ref, ...), custom_call_target="tpu_custom_call" | custom-call | tf_op jit(solution)/shard_map/pallas_call | solution.py:212
  257.0 2.3 convolution_convert_fusion.1
  259.9 2.3 add_convert_fusion.1
  265.2 24.4 %all-reduce.5.cloned.1.call-done = bf16[256,2560]{1,0:T(8,128)(2,1)} async-done(((bf16[256,2560]{1,0:T(8,128)(2,1)}), bf16[256,2560]{1,0:T(8,128)(2,1)}) %all-reduce.5.cloned.1.call-update) | async-done | bytes 1310736 | tf_op jit(solution)/shard_map/psum | solution.py:372
  289.6 2.4 multiply_reduce_fusion.1
  292.1 2.1 fusion.58
  295.8 8.0 %collective-permute-done.1 = bf16[128,2560]{1,0:T(8,128)(2,1)} collective-permute-done((bf16[128,2560]{1,0:T(8,128)(2,1)}, bf16[128,2560]{1,0:T(8,128)(2,1)}, u32[]{:S(2)}, u32[]{:S(2)}) %collective-permute-start.1) | collective-permute-done | bytes 655392 | tf_op jit(solution)/shard_map/ppermute | solution.py:224
  305.8 2.1 fusion.57
  307.9 5.6 %all-reduce.2 = (f32[256]{0:T(256)S(1)}, f32[256]{0:T(256)S(1)}) all-reduce(f32[256]{0:T(256)S(1)} %get-tuple-element.68, f32[256]{0:T(256)S(1)} %get-tuple-element.70), channel_id=1, replica_groups=mesh['seq'=32,'vocab'=4] {'vocab'}, use_global_device_ids=true, to_apply=%region_27.28 | all-reduce | flops 512 | bytes 4096 | tf_op jit(solution)/shard_map/pmax | solution.py:405
  315.3 5.8 %all-reduce.1 = (f32[256]{0:T(256)S(1)}, f32[256]{0:T(256)S(1)}, f32[256]{0:T(256)S(1)}, f32[256]{0:T(256)S(1)}) all-reduce(f32[256]{0:T(256)S(1)} %get-tuple-element.45, f32[256]{0:T(256)S(1)} %get-tuple-element.46, f32[256]{0:T(256)S(1)} %get-tuple-element.17, ...), channel_id=1, replica_groups=mesh['seq'=32,'vocab'=4] {'vocab'}, use_global_device_ids=true, to_apply=%region_25.26 | all-reduce | flops 1024 | bytes 8192 | tf_op jit(solution)/shard_map/psum | solution.py:408
  322.1 3.3 collective-permute-done.4
  326.9 3.6 %collective-permute-done.5 = f32[4]{0:T(128)S(1)} collective-permute-done((f32[4]{0:T(128)S(1)}, f32[4]{0:T(128)S(1)}, u32[]{:S(2)}, u32[]{:S(2)}) %collective-permute-start.5) | collective-permute-done | bytes 48 | tf_op jit(solution)/shard_map/ppermute | solution.py:419
  330.7 3.3 collective-permute-done.6
  335.5 3.6 %collective-permute-done.7 = f32[4]{0:T(128)S(1)} collective-permute-done((f32[4]{0:T(128)S(1)}, f32[4]{0:T(128)S(1)}, u32[]{:S(2)}, u32[]{:S(2)}) %collective-permute-start.7) | collective-permute-done | bytes 48 | tf_op jit(solution)/shard_map/ppermute | solution.py:419
  341.0 3.2 collective-permute-done.8
  (189 shorter events, 67.7 us)
Async XLA Ops:
  7.2 284.8 %copy-start = (bf16[2560,640]{1,0:T(8,128)(2,1)S(1)}, bf16[2560,640]{1,0:T(8,128)(2,1)}, u32[]{:S(2)}) copy-start(bf16[2560,640]{1,0:T(8,128)(2,1)} %param.46) | copy-start | bytes 9830404
  7.2 8.1 %copy-start.33 = (f32[2560]{0:T(1024)S(1)}, f32[2560]{0:T(1024)}, u32[]{:S(2)}) copy-start(f32[2560]{0:T(1024)} %param.49) | copy-start | bytes 30724
  7.2 115.9 %all-gather.3.cloned.1.call-start = ((), (), s32[]{:S(2)}) async-start(), calls=%async_computation | async-start | bytes 5406720 | tf_op jit(solution)/shard_map/all_gather | solution.py:339
  10.5 13.8 %copy-start.23 = (s32[4,1]{0,1:T(1,128)}, s32[4,1]{0,1:T(1,128)S(1)}, u32[]{:S(2)}) copy-start(s32[4,1]{0,1:T(1,128)S(1)} %reduce-window.8) | copy-start | bytes 52
  11.3 13.7 %copy-start.24 = (s32[4]{0:T(128)}, s32[4]{0:T(128)S(1)}, u32[]{:S(2)}) copy-start(s32[4]{0:T(128)S(1)} %bitcast_subtract_fusion) | copy-start | bytes 52
  23.6 7.9 %copy-start.12 = (bf16[256,128]{1,0:T(8,128)(2,1)S(1)}, bf16[256,128]{1,0:T(8,128)(2,1)}, u32[]{:S(2)}) copy-start(bf16[256,128]{1,0:T(8,128)(2,1)} %convolution_convert_fusion.3) | copy-start | bytes 196612
  33.0 174.7 %all-gather.5.cloned.1.call-start = ((), (), s32[]{:S(2)}) async-start(), calls=%async_computation.2 | async-start | bytes 4866048 | tf_op jit(solution)/shard_map/all_gather | solution.py:374
  36.5 253.1 %all-reduce.5.cloned.1.call-start = ((), (), s32[]{:S(2)}) async-start(), calls=%async_computation.1 | async-start | bytes 2621440 | tf_op jit(solution)/shard_map/psum | solution.py:372
  40.6 7.4 %copy-start.21 = (f32[128]{0:T(128)S(1)}, f32[128]{0:T(128)}, u32[]{:S(2)}) copy-start(f32[128]{0:T(128)} %param.42) | copy-start | bytes 1540
  53.3 7.4 %copy-start.22 = (f32[128]{0:T(128)S(1)}, f32[128]{0:T(128)}, u32[]{:S(2)}) copy-start(f32[128]{0:T(128)} %param.53) | copy-start | bytes 1540
  62.4 63.7 %copy-start.13 = (s32[320]{0:T(512)S(1)}, s32[320]{0:T(512)}, u32[]{:S(2)}) copy-start(s32[320]{0:T(512)} %pad.21.clone) | copy-start | bytes 3844
  65.0 58.1 %copy-start.15 = (s32[128]{0:T(128)}, s32[128]{0:T(128)S(1)}, u32[]{:S(2)}) copy-start(s32[128]{0:T(128)S(1)} %get-tuple-element.51) | copy-start | bytes 1540
  65.0 58.1 %copy-start.17 = (s32[128]{0:T(128)}, s32[128]{0:T(128)S(1)}, u32[]{:S(2)}) copy-start(s32[128]{0:T(128)S(1)} %get-tuple-element.75) | copy-start | bytes 1540
  170.2 37.5 %copy-start.14 = (s32[128]{0:T(128)S(1)}, s32[128]{0:T(128)}, u32[]{:S(2)}) copy-start(s32[128]{0:T(128)} %get-tuple-element.52) | copy-start | bytes 1540
  170.2 37.5 %copy-start.16 = (s32[128]{0:T(128)S(1)}, s32[128]{0:T(128)}, u32[]{:S(2)}) copy-start(s32[128]{0:T(128)} %copy-done.15) | copy-start | bytes 1540
  170.2 37.5 %copy-start.18 = (s32[128]{0:T(128)S(1)}, s32[128]{0:T(128)}, u32[]{:S(2)}) copy-start(s32[128]{0:T(128)} %copy-done.17) | copy-start | bytes 1540
  234.7 25.2 %collective-permute-start.2 = (bf16[128,2560]{1,0:T(8,128)(2,1)}, bf16[128,2560]{1,0:T(8,128)(2,1)}, u32[]{:S(2)}, u32[]{:S(2)}) collective-permute-start(bf16[128,2560]{1,0:T(8,128)(2,1)} %convolution_convert_fusion), channel_id=1, source_target_pairs={{0,1},{1,0},{2,3},{3,2},{4,5},{5,4},{6,7},{7,6},{8,9},{9,8},{10,11... | collective-permute-start | bytes 1966088 | tf_op jit(solution)/shard_map/ppermute | solution.py:224
  259.3 3.5 %collective-permute-start = (bf16[128,2560]{1,0:T(8,128)(2,1)S(1)}, bf16[128,2560]{1,0:T(8,128)(2,1)S(1)}, u32[]{:S(2)}, u32[]{:S(2)}) collective-permute-start(bf16[128,2560]{1,0:T(8,128)(2,1)S(1)} %convolution_convert_fusion.1), channel_id=1, source_target_pairs={{0,1},{1,0},{2,3},{3,2},{4,5},{5,4},{6,7},{7,6},{8,9},{9,8},{10,11... | collective-permute-start | bytes 1966088 | tf_op jit(solution)/shard_map/ppermute | solution.py:224
  262.2 29.8 %copy-start.34 = (f32[2560]{0:T(1024)S(1)}, f32[2560]{0:T(1024)}, u32[]{:S(2)}) copy-start(f32[2560]{0:T(1024)} %param.45) | copy-start | bytes 30724
  262.2 32.0 %collective-permute-start.3 = (bf16[128,2560]{1,0:T(8,128)(2,1)}, bf16[128,2560]{1,0:T(8,128)(2,1)}, u32[]{:S(2)}, u32[]{:S(2)}) collective-permute-start(bf16[128,2560]{1,0:T(8,128)(2,1)} %add_convert_fusion.1), channel_id=1, source_target_pairs={{0,2},{1,3},{2,0},{3,1},{4,6},{5,7},{6,4},{7,5},{8,10},{9,11},{10,... | collective-permute-start | bytes 1966088 | tf_op jit(solution)/shard_map/ppermute | solution.py:224
  263.8 39.9 %collective-permute-start.1 = (bf16[128,2560]{1,0:T(8,128)(2,1)}, bf16[128,2560]{1,0:T(8,128)(2,1)}, u32[]{:S(2)}, u32[]{:S(2)}) collective-permute-start(bf16[128,2560]{1,0:T(8,128)(2,1)} %add_convert_fusion.3), channel_id=1, source_target_pairs={{0,2},{1,3},{2,0},{3,1},{4,6},{5,7},{6,4},{7,5},{8,10},{9,11},{10,... | collective-permute-start | bytes 1966088 | tf_op jit(solution)/shard_map/ppermute | solution.py:224
  294.2 11.0 %copy-start.5 = (bf16[256,2560]{1,0:T(8,128)(2,1)S(1)}, bf16[256,2560]{1,0:T(8,128)(2,1)}, u32[]{:S(2)}) copy-start(bf16[256,2560]{1,0:T(8,128)(2,1)} %param.32) | copy-start | bytes 3932164
  295.8 9.9 %copy-start.30 = (bf16[2560,640]{1,0:T(8,128)(2,1)S(1)}, bf16[2560,640]{1,0:T(8,128)(2,1)}, u32[]{:S(2)}) copy-start(bf16[2560,640]{1,0:T(8,128)(2,1)} %param.57) | copy-start | bytes 9830404
  295.8 9.9 %copy-start.35 = (f32[2560]{0:T(1024)S(1)}, f32[2560]{0:T(1024)}, u32[]{:S(2)}) copy-start(f32[2560]{0:T(1024)} %param.56) | copy-start | bytes 30724
  305.7 7.8 %copy-start.27 = (s32[256]{0:T(256)S(1)}, s32[256]{0:T(256)}, u32[]{:S(2)}) copy-start(s32[256]{0:T(256)} %param.33) | copy-start | bytes 3076
  305.8 15.3 %copy-start.19 = (s32[256]{0:T(256)S(1)}, s32[256]{0:T(256)}, u32[]{:S(2)}) copy-start(s32[256]{0:T(256)} %get-tuple-element.23) | copy-start | bytes 3076
  305.8 15.9 %copy-start.20 = (s32[256]{0:T(256)S(1)}, s32[256]{0:T(256)}, u32[]{:S(2)}) copy-start(s32[256]{0:T(256)} %get-tuple-element.22) | copy-start | bytes 3076
  321.8 3.6 %collective-permute-start.4 = (f32[4]{0:T(128)S(1)}, f32[4]{0:T(128)S(1)}, u32[]{:S(2)}, u32[]{:S(2)}) collective-permute-start(f32[4]{0:T(128)S(1)} %select_reduce_fusion.1), channel_id=1, source_target_pairs={{0,4},{4,0},{8,12},{12,8},{16,20},{20,16},{24,28},{28,24},{32,36},... | collective-permute-start | bytes 56 | tf_op jit(solution)/shard_map/ppermute | solution.py:419
  325.4 5.1 %collective-permute-start.5 = (f32[4]{0:T(128)S(1)}, f32[4]{0:T(128)S(1)}, u32[]{:S(2)}, u32[]{:S(2)}) collective-permute-start(f32[4]{0:T(128)S(1)} %add.300), channel_id=1, source_target_pairs={{0,8},{4,12},{8,0},{12,4},{16,24},{20,28},{24,16},{28,20},{32,40},... | collective-permute-start | bytes 56 | tf_op jit(solution)/shard_map/ppermute | solution.py:419
  330.5 3.6 %collective-permute-start.6 = (f32[4]{0:T(128)S(1)}, f32[4]{0:T(128)S(1)}, u32[]{:S(2)}, u32[]{:S(2)}) collective-permute-start(f32[4]{0:T(128)S(1)} %add.301), channel_id=1, source_target_pairs={{0,16},{4,20},{8,24},{12,28},{16,0},{20,4},{24,8},{28,12},{32,48},... | collective-permute-start | bytes 56 | tf_op jit(solution)/shard_map/ppermute | solution.py:419
  334.1 5.1 %collective-permute-start.7 = (f32[4]{0:T(128)S(1)}, f32[4]{0:T(128)S(1)}, u32[]{:S(2)}, u32[]{:S(2)}) collective-permute-start(f32[4]{0:T(128)S(1)} %add.302), channel_id=1, source_target_pairs={{0,32},{4,36},{8,40},{12,44},{16,48},{20,52},{24,56},{28,60},{32,0... | collective-permute-start | bytes 56 | tf_op jit(solution)/shard_map/ppermute | solution.py:419
  339.1 5.1 %collective-permute-start.8 = (f32[4]{0:T(128)S(1)}, f32[4]{0:T(128)S(1)}, u32[]{:S(2)}, u32[]{:S(2)}) collective-permute-start(f32[4]{0:T(128)S(1)} %add.303), channel_id=1, source_target_pairs={{0,64},{4,68},{8,72},{12,76},{16,80},{20,84},{24,88},{28,92},{32,9... | collective-permute-start | bytes 56 | tf_op jit(solution)/shard_map/ppermute | solution.py:419
  (16 other events, 57.9 us)
Sparse Core Ops, SparseCore 0:
  33.1 89.9 all-gather.2
  126.2 81.4 all-gather.4
  237.3 52.2 all-reduce.4

commit v9 on v8

--- a/solution.py
+++ b/solution.py
@@ -369,7 +369,7 @@
         query_high,
         policy_out_weight,
     )
-    policy_summed = lax.psum(policy_part.astype(jnp.bfloat16), "vocab")
+    policy_summed = exchange_sum(policy_part.astype(jnp.bfloat16), "vocab")
     policy_mixed = policy_summed.astype(jnp.float32)
     reference_gathered = lax.all_gather(reference_stack, "seq", axis=0, tiled=True)
     _, reference_gathered = lax.optimization_barrier((policy_part, reference_gathered))

time: 353 us -> 364 us (1.031)
  waiting for transfers between devices: 134 us -> 149 us
  other arithmetic: 53.9 us -> 49.7 us
    ppermute x4 -> x6, waiting for transfers between devices: 7.96 us -> 51.2 us  [exchange_sum(): lax.ppermute(values, axis_name, [(i, i ^ stride) for i in range(count)])]
    psum x1 -> x0, waiting for transfers between devices: 24.4 us -> none  [local(): policy_summed = lax.psum(policy_part.astype(jnp.bfloat16), 'vocab')]
    all_gather x1, waiting for transfers between devices: 32.7 us -> 27.9 us  [local(): lax.all_gather(reference_stack, 'seq', axis=0, tiled=True)]
  transfers between devices with their start and end apart: 12 -> 13, of which waited for: 9 -> 10; matrix products, arithmetic and copies ran while one was open for 19% -> 19% of each run, Pallas kernels for 16% -> 16%
where the time goes in v9:
time: 364 us; the launch traced here: 363 us
  waiting for transfers between devices  149 us (41%)
  Pallas kernels  75.1 us (21%)
  other arithmetic  49.7 us (14%)
  matrix products  29.7 us (8%)
  local copies, waits for them, and re-layouts  24.3 us (7%)
  between operations  14.6 us (4%)
  blocking collectives  11.4 us (3%)
  starting transfers between devices  9.42 us (3%)
    pallas_call x3, Pallas kernels, flash_attend(): pl.pallas_call(flash_kernel, grid_spec=grid_spec, out_shape=jax.ShapeDtyp...  75.1 us
    all_gather x1, waiting for transfers between devices, local(): lax.all_gather(jnp.concatenate([policy_stack, carrier], axis=0), 'seq', a...  52.4 us
    ppermute x6, waiting for transfers between devices, exchange_sum(): lax.ppermute(values, axis_name, [(i, i ^ stride) for i in range(count)])  51.2 us
    all_gather x1, waiting for transfers between devices, local(): lax.all_gather(reference_stack, 'seq', axis=0, tiled=True)  27.9 us
    ppermute x5, waiting for transfers between devices, local(): lax.ppermute(rollout_mean, 'seq', [(i, i ^ stride) for i in range(seq_cou...  17 us
    dot_general x3, matrix products, attend_model(): return jnp.dot(attended, out_weight, preferred_element_type=jnp.float32)  9.18 us
    dot_general x2, matrix products, project(): jnp.dot(normed, query_weight, preferred_element_type=jnp.float32)  7.73 us
    reduce_sum x6, other arithmetic, rms_scale(): jnp.mean(values * values, axis=-1, keepdims=True) + EPSILON  7.36 us
  transfers between devices with their start and end apart: 13, of which 10 were waited for; matrix products, arithmetic and copies ran while one was open for 19% of the time, Pallas kernels for 16%

profile of v9, /device:TPU:0, one launch (start us, length us, event | category | flops | bytes accessed | tf_op | source)
XLA Modules:
  0.0 362.7 jit_solution(15580590405067176687)
XLA Ops:
  17.4 2.7 convolution_convert_fusion.3
  20.1 2.5 multiply_reduce_fusion.5
  33.2 2.1 convolution_convert_fusion.2
  36.7 3.9 %fusion.49 = f32[256,512]{1,0:T(8,128)} fusion(bf16[2560,512]{1,0:T(8,128)(2,1)} %param.39, bf16[256,2560]{1,0:T(8,128)(2,1)} %param.31, f32[2560]{0:T(1024)} %param.38, f32[256]{0:T(256)} %add_rsqrt_fusion.7), kind=kOutput, calls=%fused_computation.151 | convolution fusion | flops 673710080 | bytes 4467712 | tf_op jit(solution)/shard_map/dot_general | solution.py:56
  40.6 2.0 reshape.522
  42.6 2.0 reshape.521
  53.2 3.9 %fusion.47 = f32[256,512]{1,0:T(8,128)} fusion(bf16[2560,512]{1,0:T(8,128)(2,1)} %param.50, bf16[256,2560]{1,0:T(8,128)(2,1)} %param.32, f32[2560]{0:T(1024)} %param.49, f32[256]{0:T(256)} %copy-done.25), kind=kOutput, calls=%fused_computation.150 | convolution fusion | flops 673710080 | bytes 4467712 | tf_op jit(solution)/shard_map/dot_general | solution.py:56
  57.1 2.0 reshape.526
  68.2 2.6 fusion.41
  70.7 52.4 %all-gather.3.cloned.1.call-done.kv_ref = bf16[10240,256]{1,0:T(8,128)(2,1)} async-done(((bf16[320,256]{1,0:T(8,128)(2,1)}), bf16[10240,256]{1,0:T(8,128)(2,1)}) %all-gather.3.cloned.1.call-update) | async-done | bytes 5242896 | tf_op jit(solution)/shard_map/all_gather | solution.py:339
  128.4 2.9 and_reduce_fusion
  131.9 38.5 %shard_map.284 = bf16[1024,128]{1,0:T(8,128)(2,1)} custom-call(s32[10]{0:T(128)} %convert_element_type.163.flags_ref, bf16[1024,128]{1,0:T(8,128)(2,1)} %bitcast.101, bf16[10240,256]{1,0:T(8,128)(2,1)} %all-gather.3.cloned.1.call-done.kv_ref, s32[1,10240]{1,0:T(1,128)} %broadcast_in_dim_reshape.4.kcode_ref, s32[1024,1]{1,0:T(8,128)} %bitcast.99, ...), custom_call_target="tpu_custom_call" | custom-call | tf_op jit(solution)/shard_map/pallas_call | solution.py:212
  171.5 4.0 %and_reduce_fusion.2 = (pred[9]{0:T(512)(128)(4,1)}, pred[9]{0:T(512)(128)(4,1)S(1)}) fusion(s32[9,1024]{1,0:T(8,128)} %ge.80, s32[128]{0:T(128)S(1)} %get-tuple-element.74, s32[128]{0:T(128)S(1)} %copy-done.14, s32[128]{0:T(128)S(1)} %copy-done.18, s32[128]{0:T(128)S(1)} %copy-done.16), kind=kLoop, calls=%fused_computation.2 | loop fusion | flops 9437166 | bytes 38930 | tf_op jit(solution)/shard_map/reduce_or | solution.py:232
  176.0 3.8 %fusion.59 = bf16[256,2560]{1,0:T(8,128)(2,1)} fusion(bf16[256,512]{0,1:T(8,128)(2,1)S(1)} %bitcast.102, bf16[512,2560]{1,0:T(8,128)(2,1)} %param.44), kind=kOutput, calls=%fused_computation.158 | convolution fusion | flops 671088640 | bytes 4194304 | tf_op jit(solution)/shard_map/dot_general | solution.py:243
  179.8 27.9 %all-gather.5.cloned.1.call-done.kv_ref = bf16[9216,256]{1,0:T(8,128)(2,1)} async-done(((bf16[288,256]{1,0:T(8,128)(2,1)}), bf16[9216,256]{1,0:T(8,128)(2,1)}) %all-gather.5.cloned.1.call-update) | async-done | bytes 4718608 | tf_op jit(solution)/shard_map/all_gather | solution.py:374
  207.7 18.3 %shard_map.286 = bf16[512,128]{1,0:T(8,128)(2,1)} custom-call(s32[9]{0:T(128)} %convert_element_type.187.flags_ref, bf16[512,128]{1,0:T(8,128)(2,1)} %bitcast.104, bf16[9216,256]{1,0:T(8,128)(2,1)} %all-gather.5.cloned.1.call-done.kv_ref, s32[1,9216]{1,0:T(1,128)} %broadcast_in_dim_reshape.5.kcode_ref, s32[512,1]{1,0:T(8,128)} %copy.109.qlo_ref, ...), custom_call_target="tpu_custom_call" | custom-call | tf_op jit(solution)/shard_map/pallas_call | solution.py:212
  227.1 3.1 convolution_convert_fusion
  233.7 18.3 %shard_map.285 = bf16[512,128]{1,0:T(8,128)(2,1)} custom-call(s32[9]{0:T(128)} %convert_element_type.175.flags_ref, bf16[512,128]{1,0:T(8,128)(2,1)} %bitcast.105, bf16[9216,256]{1,0:T(8,128)(2,1)} %all-gather.5.cloned.1.call-done.kv_ref, s32[1,9216]{1,0:T(1,128)} %broadcast_in_dim_reshape.5.kcode_ref, s32[512,1]{1,0:T(8,128)} %copy.105.qlo_ref, ...), custom_call_target="tpu_custom_call" | custom-call | tf_op jit(solution)/shard_map/pallas_call | solution.py:212
  253.0 2.3 convolution_convert_fusion.1
  262.0 12.6 %collective-permute-done.5 = bf16[128,2560]{1,0:T(8,128)(2,1)S(1)} collective-permute-done((bf16[128,2560]{1,0:T(8,128)(2,1)S(1)}, bf16[128,2560]{1,0:T(8,128)(2,1)S(1)}, u32[]{:S(2)}, u32[]{:S(2)}) %collective-permute-start.5) | collective-permute-done | bytes 655392 | tf_op jit(solution)/shard_map/ppermute | solution.py:224
  274.8 13.9 %collective-permute-done.3 = bf16[128,2560]{1,0:T(8,128)(2,1)S(1)} collective-permute-done((bf16[128,2560]{1,0:T(8,128)(2,1)S(1)}, bf16[128,2560]{1,0:T(8,128)(2,1)S(1)}, u32[]{:S(2)}, u32[]{:S(2)}) %collective-permute-start.3) | collective-permute-done | bytes 655392 | tf_op jit(solution)/shard_map/ppermute | solution.py:224
  289.4 2.1 fusion.57
  291.5 24.7 %collective-permute-done.1 = bf16[256,2560]{1,0:T(8,128)(2,1)S(1)} collective-permute-done((bf16[256,2560]{1,0:T(8,128)(2,1)S(1)}, bf16[256,2560]{1,0:T(8,128)(2,1)S(1)}, u32[]{:S(2)}, u32[]{:S(2)}) %collective-permute-start.1) | collective-permute-done | bytes 1310752 | tf_op jit(solution)/shard_map/ppermute | solution.py:224
  316.9 2.1 fusion.58
  319.0 5.6 %all-reduce.2 = (f32[256]{0:T(256)S(1)}, f32[256]{0:T(256)S(1)}) all-reduce(f32[256]{0:T(256)S(1)} %get-tuple-element.68, f32[256]{0:T(256)S(1)} %get-tuple-element.70), channel_id=1, replica_groups=mesh['seq'=32,'vocab'=4] {'vocab'}, use_global_device_ids=true, to_apply=%region_26.27 | all-reduce | flops 512 | bytes 4096 | tf_op jit(solution)/shard_map/pmax | solution.py:405
  326.4 5.8 %all-reduce.1 = (f32[256]{0:T(256)S(1)}, f32[256]{0:T(256)S(1)}, f32[256]{0:T(256)S(1)}, f32[256]{0:T(256)S(1)}) all-reduce(f32[256]{0:T(256)S(1)} %get-tuple-element.45, f32[256]{0:T(256)S(1)} %get-tuple-element.46, f32[256]{0:T(256)S(1)} %get-tuple-element.17, ...), channel_id=1, replica_groups=mesh['seq'=32,'vocab'=4] {'vocab'}, use_global_device_ids=true, to_apply=%region_24.25 | all-reduce | flops 1024 | bytes 8192 | tf_op jit(solution)/shard_map/psum | solution.py:408
  333.2 3.3 collective-permute-done.6
  338.0 3.6 collective-permute-done.7
  341.9 3.3 collective-permute-done.8
  346.7 3.6 collective-permute-done.9
  350.3 1.9 collective-permute-start.10
  352.2 3.2 collective-permute-done.10
  (191 shorter events, 67.2 us)
Async XLA Ops:
  7.2 282.2 %copy-start = (bf16[2560,640]{1,0:T(8,128)(2,1)S(1)}, bf16[2560,640]{1,0:T(8,128)(2,1)}, u32[]{:S(2)}) copy-start(bf16[2560,640]{1,0:T(8,128)(2,1)} %param.57) | copy-start | bytes 9830404
  7.2 8.1 %copy-start.33 = (f32[2560]{0:T(1024)S(1)}, f32[2560]{0:T(1024)}, u32[]{:S(2)}) copy-start(f32[2560]{0:T(1024)} %param.49) | copy-start | bytes 30724
  7.2 115.9 %all-gather.3.cloned.1.call-start = ((), (), s32[]{:S(2)}) async-start(), calls=%async_computation | async-start | bytes 5406720 | tf_op jit(solution)/shard_map/all_gather | solution.py:339
  10.5 13.8 %copy-start.23 = (s32[4,1]{0,1:T(1,128)}, s32[4,1]{0,1:T(1,128)S(1)}, u32[]{:S(2)}) copy-start(s32[4,1]{0,1:T(1,128)S(1)} %reduce-window.8) | copy-start | bytes 52
  11.3 13.7 %copy-start.24 = (s32[4]{0:T(128)}, s32[4]{0:T(128)S(1)}, u32[]{:S(2)}) copy-start(s32[4]{0:T(128)S(1)} %bitcast_subtract_fusion) | copy-start | bytes 52
  23.6 7.9 %copy-start.12 = (bf16[256,128]{1,0:T(8,128)(2,1)S(1)}, bf16[256,128]{1,0:T(8,128)(2,1)}, u32[]{:S(2)}) copy-start(bf16[256,128]{1,0:T(8,128)(2,1)} %convolution_convert_fusion.3) | copy-start | bytes 196612
  33.0 174.7 %all-gather.5.cloned.1.call-start = ((), (), s32[]{:S(2)}) async-start(), calls=%async_computation.1 | async-start | bytes 4866048 | tf_op jit(solution)/shard_map/all_gather | solution.py:374
  62.4 63.8 %copy-start.13 = (s32[320]{0:T(512)S(1)}, s32[320]{0:T(512)}, u32[]{:S(2)}) copy-start(s32[320]{0:T(512)} %pad.21.clone) | copy-start | bytes 3844
  65.0 58.1 %copy-start.15 = (s32[128]{0:T(128)}, s32[128]{0:T(128)S(1)}, u32[]{:S(2)}) copy-start(s32[128]{0:T(128)S(1)} %get-tuple-element.51) | copy-start | bytes 1540
  65.0 58.1 %copy-start.17 = (s32[128]{0:T(128)}, s32[128]{0:T(128)S(1)}, u32[]{:S(2)}) copy-start(s32[128]{0:T(128)S(1)} %get-tuple-element.75) | copy-start | bytes 1540
  131.9 39.6 %copy-start.14 = (s32[128]{0:T(128)S(1)}, s32[128]{0:T(128)}, u32[]{:S(2)}) copy-start(s32[128]{0:T(128)} %get-tuple-element.52) | copy-start | bytes 1540
  131.9 39.6 %copy-start.16 = (s32[128]{0:T(128)S(1)}, s32[128]{0:T(128)}, u32[]{:S(2)}) copy-start(s32[128]{0:T(128)} %copy-done.15) | copy-start | bytes 1540
  131.9 39.6 %copy-start.18 = (s32[128]{0:T(128)S(1)}, s32[128]{0:T(128)}, u32[]{:S(2)}) copy-start(s32[128]{0:T(128)} %copy-done.17) | copy-start | bytes 1540
  230.2 25.2 %collective-permute-start.4 = (bf16[128,2560]{1,0:T(8,128)(2,1)}, bf16[128,2560]{1,0:T(8,128)(2,1)}, u32[]{:S(2)}, u32[]{:S(2)}) collective-permute-start(bf16[128,2560]{1,0:T(8,128)(2,1)} %convolution_convert_fusion), channel_id=1, source_target_pairs={{0,1},{1,0},{2,3},{3,2},{4,5},{5,4},{6,7},{7,6},{8,9},{9,8},{10,11... | collective-permute-start | bytes 1966088 | tf_op jit(solution)/shard_map/ppermute | solution.py:224
  232.6 27.0 %collective-permute-start = (bf16[256,2560]{1,0:T(8,128)(2,1)}, bf16[256,2560]{1,0:T(8,128)(2,1)}, u32[]{:S(2)}, u32[]{:S(2)}) collective-permute-start(bf16[256,2560]{1,0:T(8,128)(2,1)} %fusion.59), channel_id=1, source_target_pairs={{0,1},{1,0},{2,3},{3,2},{4,5},{5,4},{6,7},{7,6},{8,9},{9,8},{10,11... | collective-permute-start | bytes 3932168 | tf_op jit(solution)/shard_map/ppermute | solution.py:224
  255.3 2.4 collective-permute-start.2
  257.0 17.7 %collective-permute-start.5 = (bf16[128,2560]{1,0:T(8,128)(2,1)S(1)}, bf16[128,2560]{1,0:T(8,128)(2,1)S(1)}, u32[]{:S(2)}, u32[]{:S(2)}) collective-permute-start(bf16[128,2560]{1,0:T(8,128)(2,1)S(1)} %add_convert_fusion.3), channel_id=1, source_target_pairs={{0,2},{1,3},{2,0},{3,1},{4,6},{5,7},{6,4},{7,5},{8,10},{9,11},{10,... | collective-permute-start | bytes 1966088 | tf_op jit(solution)/shard_map/ppermute | solution.py:224
  257.9 30.8 %collective-permute-start.3 = (bf16[128,2560]{1,0:T(8,128)(2,1)S(1)}, bf16[128,2560]{1,0:T(8,128)(2,1)S(1)}, u32[]{:S(2)}, u32[]{:S(2)}) collective-permute-start(bf16[128,2560]{1,0:T(8,128)(2,1)S(1)} %add_convert_fusion.5), channel_id=1, source_target_pairs={{0,2},{1,3},{2,0},{3,1},{4,6},{5,7},{6,4},{7,5},{8,10},{9,11},{10,... | collective-permute-start | bytes 1966088 | tf_op jit(solution)/shard_map/ppermute | solution.py:224
  261.3 27.5 %copy-start.3 = (bf16[256,2560]{1,0:T(8,128)(2,1)S(1)}, bf16[256,2560]{1,0:T(8,128)(2,1)}, u32[]{:S(2)}) copy-start(bf16[256,2560]{1,0:T(8,128)(2,1)} %param.32) | copy-start | bytes 3932164
  261.3 54.9 %collective-permute-start.1 = (bf16[256,2560]{1,0:T(8,128)(2,1)S(1)}, bf16[256,2560]{1,0:T(8,128)(2,1)S(1)}, u32[]{:S(2)}, u32[]{:S(2)}) collective-permute-start(bf16[256,2560]{1,0:T(8,128)(2,1)S(1)} %add_convert_fusion.1), channel_id=1, source_target_pairs={{0,2},{1,3},{2,0},{3,1},{4,6},{5,7},{6,4},{7,5},{8,10},{9,11},{10,... | collective-permute-start | bytes 3932168 | tf_op jit(solution)/shard_map/ppermute | solution.py:224
  274.8 14.6 %copy-start.34 = (f32[2560]{0:T(1024)S(1)}, f32[2560]{0:T(1024)}, u32[]{:S(2)}) copy-start(f32[2560]{0:T(1024)} %param.56) | copy-start | bytes 30724
  289.4 26.8 %copy-start.5 = (bf16[256,2560]{1,0:T(8,128)(2,1)S(1)}, bf16[256,2560]{1,0:T(8,128)(2,1)}, u32[]{:S(2)}) copy-start(bf16[256,2560]{1,0:T(8,128)(2,1)} %param.31) | copy-start | bytes 3932164
  291.5 25.4 %copy-start.30 = (bf16[2560,640]{1,0:T(8,128)(2,1)S(1)}, bf16[2560,640]{1,0:T(8,128)(2,1)}, u32[]{:S(2)}) copy-start(bf16[2560,640]{1,0:T(8,128)(2,1)} %param.46) | copy-start | bytes 9830404
  291.5 25.4 %copy-start.35 = (f32[2560]{0:T(1024)S(1)}, f32[2560]{0:T(1024)}, u32[]{:S(2)}) copy-start(f32[2560]{0:T(1024)} %param.45) | copy-start | bytes 30724
  316.9 7.8 %copy-start.27 = (s32[256]{0:T(256)S(1)}, s32[256]{0:T(256)}, u32[]{:S(2)}) copy-start(s32[256]{0:T(256)} %param.33) | copy-start | bytes 3076
  316.9 15.3 %copy-start.19 = (s32[256]{0:T(256)S(1)}, s32[256]{0:T(256)}, u32[]{:S(2)}) copy-start(s32[256]{0:T(256)} %get-tuple-element.23) | copy-start | bytes 3076
  316.9 15.9 %copy-start.20 = (s32[256]{0:T(256)S(1)}, s32[256]{0:T(256)}, u32[]{:S(2)}) copy-start(s32[256]{0:T(256)} %get-tuple-element.22) | copy-start | bytes 3076
  332.9 3.6 %collective-permute-start.6 = (f32[4]{0:T(128)S(1)}, f32[4]{0:T(128)S(1)}, u32[]{:S(2)}, u32[]{:S(2)}) collective-permute-start(f32[4]{0:T(128)S(1)} %select_reduce_fusion.1), channel_id=1, source_target_pairs={{0,4},{4,0},{8,12},{12,8},{16,20},{20,16},{24,28},{28,24},{32,36},... | collective-permute-start | bytes 56 | tf_op jit(solution)/shard_map/ppermute | solution.py:419
  336.6 5.1 %collective-permute-start.7 = (f32[4]{0:T(128)S(1)}, f32[4]{0:T(128)S(1)}, u32[]{:S(2)}, u32[]{:S(2)}) collective-permute-start(f32[4]{0:T(128)S(1)} %add.306), channel_id=1, source_target_pairs={{0,8},{4,12},{8,0},{12,4},{16,24},{20,28},{24,16},{28,20},{32,40},... | collective-permute-start | bytes 56 | tf_op jit(solution)/shard_map/ppermute | solution.py:419
  341.6 3.6 collective-permute-start.8
  345.2 5.1 %collective-permute-start.9 = (f32[4]{0:T(128)S(1)}, f32[4]{0:T(128)S(1)}, u32[]{:S(2)}, u32[]{:S(2)}) collective-permute-start(f32[4]{0:T(128)S(1)} %add.308), channel_id=1, source_target_pairs={{0,32},{4,36},{8,40},{12,44},{16,48},{20,52},{24,56},{28,60},{32,0... | collective-permute-start | bytes 56 | tf_op jit(solution)/shard_map/ppermute | solution.py:419
  350.3 5.1 %collective-permute-start.10 = (f32[4]{0:T(128)S(1)}, f32[4]{0:T(128)S(1)}, u32[]{:S(2)}, u32[]{:S(2)}) collective-permute-start(f32[4]{0:T(128)S(1)} %add.309), channel_id=1, source_target_pairs={{0,64},{4,68},{8,72},{12,76},{16,80},{20,84},{24,88},{28,92},{32,9... | collective-permute-start | bytes 56 | tf_op jit(solution)/shard_map/ppermute | solution.py:419
  (17 other events, 74.0 us)
Sparse Core Ops, SparseCore 0:
  33.1 89.9 all-gather.2
  126.2 81.4 all-gather.4

commit v10 on v6

--- a/solution.py
+++ b/solution.py
@@ -395,12 +395,21 @@
     reference_logits, reference_max, reference_target = head_terms(
         reference_final, reference_head, targets, vocab_start
     )
-    policy_top, reference_top = lax.pmax((policy_max, reference_max), "vocab")
-    policy_local = jnp.sum(jnp.exp(policy_logits - policy_top[:, None]), axis=-1)
-    reference_local = jnp.sum(jnp.exp(reference_logits - reference_top[:, None]), axis=-1)
-    totals = lax.psum((policy_local, reference_local, policy_target, reference_target), "vocab")
-    policy_score = totals[2] - (policy_top + jnp.log(totals[0]))
-    reference_score = totals[3] - (reference_top + jnp.log(totals[1]))
+    policy_local = jnp.sum(jnp.exp(policy_logits - policy_max[:, None]), axis=-1)
+    reference_local = jnp.sum(jnp.exp(reference_logits - reference_max[:, None]), axis=-1)
+    terms = lax.all_gather(
+        jnp.stack(
+            [policy_max, reference_max, policy_local, reference_local, policy_target, reference_target]
+        ),
+        "vocab",
+        axis=0,
+    )
+    policy_top = jnp.max(terms[:, 0], axis=0)
+    reference_top = jnp.max(terms[:, 1], axis=0)
+    policy_total = jnp.sum(terms[:, 2] * jnp.exp(terms[:, 0] - policy_top[None]), axis=0)
+    reference_total = jnp.sum(terms[:, 3] * jnp.exp(terms[:, 1] - reference_top[None]), axis=0)
+    policy_score = jnp.sum(terms[:, 4], axis=0) - (policy_top + jnp.log(policy_total))
+    reference_score = jnp.sum(terms[:, 5], axis=0) - (reference_top + jnp.log(reference_total))
     token_diff = policy_score - reference_score
     per_token = token_diff / length_of.astype(jnp.float32)
     partial_sums = jnp.sum(

time: 339 us -> 331 us (0.976)
  blocking collectives: 11.4 us -> 5.19 us
    pmax x1 -> x0, blocking collectives: 5.73 us -> none  [local(): policy_top, reference_top = lax.pmax((policy_max, reference_max), 'vocab')]
    psum x1 -> x0, blocking collectives: 5.67 us -> none  [local(): lax.psum((policy_local, reference_local, policy_target, reference_target)...]
    all_gather x0 -> x1, blocking collectives: none -> 5.19 us  [local(): lax.all_gather(jnp.stack([policy_max, reference_max, policy_local, refere...]
  transfers between devices with their start and end apart: 10 -> 10, of which waited for: 10 -> 10; matrix products, arithmetic and copies ran while one was open for 22% -> 23% of each run, Pallas kernels for 22% -> 22%
where the time goes in v10:
time: 331 us; the launch traced here: 329 us
  waiting for transfers between devices  115 us (35%)
  Pallas kernels  72.6 us (22%)
  other arithmetic  52.7 us (16%)
  local copies, waits for them, and re-layouts  28.9 us (9%)
  matrix products  28.1 us (8%)
  between operations  14.3 us (4%)
  starting transfers between devices  12.5 us (4%)
  blocking collectives  5.19 us (2%)
    pallas_call x2, Pallas kernels, flash_attend(): pl.pallas_call(flash_kernel, grid_spec=grid_spec, out_shape=jax.ShapeDtyp...  72.6 us
    all_gather x1, waiting for transfers between devices, local(): lax.all_gather(jnp.concatenate([policy_stack, carrier], axis=0), 'seq', a...  56.6 us
    ppermute x2, waiting for transfers between devices, exchange_sum(): lax.ppermute(values, axis_name, [(i, i ^ stride) for i in range(count)])  30.1 us
    all_gather x1, waiting for transfers between devices, local(): lax.all_gather(reference_stack, 'seq', axis=0, tiled=True)  12.7 us
    ppermute x5, starting transfers between devices, local(): lax.ppermute(rollout_mean, 'seq', [(i, i ^ stride) for i in range(seq_cou...  11.9 us
    reduce_sum x6, other arithmetic, rms_scale(): jnp.mean(values * values, axis=-1, keepdims=True) + EPSILON  10.8 us
    ppermute x5, waiting for transfers between devices, local(): lax.ppermute(rollout_mean, 'seq', [(i, i ^ stride) for i in range(seq_cou...  10.6 us
    reshape x4, local copies, waits for them, and re-layouts, project(): jnp.dot(normed, query_weight, preferred_element_type=jnp.float32)  8.09 us
  transfers between devices with their start and end apart: 10, of which 10 were waited for; matrix products, arithmetic and copies ran while one was open for 23% of the time, Pallas kernels for 22%

profile of v10, /device:TPU:0, one launch (start us, length us, event | category | flops | bytes accessed | tf_op | source)
XLA Modules:
  0.0 328.8 jit_solution(5623736084536985504)
XLA Ops:
  16.1 2.8 convolution_convert_fusion.2
  18.9 2.6 multiply_reduce_fusion.5
  31.4 2.1 convolution_convert_fusion.1
  35.0 3.9 %fusion.55 = f32[256,512]{1,0:T(8,128)} fusion(bf16[2560,512]{1,0:T(8,128)(2,1)} %param.50, bf16[256,2560]{1,0:T(8,128)(2,1)} %param.32, f32[2560]{0:T(1024)} %param.49, f32[256]{0:T(256)} %copy-done.28), kind=kOutput, calls=%fused_computation.157 | convolution fusion | flops 673710080 | bytes 4467712 | tf_op jit(solution)/shard_map/dot_general | solution.py:56
  38.9 2.0 reshape.564
  42.9 4.0 %fusion.57 = f32[256,512]{1,0:T(8,128)} fusion(bf16[2560,512]{1,0:T(8,128)(2,1)} %param.39, bf16[256,2560]{1,0:T(8,128)(2,1)} %param.31, f32[2560]{0:T(1024)} %param.38, f32[256]{0:T(256)S(1)} %copy-done.27), kind=kOutput, calls=%fused_computation.158 | convolution fusion | flops 673710080 | bytes 4467712 | tf_op jit(solution)/shard_map/dot_general | solution.py:56
  46.9 2.0 reshape.559
  61.8 3.1 fusion.50
  64.9 56.6 %all-gather.5.cloned.1.call-done.kv_ref = bf16[10240,256]{1,0:T(8,128)(2,1)} async-done(((bf16[320,256]{1,0:T(8,128)(2,1)}), bf16[10240,256]{1,0:T(8,128)(2,1)}) %all-gather.5.cloned.1.call-update) | async-done | bytes 5242896 | tf_op jit(solution)/shard_map/all_gather | solution.py:339
  139.2 3.7 %and_reduce_fusion = pred[10]{0:T(512)(128)(4,1)S(1)} fusion(s32[10,1024]{1,0:T(8,128)} %ge.64, s32[256]{0:T(256)} %copy-done.18, s32[256]{0:T(256)} %copy-done.19), kind=kLoop, calls=%fused_computation | loop fusion | flops 10485750 | bytes 43018 | tf_op jit(solution)/shard_map/reduce_or | solution.py:232
  143.4 38.1 %shard_map.284 = bf16[1024,128]{1,0:T(8,128)(2,1)} custom-call(s32[10]{0:T(128)} %convert_element_type.132.flags_ref, bf16[1024,128]{1,0:T(8,128)(2,1)} %bitcast.121, bf16[10240,256]{1,0:T(8,128)(2,1)} %all-gather.5.cloned.1.call-done.kv_ref, s32[1,10240]{1,0:T(1,128)} %broadcast_in_dim_reshape.4.kcode_ref, s32[1024,1]{1,0:T(8,128)} %bitcast.117, ...), custom_call_target="tpu_custom_call" | custom-call | tf_op jit(solution)/shard_map/pallas_call | solution.py:212
  183.3 3.8 %convolution_convert_fusion = bf16[256,2560]{1,0:T(8,128)(2,1)} fusion(bf16[256,512]{0,1:T(8,128)(2,1)} %bitcast.125, bf16[512,2560]{1,0:T(8,128)(2,1)} %param.44), kind=kOutput, calls=%fused_computation.8 | convolution fusion | flops 671744000 | bytes 4194304 | tf_op jit(solution)/shard_map/dot_general | solution.py:243
  189.5 3.3 %and_reduce_fusion.1 = pred[9]{0:T(512)(128)(4,1)S(1)} fusion(s32[9,1024]{1,0:T(8,128)S(1)} %ge.68, s32[256]{0:T(256)} %copy-done.18, s32[256]{0:T(256)} %copy-done.19), kind=kLoop, calls=%fused_computation.1 | loop fusion | flops 9437175 | bytes 38921 | tf_op jit(solution)/shard_map/reduce_or | solution.py:232
  193.3 12.7 %all-gather.7.cloned.1.call-done.kv_ref = bf16[9216,256]{1,0:T(8,128)(2,1)} async-done(((bf16[288,256]{1,0:T(8,128)(2,1)}), bf16[9216,256]{1,0:T(8,128)(2,1)}) %all-gather.7.cloned.1.call-update) | async-done | bytes 4718608 | tf_op jit(solution)/shard_map/all_gather | solution.py:374
  206.0 34.6 %shard_map.285 = bf16[1024,128]{1,0:T(8,128)(2,1)} custom-call(s32[9]{0:T(128)} %convert_element_type.135.flags_ref, bf16[1024,128]{1,0:T(8,128)(2,1)} %bitcast.122, bf16[9216,256]{1,0:T(8,128)(2,1)} %all-gather.7.cloned.1.call-done.kv_ref, s32[1,9216]{1,0:T(1,128)} %broadcast_in_dim_reshape.5.kcode_ref, s32[1024,1]{1,0:T(8,128)} %bitcast.118, ...), custom_call_target="tpu_custom_call" | custom-call | tf_op jit(solution)/shard_map/pallas_call | solution.py:212
  241.7 3.7 %fusion.65 = bf16[256,2560]{1,0:T(8,128)(2,1)} fusion(bf16[256,512]{0,1:T(8,128)(2,1)S(1)} %bitcast.126, bf16[512,2560]{1,0:T(8,128)(2,1)} %param.55), kind=kOutput, calls=%fused_computation.163 | convolution fusion | flops 671088640 | bytes 4194304 | tf_op jit(solution)/shard_map/dot_general | solution.py:243
  245.4 4.5 %all-reduce.3.cloned.1.call-done = bf16[256,2560]{1,0:T(8,128)(2,1)} async-done(((bf16[256,2560]{1,0:T(8,128)(2,1)}), bf16[256,2560]{1,0:T(8,128)(2,1)}) %all-reduce.3.cloned.1.call-update) | async-done | bytes 1310736 | tf_op jit(solution)/shard_map/psum | solution.py:381
  250.2 3.0 collective-permute-done
  253.2 2.8 add_convert_fusion.1
  256.2 2.4 multiply_reduce_fusion.1
  260.1 27.1 %collective-permute-done.1 = bf16[256,2560]{1,0:T(8,128)(2,1)} collective-permute-done((bf16[256,2560]{1,0:T(8,128)(2,1)}, bf16[256,2560]{1,0:T(8,128)(2,1)}, u32[]{:S(2)}, u32[]{:S(2)}) %collective-permute-start.1) | collective-permute-done | bytes 1310752 | tf_op jit(solution)/shard_map/ppermute | solution.py:224
  287.2 2.4 multiply_reduce_fusion
  289.6 3.2 fusion.64
  293.3 5.2 %all-gather.1 = f32[4,6,256]{2,1,0:T(8,128)S(1)} all-gather(f32[1,6,256]{2,1,0:T(8,128)S(1)} %bitcast.128), channel_id=2, replica_groups=mesh['seq'=32,'vocab'=4] {'vocab'}, dimensions={0}, use_global_device_ids=true | all-gather | bytes 30720 | tf_op jit(solution)/shard_map/all_gather | solution.py:400
  300.9 2.1 collective-permute-done.2
  303.0 3.0 collective-permute-start.3
  306.0 2.1 collective-permute-done.3
  309.5 2.1 collective-permute-done.4
  311.6 3.0 collective-permute-start.5
  314.6 2.1 collective-permute-done.5
  316.7 2.9 collective-permute-start.6
  319.5 2.2 collective-permute-done.6
  (171 shorter events, 65.6 us)
Async XLA Ops:
  7.2 251.4 %copy-start = (bf16[2560,640]{1,0:T(8,128)(2,1)S(1)}, bf16[2560,640]{1,0:T(8,128)(2,1)}, u32[]{:S(2)}) copy-start(bf16[2560,640]{1,0:T(8,128)(2,1)} %param.46) | copy-start | bytes 9830404
  7.2 8.0 %copy-start.34 = (f32[2560]{0:T(1024)S(1)}, f32[2560]{0:T(1024)}, u32[]{:S(2)}) copy-start(f32[2560]{0:T(1024)} %param.49) | copy-start | bytes 30724
  7.2 114.3 %all-gather.5.cloned.1.call-start = ((), (), s32[]{:S(2)}) async-start(), calls=%async_computation | async-start | bytes 5406720 | tf_op jit(solution)/shard_map/all_gather | solution.py:339
  10.5 12.7 %copy-start.25 = (s32[4,1]{0,1:T(1,128)}, s32[4,1]{0,1:T(1,128)S(1)}, u32[]{:S(2)}) copy-start(s32[4,1]{0,1:T(1,128)S(1)} %reduce-window.8) | copy-start | bytes 52
  10.5 4.7 %copy-start.3 = (bf16[256,2560]{1,0:T(8,128)(2,1)S(1)}, bf16[256,2560]{1,0:T(8,128)(2,1)}, u32[]{:S(2)}) copy-start(bf16[256,2560]{1,0:T(8,128)(2,1)} %param.32) | copy-start | bytes 3932164
  10.5 4.7 %copy-start.32 = (bf16[2560,128]{1,0:T(8,128)(2,1)S(1)}, bf16[2560,128]{1,0:T(8,128)(2,1)}, u32[]{:S(2)}) copy-start(bf16[2560,128]{1,0:T(8,128)(2,1)} %param.51) | copy-start | bytes 1966084
  11.3 12.7 %copy-start.26 = (s32[4]{0:T(128)}, s32[4]{0:T(128)S(1)}, u32[]{:S(2)}) copy-start(s32[4]{0:T(128)S(1)} %bitcast_subtract_fusion.1) | copy-start | bytes 52
  16.1 10.0 %copy-start.22 = (f32[128]{0:T(128)S(1)}, f32[128]{0:T(128)}, u32[]{:S(2)}) copy-start(f32[128]{0:T(128)} %param.54) | copy-start | bytes 1540
  22.5 7.4 %copy-start.17 = (bf16[256,128]{1,0:T(8,128)(2,1)S(1)}, bf16[256,128]{1,0:T(8,128)(2,1)}, u32[]{:S(2)}) copy-start(bf16[256,128]{1,0:T(8,128)(2,1)} %convolution_convert_fusion.2) | copy-start | bytes 196612
  26.1 32.1 %copy-start.18 = (s32[256]{0:T(256)}, s32[256]{0:T(256)S(1)}, u32[]{:S(2)}) copy-start(s32[256]{0:T(256)S(1)} %get-tuple-element.49) | copy-start | bytes 3076
  26.1 32.1 %copy-start.19 = (s32[256]{0:T(256)}, s32[256]{0:T(256)S(1)}, u32[]{:S(2)}) copy-start(s32[256]{0:T(256)S(1)} %get-tuple-element.53) | copy-start | bytes 3076
  31.4 174.7 %all-gather.7.cloned.1.call-start = ((), (), s32[]{:S(2)}) async-start(), calls=%async_computation.2 | async-start | bytes 4866048 | tf_op jit(solution)/shard_map/all_gather | solution.py:374
  34.9 8.0 %copy-start.27 = (f32[256]{0:T(256)S(1)}, f32[256]{0:T(256)}, u32[]{:S(2)}) copy-start(f32[256]{0:T(256)} %add_rsqrt_fusion.7) | copy-start | bytes 3076
  34.9 215.0 %all-reduce.3.cloned.1.call-start = ((), (), s32[]{:S(2)}) async-start(), calls=%async_computation.1 | async-start | bytes 2621440 | tf_op jit(solution)/shard_map/psum | solution.py:381
  42.9 8.7 %copy-start.11 = (f32[256,64]{1,0:T(8,128)S(1)}, f32[256,64]{1,0:T(8,128)}, u32[]{:S(2)}) copy-start(f32[256,64]{1,0:T(8,128)} %copy-done.10) | copy-start | bytes 196612
  42.9 8.7 %copy-start.13 = (f32[256,64]{1,0:T(8,128)S(1)}, f32[256,64]{1,0:T(8,128)}, u32[]{:S(2)}) copy-start(f32[256,64]{1,0:T(8,128)} %copy-done.12) | copy-start | bytes 196612
  46.9 7.7 %copy-start.23 = (f32[128]{0:T(128)S(1)}, f32[128]{0:T(128)}, u32[]{:S(2)}) copy-start(f32[128]{0:T(128)} %param.53) | copy-start | bytes 1540
  46.9 8.1 %copy-start.24 = (f32[128]{0:T(128)S(1)}, f32[128]{0:T(128)}, u32[]{:S(2)}) copy-start(f32[128]{0:T(128)} %param.42) | copy-start | bytes 1540
  50.9 4.1 %copy-start.6 = (f32[256,4,128]{2,1,0:T(4,128)S(1)}, f32[256,4,128]{2,1,0:T(4,128)}, u32[]{:S(2)}) copy-start(f32[256,4,128]{2,1,0:T(4,128)} %reshape.559) | copy-start | bytes 1572868
  245.4 13.2 %copy-start.35 = (f32[2560]{0:T(1024)S(1)}, f32[2560]{0:T(1024)}, u32[]{:S(2)}) copy-start(f32[2560]{0:T(1024)} %param.45) | copy-start | bytes 30724
  249.9 3.2 collective-permute-start
  256.0 31.2 %collective-permute-start.1 = (bf16[256,2560]{1,0:T(8,128)(2,1)}, bf16[256,2560]{1,0:T(8,128)(2,1)}, u32[]{:S(2)}, u32[]{:S(2)}) collective-permute-start(bf16[256,2560]{1,0:T(8,128)(2,1)} %add_convert_fusion.1), channel_id=1, source_target_pairs={{0,2},{1,3},{2,0},{3,1},{4,6},{5,7},{6,4},{7,5},{8,10},{9,11},{10,... | collective-permute-start | bytes 3932168 | tf_op jit(solution)/shard_map/ppermute | solution.py:224
  258.7 28.5 %copy-start.4 = (bf16[256,2560]{1,0:T(8,128)(2,1)S(1)}, bf16[256,2560]{1,0:T(8,128)(2,1)}, u32[]{:S(2)}) copy-start(bf16[256,2560]{1,0:T(8,128)(2,1)} %param.32) | copy-start | bytes 3932164
  260.1 29.5 %copy-start.31 = (bf16[2560,640]{1,0:T(8,128)(2,1)S(1)}, bf16[2560,640]{1,0:T(8,128)(2,1)}, u32[]{:S(2)}) copy-start(bf16[2560,640]{1,0:T(8,128)(2,1)} %param.57) | copy-start | bytes 9830404
  260.1 29.5 %copy-start.36 = (f32[2560]{0:T(1024)S(1)}, f32[2560]{0:T(1024)}, u32[]{:S(2)}) copy-start(f32[2560]{0:T(1024)} %param.56) | copy-start | bytes 30724
  289.6 9.0 %copy-start.20 = (s32[256]{0:T(256)S(1)}, s32[256]{0:T(256)}, u32[]{:S(2)}) copy-start(s32[256]{0:T(256)} %get-tuple-element.29) | copy-start | bytes 3076
  289.6 9.6 %copy-start.21 = (s32[256]{0:T(256)S(1)}, s32[256]{0:T(256)}, u32[]{:S(2)}) copy-start(s32[256]{0:T(256)} %get-tuple-element.28) | copy-start | bytes 3076
  299.3 3.6 %collective-permute-start.2 = (f32[4]{0:T(128)S(1)}, f32[4]{0:T(128)S(1)}, u32[]{:S(2)}, u32[]{:S(2)}) collective-permute-start(f32[4]{0:T(128)S(1)} %select_reduce_fusion.1), channel_id=1, source_target_pairs={{0,4},{4,0},{8,12},{12,8},{16,20},{20,16},{24,28},{28,24},{32,36},... | collective-permute-start | bytes 56 | tf_op jit(solution)/shard_map/ppermute | solution.py:421
  303.0 5.1 %collective-permute-start.3 = (f32[4]{0:T(128)S(1)}, f32[4]{0:T(128)S(1)}, u32[]{:S(2)}, u32[]{:S(2)}) collective-permute-start(f32[4]{0:T(128)S(1)} %add.299), channel_id=1, source_target_pairs={{0,8},{4,12},{8,0},{12,4},{16,24},{20,28},{24,16},{28,20},{32,40},... | collective-permute-start | bytes 56 | tf_op jit(solution)/shard_map/ppermute | solution.py:421
  308.0 3.6 %collective-permute-start.4 = (f32[4]{0:T(128)S(1)}, f32[4]{0:T(128)S(1)}, u32[]{:S(2)}, u32[]{:S(2)}) collective-permute-start(f32[4]{0:T(128)S(1)} %add.300), channel_id=1, source_target_pairs={{0,16},{4,20},{8,24},{12,28},{16,0},{20,4},{24,8},{28,12},{32,48},... | collective-permute-start | bytes 56 | tf_op jit(solution)/shard_map/ppermute | solution.py:421
  311.6 5.1 %collective-permute-start.5 = (f32[4]{0:T(128)S(1)}, f32[4]{0:T(128)S(1)}, u32[]{:S(2)}, u32[]{:S(2)}) collective-permute-start(f32[4]{0:T(128)S(1)} %add.301), channel_id=1, source_target_pairs={{0,32},{4,36},{8,40},{12,44},{16,48},{20,52},{24,56},{28,60},{32,0... | collective-permute-start | bytes 56 | tf_op jit(solution)/shard_map/ppermute | solution.py:421
  316.7 5.1 %collective-permute-start.6 = (f32[4]{0:T(128)S(1)}, f32[4]{0:T(128)S(1)}, u32[]{:S(2)}, u32[]{:S(2)}) collective-permute-start(f32[4]{0:T(128)S(1)} %add.302), channel_id=1, source_target_pairs={{0,64},{4,68},{8,72},{12,76},{16,80},{20,84},{24,88},{28,92},{32,9... | collective-permute-start | bytes 56 | tf_op jit(solution)/shard_map/ppermute | solution.py:421
  (15 other events, 29.2 us)
Sparse Core Ops, SparseCore 0:
  31.5 89.9 all-gather.4
  124.5 81.4 all-gather.6
  208.6 41.3 all-reduce.2

commit v11 on v10

--- a/solution.py
+++ b/solution.py
@@ -418,10 +418,22 @@
     rollout_mean = partial_sums
     stride = 1
     while stride < seq_count:
-        rollout_mean = rollout_mean + lax.ppermute(
-            rollout_mean, "seq", [(i, i ^ stride) for i in range(seq_count)]
-        )
-        stride *= 2
+        radix = 4 if seq_count % (stride * 4) == 0 else 2
+        digit = (lax.axis_index("seq") // stride) % radix
+        slots = [jnp.where(digit == k, rollout_mean, 0.0) for k in range(radix)]
+        for offset in range(1, radix):
+            pairs = [
+                (i, i + (((i // stride) % radix + offset) % radix - (i // stride) % radix) * stride)
+                for i in range(seq_count)
+            ]
+            received = lax.ppermute(rollout_mean, "seq", pairs)
+            source = (digit - offset) % radix
+            slots = [slots[k] + jnp.where(source == k, received, 0.0) for k in range(radix)]
+        if radix == 4:
+            rollout_mean = (slots[0] + slots[1]) + (slots[2] + slots[3])
+        else:
+            rollout_mean = slots[0] + slots[1]
+        stride *= radix
     return (token_diff, rollout_mean)
 
 

time: 331 us -> 330 us (level)
    ppermute x5 -> x7, waiting for transfers between devices: 10.6 us -> 10 us  [local(): received = lax.ppermute(rollout_mean, 'seq', pairs)]
    ppermute x5 -> x7, starting transfers between devices: 11.9 us -> 11.9 us  [local(): received = lax.ppermute(rollout_mean, 'seq', pairs)]
  transfers between devices with their start and end apart: 10 -> 12, of which waited for: 10 -> 10; matrix products, arithmetic and copies ran while one was open for 23% -> 23% of each run, Pallas kernels for 22% -> 22%
where the time goes in v11:
time: 330 us; the launch traced here: 328 us
  waiting for transfers between devices  114 us (35%)
  Pallas kernels  72.6 us (22%)
  other arithmetic  52.7 us (16%)
  local copies, waits for them, and re-layouts  28.9 us (9%)
  matrix products  28.1 us (9%)
  between operations  14.3 us (4%)
  starting transfers between devices  12.5 us (4%)
  blocking collectives  5.19 us (2%)
    pallas_call x2, Pallas kernels, flash_attend(): pl.pallas_call(flash_kernel, grid_spec=grid_spec, out_shape=jax.ShapeDtyp...  72.6 us
    all_gather x1, waiting for transfers between devices, local(): lax.all_gather(jnp.concatenate([policy_stack, carrier], axis=0), 'seq', a...  56.6 us
    ppermute x2, waiting for transfers between devices, exchange_sum(): lax.ppermute(values, axis_name, [(i, i ^ stride) for i in range(count)])  30.1 us
    all_gather x1, waiting for transfers between devices, local(): lax.all_gather(reference_stack, 'seq', axis=0, tiled=True)  12.7 us
    ppermute x7, starting transfers between devices, local(): received = lax.ppermute(rollout_mean, 'seq', pairs)  11.9 us
    reduce_sum x6, other arithmetic, rms_scale(): jnp.mean(values * values, axis=-1, keepdims=True) + EPSILON  10.8 us
    ppermute x7, waiting for transfers between devices, local(): received = lax.ppermute(rollout_mean, 'seq', pairs)  10 us
    reshape x4, local copies, waits for them, and re-layouts, project(): jnp.dot(normed, query_weight, preferred_element_type=jnp.float32)  8.09 us
  transfers between devices with their start and end apart: 12, of which 10 were waited for; matrix products, arithmetic and copies ran while one was open for 23% of the time, Pallas kernels for 22%

profile of v11, /device:TPU:0, one launch (start us, length us, event | category | flops | bytes accessed | tf_op | source)
XLA Modules:
  0.0 328.3 jit_solution(621056799523671615)
XLA Ops:
  16.1 2.8 convolution_convert_fusion.2
  18.9 2.6 multiply_reduce_fusion.5
  31.4 2.1 convolution_convert_fusion.1
  35.0 3.9 %fusion.82 = f32[256,512]{1,0:T(8,128)} fusion(bf16[2560,512]{1,0:T(8,128)(2,1)} %param.50, bf16[256,2560]{1,0:T(8,128)(2,1)} %param.32, f32[2560]{0:T(1024)} %param.49, f32[256]{0:T(256)} %copy-done.28), kind=kOutput, calls=%fused_computation.222 | convolution fusion | flops 673710080 | bytes 4467712 | tf_op jit(solution)/shard_map/dot_general | solution.py:56
  38.9 2.0 reshape.564
  40.9 2.0 reshape.563
  42.9 4.0 %fusion.84 = f32[256,512]{1,0:T(8,128)} fusion(bf16[2560,512]{1,0:T(8,128)(2,1)} %param.39, bf16[256,2560]{1,0:T(8,128)(2,1)} %param.31, f32[2560]{0:T(1024)} %param.38, f32[256]{0:T(256)S(1)} %copy-done.27), kind=kOutput, calls=%fused_computation.223 | convolution fusion | flops 673710080 | bytes 4467712 | tf_op jit(solution)/shard_map/dot_general | solution.py:56
  46.9 2.0 reshape.559
  48.9 2.0 reshape.558
  61.8 3.1 fusion.77
  64.9 56.6 %all-gather.5.cloned.1.call-done.kv_ref = bf16[10240,256]{1,0:T(8,128)(2,1)} async-done(((bf16[320,256]{1,0:T(8,128)(2,1)}), bf16[10240,256]{1,0:T(8,128)(2,1)}) %all-gather.5.cloned.1.call-update) | async-done | bytes 5242896 | tf_op jit(solution)/shard_map/all_gather | solution.py:339
  139.2 3.7 %and_reduce_fusion = pred[10]{0:T(512)(128)(4,1)S(1)} fusion(s32[10,1024]{1,0:T(8,128)} %ge.64, s32[256]{0:T(256)} %copy-done.18, s32[256]{0:T(256)} %copy-done.19), kind=kLoop, calls=%fused_computation | loop fusion | flops 10485750 | bytes 43018 | tf_op jit(solution)/shard_map/reduce_or | solution.py:232
  143.4 38.1 %shard_map.284 = bf16[1024,128]{1,0:T(8,128)(2,1)} custom-call(s32[10]{0:T(128)} %convert_element_type.132.flags_ref, bf16[1024,128]{1,0:T(8,128)(2,1)} %bitcast.121, bf16[10240,256]{1,0:T(8,128)(2,1)} %all-gather.5.cloned.1.call-done.kv_ref, s32[1,10240]{1,0:T(1,128)} %broadcast_in_dim_reshape.4.kcode_ref, s32[1024,1]{1,0:T(8,128)} %bitcast.117, ...), custom_call_target="tpu_custom_call" | custom-call | tf_op jit(solution)/shard_map/pallas_call | solution.py:212
  183.3 3.8 %convolution_convert_fusion = bf16[256,2560]{1,0:T(8,128)(2,1)} fusion(bf16[256,512]{0,1:T(8,128)(2,1)} %bitcast.125, bf16[512,2560]{1,0:T(8,128)(2,1)} %param.44), kind=kOutput, calls=%fused_computation.8 | convolution fusion | flops 671744000 | bytes 4194304 | tf_op jit(solution)/shard_map/dot_general | solution.py:243
  189.5 3.3 %and_reduce_fusion.1 = pred[9]{0:T(512)(128)(4,1)S(1)} fusion(s32[9,1024]{1,0:T(8,128)S(1)} %ge.68, s32[256]{0:T(256)} %copy-done.18, s32[256]{0:T(256)} %copy-done.19), kind=kLoop, calls=%fused_computation.1 | loop fusion | flops 9437175 | bytes 38921 | tf_op jit(solution)/shard_map/reduce_or | solution.py:232
  193.3 12.7 %all-gather.7.cloned.1.call-done.kv_ref = bf16[9216,256]{1,0:T(8,128)(2,1)} async-done(((bf16[288,256]{1,0:T(8,128)(2,1)}), bf16[9216,256]{1,0:T(8,128)(2,1)}) %all-gather.7.cloned.1.call-update) | async-done | bytes 4718608 | tf_op jit(solution)/shard_map/all_gather | solution.py:374
  206.0 34.6 %shard_map.285 = bf16[1024,128]{1,0:T(8,128)(2,1)} custom-call(s32[9]{0:T(128)} %convert_element_type.135.flags_ref, bf16[1024,128]{1,0:T(8,128)(2,1)} %bitcast.122, bf16[9216,256]{1,0:T(8,128)(2,1)} %all-gather.7.cloned.1.call-done.kv_ref, s32[1,9216]{1,0:T(1,128)} %broadcast_in_dim_reshape.5.kcode_ref, s32[1024,1]{1,0:T(8,128)} %bitcast.118, ...), custom_call_target="tpu_custom_call" | custom-call | tf_op jit(solution)/shard_map/pallas_call | solution.py:212
  241.7 3.7 %fusion.92 = bf16[256,2560]{1,0:T(8,128)(2,1)} fusion(bf16[256,512]{0,1:T(8,128)(2,1)S(1)} %bitcast.126, bf16[512,2560]{1,0:T(8,128)(2,1)} %param.55), kind=kOutput, calls=%fused_computation.228 | convolution fusion | flops 671088640 | bytes 4194304 | tf_op jit(solution)/shard_map/dot_general | solution.py:243
  245.4 4.5 %all-reduce.3.cloned.1.call-done = bf16[256,2560]{1,0:T(8,128)(2,1)} async-done(((bf16[256,2560]{1,0:T(8,128)(2,1)}), bf16[256,2560]{1,0:T(8,128)(2,1)}) %all-reduce.3.cloned.1.call-update) | async-done | bytes 1310736 | tf_op jit(solution)/shard_map/psum | solution.py:381
  250.2 3.0 collective-permute-done
  253.2 2.8 add_convert_fusion.1
  256.2 2.4 multiply_reduce_fusion.1
  260.1 27.1 %collective-permute-done.1 = bf16[256,2560]{1,0:T(8,128)(2,1)} collective-permute-done((bf16[256,2560]{1,0:T(8,128)(2,1)}, bf16[256,2560]{1,0:T(8,128)(2,1)}, u32[]{:S(2)}, u32[]{:S(2)}) %collective-permute-start.1) | collective-permute-done | bytes 1310752 | tf_op jit(solution)/shard_map/ppermute | solution.py:224
  287.2 2.4 multiply_reduce_fusion
  289.6 3.2 fusion.91
  293.3 5.2 %all-gather.1 = f32[4,6,256]{2,1,0:T(8,128)S(1)} all-gather(f32[1,6,256]{2,1,0:T(8,128)S(1)} %bitcast.128), channel_id=2, replica_groups=mesh['seq'=32,'vocab'=4] {'vocab'}, dimensions={0}, use_global_device_ids=true | all-gather | bytes 30720 | tf_op jit(solution)/shard_map/all_gather | solution.py:400
  299.3 2.8 collective-permute-start.4
  303.8 3.4 %collective-permute-done.3 = f32[4]{0:T(128)S(1)} collective-permute-done((f32[4]{0:T(128)S(1)}, f32[4]{0:T(128)S(1)}, u32[]{:S(2)}, u32[]{:S(2)}) %collective-permute-start.3) | collective-permute-done | bytes 48 | tf_op jit(solution)/shard_map/ppermute | solution.py:429
  307.7 2.8 collective-permute-start.7
  312.2 3.4 %collective-permute-done.6 = f32[4]{0:T(128)S(1)} collective-permute-done((f32[4]{0:T(128)S(1)}, f32[4]{0:T(128)S(1)}, u32[]{:S(2)}, u32[]{:S(2)}) %collective-permute-start.6) | collective-permute-done | bytes 48 | tf_op jit(solution)/shard_map/ppermute | solution.py:429
  316.1 2.9 collective-permute-start.8
  319.1 2.2 collective-permute-done.8
  (173 shorter events, 63.0 us)
Async XLA Ops:
  7.2 251.4 %copy-start = (bf16[2560,640]{1,0:T(8,128)(2,1)S(1)}, bf16[2560,640]{1,0:T(8,128)(2,1)}, u32[]{:S(2)}) copy-start(bf16[2560,640]{1,0:T(8,128)(2,1)} %param.46) | copy-start | bytes 9830404
  7.2 8.0 %copy-start.34 = (f32[2560]{0:T(1024)S(1)}, f32[2560]{0:T(1024)}, u32[]{:S(2)}) copy-start(f32[2560]{0:T(1024)} %param.49) | copy-start | bytes 30724
  7.2 114.3 %all-gather.5.cloned.1.call-start = ((), (), s32[]{:S(2)}) async-start(), calls=%async_computation | async-start | bytes 5406720 | tf_op jit(solution)/shard_map/all_gather | solution.py:339
  10.5 12.7 %copy-start.25 = (s32[4,1]{0,1:T(1,128)}, s32[4,1]{0,1:T(1,128)S(1)}, u32[]{:S(2)}) copy-start(s32[4,1]{0,1:T(1,128)S(1)} %reduce-window.8) | copy-start | bytes 52
  10.5 4.7 %copy-start.32 = (bf16[2560,128]{1,0:T(8,128)(2,1)S(1)}, bf16[2560,128]{1,0:T(8,128)(2,1)}, u32[]{:S(2)}) copy-start(bf16[2560,128]{1,0:T(8,128)(2,1)} %param.51) | copy-start | bytes 1966084
  11.3 12.7 %copy-start.26 = (s32[4]{0:T(128)}, s32[4]{0:T(128)S(1)}, u32[]{:S(2)}) copy-start(s32[4]{0:T(128)S(1)} %bitcast_subtract_fusion.1) | copy-start | bytes 52
  16.1 10.0 %copy-start.22 = (f32[128]{0:T(128)S(1)}, f32[128]{0:T(128)}, u32[]{:S(2)}) copy-start(f32[128]{0:T(128)} %param.54) | copy-start | bytes 1540
  22.5 7.4 %copy-start.17 = (bf16[256,128]{1,0:T(8,128)(2,1)S(1)}, bf16[256,128]{1,0:T(8,128)(2,1)}, u32[]{:S(2)}) copy-start(bf16[256,128]{1,0:T(8,128)(2,1)} %convolution_convert_fusion.2) | copy-start | bytes 196612
  26.1 32.1 %copy-start.18 = (s32[256]{0:T(256)}, s32[256]{0:T(256)S(1)}, u32[]{:S(2)}) copy-start(s32[256]{0:T(256)S(1)} %get-tuple-element.49) | copy-start | bytes 3076
  26.1 32.1 %copy-start.19 = (s32[256]{0:T(256)}, s32[256]{0:T(256)S(1)}, u32[]{:S(2)}) copy-start(s32[256]{0:T(256)S(1)} %get-tuple-element.53) | copy-start | bytes 3076
  31.4 174.7 %all-gather.7.cloned.1.call-start = ((), (), s32[]{:S(2)}) async-start(), calls=%async_computation.2 | async-start | bytes 4866048 | tf_op jit(solution)/shard_map/all_gather | solution.py:374
  34.9 8.0 %copy-start.27 = (f32[256]{0:T(256)S(1)}, f32[256]{0:T(256)}, u32[]{:S(2)}) copy-start(f32[256]{0:T(256)} %add_rsqrt_fusion.7) | copy-start | bytes 3076
  34.9 215.0 %all-reduce.3.cloned.1.call-start = ((), (), s32[]{:S(2)}) async-start(), calls=%async_computation.1 | async-start | bytes 2621440 | tf_op jit(solution)/shard_map/psum | solution.py:381
  42.9 8.7 %copy-start.11 = (f32[256,64]{1,0:T(8,128)S(1)}, f32[256,64]{1,0:T(8,128)}, u32[]{:S(2)}) copy-start(f32[256,64]{1,0:T(8,128)} %copy-done.10) | copy-start | bytes 196612
  42.9 8.7 %copy-start.13 = (f32[256,64]{1,0:T(8,128)S(1)}, f32[256,64]{1,0:T(8,128)}, u32[]{:S(2)}) copy-start(f32[256,64]{1,0:T(8,128)} %copy-done.12) | copy-start | bytes 196612
  46.9 7.7 %copy-start.23 = (f32[128]{0:T(128)S(1)}, f32[128]{0:T(128)}, u32[]{:S(2)}) copy-start(f32[128]{0:T(128)} %param.53) | copy-start | bytes 1540
  46.9 8.1 %copy-start.24 = (f32[128]{0:T(128)S(1)}, f32[128]{0:T(128)}, u32[]{:S(2)}) copy-start(f32[128]{0:T(128)} %param.42) | copy-start | bytes 1540
  245.4 13.2 %copy-start.35 = (f32[2560]{0:T(1024)S(1)}, f32[2560]{0:T(1024)}, u32[]{:S(2)}) copy-start(f32[2560]{0:T(1024)} %param.45) | copy-start | bytes 30724
  249.9 3.2 collective-permute-start
  256.0 31.2 %collective-permute-start.1 = (bf16[256,2560]{1,0:T(8,128)(2,1)}, bf16[256,2560]{1,0:T(8,128)(2,1)}, u32[]{:S(2)}, u32[]{:S(2)}) collective-permute-start(bf16[256,2560]{1,0:T(8,128)(2,1)} %add_convert_fusion.1), channel_id=1, source_target_pairs={{0,2},{1,3},{2,0},{3,1},{4,6},{5,7},{6,4},{7,5},{8,10},{9,11},{10,... | collective-permute-start | bytes 3932168 | tf_op jit(solution)/shard_map/ppermute | solution.py:224
  258.7 28.5 %copy-start.4 = (bf16[256,2560]{1,0:T(8,128)(2,1)S(1)}, bf16[256,2560]{1,0:T(8,128)(2,1)}, u32[]{:S(2)}) copy-start(bf16[256,2560]{1,0:T(8,128)(2,1)} %param.32) | copy-start | bytes 3932164
  260.1 29.5 %copy-start.31 = (bf16[2560,640]{1,0:T(8,128)(2,1)S(1)}, bf16[2560,640]{1,0:T(8,128)(2,1)}, u32[]{:S(2)}) copy-start(bf16[2560,640]{1,0:T(8,128)(2,1)} %param.57) | copy-start | bytes 9830404
  260.1 29.5 %copy-start.36 = (f32[2560]{0:T(1024)S(1)}, f32[2560]{0:T(1024)}, u32[]{:S(2)}) copy-start(f32[2560]{0:T(1024)} %param.56) | copy-start | bytes 30724
  289.6 9.0 %copy-start.20 = (s32[256]{0:T(256)S(1)}, s32[256]{0:T(256)}, u32[]{:S(2)}) copy-start(s32[256]{0:T(256)} %get-tuple-element.29) | copy-start | bytes 3076
  289.6 9.6 %copy-start.21 = (s32[256]{0:T(256)S(1)}, s32[256]{0:T(256)}, u32[]{:S(2)}) copy-start(s32[256]{0:T(256)} %get-tuple-element.28) | copy-start | bytes 3076
  299.3 4.5 %collective-permute-start.4 = (f32[4]{0:T(128)S(1)}, f32[4]{0:T(128)S(1)}, u32[]{:S(2)}, u32[]{:S(2)}) collective-permute-start(f32[4]{0:T(128)S(1)} %select_reduce_fusion.1), channel_id=1, source_target_pairs={{0,12},{4,0},{8,4},{12,8},{16,28},{20,16},{24,20},{28,24},{32,44},... | collective-permute-start | bytes 56 | tf_op jit(solution)/shard_map/ppermute | solution.py:429
  302.1 5.1 %collective-permute-start.3 = (f32[4]{0:T(128)S(1)}, f32[4]{0:T(128)S(1)}, u32[]{:S(2)}, u32[]{:S(2)}) collective-permute-start(f32[4]{0:T(128)S(1)} %select_reduce_fusion.1), channel_id=1, source_target_pairs={{0,8},{4,12},{8,0},{12,4},{16,24},{20,28},{24,16},{28,20},{32,40},... | collective-permute-start | bytes 56 | tf_op jit(solution)/shard_map/ppermute | solution.py:429
  302.9 4.8 %collective-permute-start.2 = (f32[4]{0:T(128)S(1)}, f32[4]{0:T(128)S(1)}, u32[]{:S(2)}, u32[]{:S(2)}) collective-permute-start(f32[4]{0:T(128)S(1)} %select_reduce_fusion.1), channel_id=1, source_target_pairs={{0,4},{4,8},{8,12},{12,0},{16,20},{20,24},{24,28},{28,16},{32,36},... | collective-permute-start | bytes 56 | tf_op jit(solution)/shard_map/ppermute | solution.py:429
  307.7 4.5 %collective-permute-start.7 = (f32[4]{0:T(128)S(1)}, f32[4]{0:T(128)S(1)}, u32[]{:S(2)}, u32[]{:S(2)}) collective-permute-start(f32[4]{0:T(128)S(1)} %add_add_fusion.2), channel_id=1, source_target_pairs={{0,48},{4,52},{8,56},{12,60},{16,0},{20,4},{24,8},{28,12},{32,16},... | collective-permute-start | bytes 56 | tf_op jit(solution)/shard_map/ppermute | solution.py:429
  310.5 5.1 %collective-permute-start.6 = (f32[4]{0:T(128)S(1)}, f32[4]{0:T(128)S(1)}, u32[]{:S(2)}, u32[]{:S(2)}) collective-permute-start(f32[4]{0:T(128)S(1)} %add_add_fusion.2), channel_id=1, source_target_pairs={{0,32},{4,36},{8,40},{12,44},{16,48},{20,52},{24,56},{28,60},{32,0... | collective-permute-start | bytes 56 | tf_op jit(solution)/shard_map/ppermute | solution.py:429
  311.3 4.8 %collective-permute-start.5 = (f32[4]{0:T(128)S(1)}, f32[4]{0:T(128)S(1)}, u32[]{:S(2)}, u32[]{:S(2)}) collective-permute-start(f32[4]{0:T(128)S(1)} %add_add_fusion.2), channel_id=1, source_target_pairs={{0,16},{4,20},{8,24},{12,28},{16,32},{20,36},{24,40},{28,44},{32,4... | collective-permute-start | bytes 56 | tf_op jit(solution)/shard_map/ppermute | solution.py:429
  316.1 5.2 %collective-permute-start.8 = (f32[4]{0:T(128)S(1)}, f32[4]{0:T(128)S(1)}, u32[]{:S(2)}, u32[]{:S(2)}) collective-permute-start(f32[4]{0:T(128)S(1)} %add_add_fusion.1), channel_id=1, source_target_pairs={{0,64},{4,68},{8,72},{12,76},{16,80},{20,84},{24,88},{28,92},{32,9... | collective-permute-start | bytes 56 | tf_op jit(solution)/shard_map/ppermute | solution.py:429
  (17 other events, 38.0 us)
Sparse Core Ops, SparseCore 0:
  31.5 89.9 all-gather.4
  124.5 81.4 all-gather.6
  208.6 41.3 all-reduce.2

commit v12 on v11

--- a/solution.py
+++ b/solution.py
@@ -151,7 +151,7 @@
     return fold_pieces
 
 
-Q_TILE = 512
+Q_TILE = 1024
 K_TILE = 1024
 CODE_STRIDE = 65536
 

time: 330 us -> 330 us (level)
  transfers between devices with their start and end apart: 12 -> 12, of which waited for: 10 -> 10; matrix products, arithmetic and copies ran while one was open for 23% -> 23% of each run, Pallas kernels for 22% -> 23%
where the time goes in v12:
time: 330 us; the launch traced here: 328 us
  waiting for transfers between devices  111 us (34%)
  Pallas kernels  75.8 us (23%)
  other arithmetic  52.7 us (16%)
  local copies, waits for them, and re-layouts  28.9 us (9%)
  matrix products  28.1 us (9%)
  between operations  14.3 us (4%)
  starting transfers between devices  12.5 us (4%)
  blocking collectives  5.19 us (2%)
    pallas_call x2, Pallas kernels, flash_attend(): pl.pallas_call(flash_kernel, grid_spec=grid_spec, out_shape=jax.ShapeDtyp...  75.8 us
    all_gather x1, waiting for transfers between devices, local(): lax.all_gather(jnp.concatenate([policy_stack, carrier], axis=0), 'seq', a...  56.6 us
    ppermute x2, waiting for transfers between devices, exchange_sum(): lax.ppermute(values, axis_name, [(i, i ^ stride) for i in range(count)])  30.1 us
    ppermute x7, starting transfers between devices, local(): received = lax.ppermute(rollout_mean, 'seq', pairs)  11.9 us
    all_gather x1, waiting for transfers between devices, local(): lax.all_gather(reference_stack, 'seq', axis=0, tiled=True)  11.1 us
    reduce_sum x6, other arithmetic, rms_scale(): jnp.mean(values * values, axis=-1, keepdims=True) + EPSILON  10.8 us
    ppermute x7, waiting for transfers between devices, local(): received = lax.ppermute(rollout_mean, 'seq', pairs)  10 us
    reshape x4, local copies, waits for them, and re-layouts, project(): jnp.dot(normed, query_weight, preferred_element_type=jnp.float32)  8.09 us
  transfers between devices with their start and end apart: 12, of which 10 were waited for; matrix products, arithmetic and copies ran while one was open for 23% of the time, Pallas kernels for 23%

profile of v12, /device:TPU:0, one launch (start us, length us, event | category | flops | bytes accessed | tf_op | source)
XLA Modules:
  0.0 328.4 jit_solution(6827136872539969974)
XLA Ops:
  16.1 2.8 convolution_convert_fusion.2
  18.9 2.6 multiply_reduce_fusion.5
  31.4 2.1 convolution_convert_fusion.1
  35.0 3.9 %fusion.82 = f32[256,512]{1,0:T(8,128)} fusion(bf16[2560,512]{1,0:T(8,128)(2,1)} %param.50, bf16[256,2560]{1,0:T(8,128)(2,1)} %param.32, f32[2560]{0:T(1024)} %param.49, f32[256]{0:T(256)} %copy-done.28), kind=kOutput, calls=%fused_computation.222 | convolution fusion | flops 673710080 | bytes 4467712 | tf_op jit(solution)/shard_map/dot_general | solution.py:56
  38.9 2.0 reshape.564
  40.9 2.0 reshape.563
  42.9 4.0 %fusion.84 = f32[256,512]{1,0:T(8,128)} fusion(bf16[2560,512]{1,0:T(8,128)(2,1)} %param.39, bf16[256,2560]{1,0:T(8,128)(2,1)} %param.31, f32[2560]{0:T(1024)} %param.38, f32[256]{0:T(256)S(1)} %copy-done.27), kind=kOutput, calls=%fused_computation.223 | convolution fusion | flops 673710080 | bytes 4467712 | tf_op jit(solution)/shard_map/dot_general | solution.py:56
  46.9 2.0 reshape.559
  48.9 2.0 reshape.558
  61.8 3.1 fusion.77
  64.9 56.6 %all-gather.5.cloned.1.call-done.kv_ref = bf16[10240,256]{1,0:T(8,128)(2,1)} async-done(((bf16[320,256]{1,0:T(8,128)(2,1)}), bf16[10240,256]{1,0:T(8,128)(2,1)}) %all-gather.5.cloned.1.call-update) | async-done | bytes 5242896 | tf_op jit(solution)/shard_map/all_gather | solution.py:339
  139.2 3.7 %and_reduce_fusion = pred[10]{0:T(512)(128)(4,1)S(1)} fusion(s32[10,1024]{1,0:T(8,128)} %ge.64, s32[256]{0:T(256)} %copy-done.18, s32[256]{0:T(256)} %copy-done.19), kind=kLoop, calls=%fused_computation | loop fusion | flops 10485750 | bytes 43018 | tf_op jit(solution)/shard_map/reduce_or | solution.py:232
  143.4 39.7 %shard_map.284 = bf16[1024,128]{1,0:T(8,128)(2,1)} custom-call(s32[10]{0:T(128)} %convert_element_type.132.flags_ref, bf16[1024,128]{1,0:T(8,128)(2,1)} %bitcast.121, bf16[10240,256]{1,0:T(8,128)(2,1)} %all-gather.5.cloned.1.call-done.kv_ref, s32[1,10240]{1,0:T(1,128)} %broadcast_in_dim_reshape.4.kcode_ref, s32[1024,1]{1,0:T(8,128)} %bitcast.117, ...), custom_call_target="tpu_custom_call" | custom-call | tf_op jit(solution)/shard_map/pallas_call | solution.py:212
  185.0 3.8 %convolution_convert_fusion = bf16[256,2560]{1,0:T(8,128)(2,1)} fusion(bf16[256,512]{0,1:T(8,128)(2,1)} %bitcast.125, bf16[512,2560]{1,0:T(8,128)(2,1)} %param.44), kind=kOutput, calls=%fused_computation.8 | convolution fusion | flops 671744000 | bytes 4194304 | tf_op jit(solution)/shard_map/dot_general | solution.py:243
  191.1 3.3 %and_reduce_fusion.1 = pred[9]{0:T(512)(128)(4,1)S(1)} fusion(s32[9,1024]{1,0:T(8,128)S(1)} %ge.68, s32[256]{0:T(256)} %copy-done.18, s32[256]{0:T(256)} %copy-done.19), kind=kLoop, calls=%fused_computation.1 | loop fusion | flops 9437175 | bytes 38921 | tf_op jit(solution)/shard_map/reduce_or | solution.py:232
  194.9 11.1 %all-gather.7.cloned.1.call-done.kv_ref = bf16[9216,256]{1,0:T(8,128)(2,1)} async-done(((bf16[288,256]{1,0:T(8,128)(2,1)}), bf16[9216,256]{1,0:T(8,128)(2,1)}) %all-gather.7.cloned.1.call-update) | async-done | bytes 4718608 | tf_op jit(solution)/shard_map/all_gather | solution.py:374
  206.0 36.1 %shard_map.285 = bf16[1024,128]{1,0:T(8,128)(2,1)} custom-call(s32[9]{0:T(128)} %convert_element_type.135.flags_ref, bf16[1024,128]{1,0:T(8,128)(2,1)} %bitcast.122, bf16[9216,256]{1,0:T(8,128)(2,1)} %all-gather.7.cloned.1.call-done.kv_ref, s32[1,9216]{1,0:T(1,128)} %broadcast_in_dim_reshape.5.kcode_ref, s32[1024,1]{1,0:T(8,128)} %bitcast.118, ...), custom_call_target="tpu_custom_call" | custom-call | tf_op jit(solution)/shard_map/pallas_call | solution.py:212
  243.2 3.7 %fusion.92 = bf16[256,2560]{1,0:T(8,128)(2,1)} fusion(bf16[256,512]{0,1:T(8,128)(2,1)S(1)} %bitcast.126, bf16[512,2560]{1,0:T(8,128)(2,1)} %param.55), kind=kOutput, calls=%fused_computation.228 | convolution fusion | flops 671088640 | bytes 4194304 | tf_op jit(solution)/shard_map/dot_general | solution.py:243
  246.9 3.1 all-reduce.3.cloned.1.call-done
  250.2 3.0 collective-permute-done
  253.2 2.8 add_convert_fusion.1
  256.3 2.4 multiply_reduce_fusion.1
  260.1 27.1 %collective-permute-done.1 = bf16[256,2560]{1,0:T(8,128)(2,1)} collective-permute-done((bf16[256,2560]{1,0:T(8,128)(2,1)}, bf16[256,2560]{1,0:T(8,128)(2,1)}, u32[]{:S(2)}, u32[]{:S(2)}) %collective-permute-start.1) | collective-permute-done | bytes 1310752 | tf_op jit(solution)/shard_map/ppermute | solution.py:224
  287.3 2.4 multiply_reduce_fusion
  289.7 3.2 fusion.91
  293.4 5.2 %all-gather.1 = f32[4,6,256]{2,1,0:T(8,128)S(1)} all-gather(f32[1,6,256]{2,1,0:T(8,128)S(1)} %bitcast.128), channel_id=2, replica_groups=mesh['seq'=32,'vocab'=4] {'vocab'}, dimensions={0}, use_global_device_ids=true | all-gather | bytes 30720 | tf_op jit(solution)/shard_map/all_gather | solution.py:400
  299.4 2.8 collective-permute-start.4
  303.9 3.4 %collective-permute-done.3 = f32[4]{0:T(128)S(1)} collective-permute-done((f32[4]{0:T(128)S(1)}, f32[4]{0:T(128)S(1)}, u32[]{:S(2)}, u32[]{:S(2)}) %collective-permute-start.3) | collective-permute-done | bytes 48 | tf_op jit(solution)/shard_map/ppermute | solution.py:429
  307.8 2.8 collective-permute-start.7
  312.3 3.4 %collective-permute-done.6 = f32[4]{0:T(128)S(1)} collective-permute-done((f32[4]{0:T(128)S(1)}, f32[4]{0:T(128)S(1)}, u32[]{:S(2)}, u32[]{:S(2)}) %collective-permute-start.6) | collective-permute-done | bytes 48 | tf_op jit(solution)/shard_map/ppermute | solution.py:429
  316.2 2.9 collective-permute-start.8
  319.1 2.2 collective-permute-done.8
  (173 shorter events, 63.1 us)
Async XLA Ops:
  7.2 251.5 %copy-start = (bf16[2560,640]{1,0:T(8,128)(2,1)S(1)}, bf16[2560,640]{1,0:T(8,128)(2,1)}, u32[]{:S(2)}) copy-start(bf16[2560,640]{1,0:T(8,128)(2,1)} %param.46) | copy-start | bytes 9830404
  7.2 8.0 %copy-start.34 = (f32[2560]{0:T(1024)S(1)}, f32[2560]{0:T(1024)}, u32[]{:S(2)}) copy-start(f32[2560]{0:T(1024)} %param.49) | copy-start | bytes 30724
  7.2 114.3 %all-gather.5.cloned.1.call-start = ((), (), s32[]{:S(2)}) async-start(), calls=%async_computation | async-start | bytes 5406720 | tf_op jit(solution)/shard_map/all_gather | solution.py:339
  10.5 12.7 %copy-start.25 = (s32[4,1]{0,1:T(1,128)}, s32[4,1]{0,1:T(1,128)S(1)}, u32[]{:S(2)}) copy-start(s32[4,1]{0,1:T(1,128)S(1)} %reduce-window.8) | copy-start | bytes 52
  10.5 4.7 %copy-start.32 = (bf16[2560,128]{1,0:T(8,128)(2,1)S(1)}, bf16[2560,128]{1,0:T(8,128)(2,1)}, u32[]{:S(2)}) copy-start(bf16[2560,128]{1,0:T(8,128)(2,1)} %param.51) | copy-start | bytes 1966084
  11.3 12.7 %copy-start.26 = (s32[4]{0:T(128)}, s32[4]{0:T(128)S(1)}, u32[]{:S(2)}) copy-start(s32[4]{0:T(128)S(1)} %bitcast_subtract_fusion.1) | copy-start | bytes 52
  16.1 10.0 %copy-start.22 = (f32[128]{0:T(128)S(1)}, f32[128]{0:T(128)}, u32[]{:S(2)}) copy-start(f32[128]{0:T(128)} %param.54) | copy-start | bytes 1540
  22.5 7.4 %copy-start.17 = (bf16[256,128]{1,0:T(8,128)(2,1)S(1)}, bf16[256,128]{1,0:T(8,128)(2,1)}, u32[]{:S(2)}) copy-start(bf16[256,128]{1,0:T(8,128)(2,1)} %convolution_convert_fusion.2) | copy-start | bytes 196612
  26.1 32.1 %copy-start.18 = (s32[256]{0:T(256)}, s32[256]{0:T(256)S(1)}, u32[]{:S(2)}) copy-start(s32[256]{0:T(256)S(1)} %get-tuple-element.49) | copy-start | bytes 3076
  26.1 32.1 %copy-start.19 = (s32[256]{0:T(256)}, s32[256]{0:T(256)S(1)}, u32[]{:S(2)}) copy-start(s32[256]{0:T(256)S(1)} %get-tuple-element.53) | copy-start | bytes 3076
  31.4 174.7 %all-gather.7.cloned.1.call-start = ((), (), s32[]{:S(2)}) async-start(), calls=%async_computation.2 | async-start | bytes 4866048 | tf_op jit(solution)/shard_map/all_gather | solution.py:374
  34.9 8.0 %copy-start.27 = (f32[256]{0:T(256)S(1)}, f32[256]{0:T(256)}, u32[]{:S(2)}) copy-start(f32[256]{0:T(256)} %add_rsqrt_fusion.7) | copy-start | bytes 3076
  34.9 215.1 %all-reduce.3.cloned.1.call-start = ((), (), s32[]{:S(2)}) async-start(), calls=%async_computation.1 | async-start | bytes 2621440 | tf_op jit(solution)/shard_map/psum | solution.py:381
  42.9 8.7 %copy-start.11 = (f32[256,64]{1,0:T(8,128)S(1)}, f32[256,64]{1,0:T(8,128)}, u32[]{:S(2)}) copy-start(f32[256,64]{1,0:T(8,128)} %copy-done.10) | copy-start | bytes 196612
  42.9 8.7 %copy-start.13 = (f32[256,64]{1,0:T(8,128)S(1)}, f32[256,64]{1,0:T(8,128)}, u32[]{:S(2)}) copy-start(f32[256,64]{1,0:T(8,128)} %copy-done.12) | copy-start | bytes 196612
  46.9 7.7 %copy-start.23 = (f32[128]{0:T(128)S(1)}, f32[128]{0:T(128)}, u32[]{:S(2)}) copy-start(f32[128]{0:T(128)} %param.53) | copy-start | bytes 1540
  46.9 8.1 %copy-start.24 = (f32[128]{0:T(128)S(1)}, f32[128]{0:T(128)}, u32[]{:S(2)}) copy-start(f32[128]{0:T(128)} %param.42) | copy-start | bytes 1540
  246.9 11.7 %copy-start.35 = (f32[2560]{0:T(1024)S(1)}, f32[2560]{0:T(1024)}, u32[]{:S(2)}) copy-start(f32[2560]{0:T(1024)} %param.45) | copy-start | bytes 30724
  250.0 3.2 collective-permute-start
  256.0 31.2 %collective-permute-start.1 = (bf16[256,2560]{1,0:T(8,128)(2,1)}, bf16[256,2560]{1,0:T(8,128)(2,1)}, u32[]{:S(2)}, u32[]{:S(2)}) collective-permute-start(bf16[256,2560]{1,0:T(8,128)(2,1)} %add_convert_fusion.1), channel_id=1, source_target_pairs={{0,2},{1,3},{2,0},{3,1},{4,6},{5,7},{6,4},{7,5},{8,10},{9,11},{10,... | collective-permute-start | bytes 3932168 | tf_op jit(solution)/shard_map/ppermute | solution.py:224
  258.8 28.5 %copy-start.4 = (bf16[256,2560]{1,0:T(8,128)(2,1)S(1)}, bf16[256,2560]{1,0:T(8,128)(2,1)}, u32[]{:S(2)}) copy-start(bf16[256,2560]{1,0:T(8,128)(2,1)} %param.32) | copy-start | bytes 3932164
  260.1 29.5 %copy-start.31 = (bf16[2560,640]{1,0:T(8,128)(2,1)S(1)}, bf16[2560,640]{1,0:T(8,128)(2,1)}, u32[]{:S(2)}) copy-start(bf16[2560,640]{1,0:T(8,128)(2,1)} %param.57) | copy-start | bytes 9830404
  260.1 29.5 %copy-start.36 = (f32[2560]{0:T(1024)S(1)}, f32[2560]{0:T(1024)}, u32[]{:S(2)}) copy-start(f32[2560]{0:T(1024)} %param.56) | copy-start | bytes 30724
  289.7 9.0 %copy-start.20 = (s32[256]{0:T(256)S(1)}, s32[256]{0:T(256)}, u32[]{:S(2)}) copy-start(s32[256]{0:T(256)} %get-tuple-element.29) | copy-start | bytes 3076
  289.7 9.6 %copy-start.21 = (s32[256]{0:T(256)S(1)}, s32[256]{0:T(256)}, u32[]{:S(2)}) copy-start(s32[256]{0:T(256)} %get-tuple-element.28) | copy-start | bytes 3076
  299.4 4.5 %collective-permute-start.4 = (f32[4]{0:T(128)S(1)}, f32[4]{0:T(128)S(1)}, u32[]{:S(2)}, u32[]{:S(2)}) collective-permute-start(f32[4]{0:T(128)S(1)} %select_reduce_fusion.1), channel_id=1, source_target_pairs={{0,12},{4,0},{8,4},{12,8},{16,28},{20,16},{24,20},{28,24},{32,44},... | collective-permute-start | bytes 56 | tf_op jit(solution)/shard_map/ppermute | solution.py:429
  302.2 5.1 %collective-permute-start.3 = (f32[4]{0:T(128)S(1)}, f32[4]{0:T(128)S(1)}, u32[]{:S(2)}, u32[]{:S(2)}) collective-permute-start(f32[4]{0:T(128)S(1)} %select_reduce_fusion.1), channel_id=1, source_target_pairs={{0,8},{4,12},{8,0},{12,4},{16,24},{20,28},{24,16},{28,20},{32,40},... | collective-permute-start | bytes 56 | tf_op jit(solution)/shard_map/ppermute | solution.py:429
  303.0 4.8 %collective-permute-start.2 = (f32[4]{0:T(128)S(1)}, f32[4]{0:T(128)S(1)}, u32[]{:S(2)}, u32[]{:S(2)}) collective-permute-start(f32[4]{0:T(128)S(1)} %select_reduce_fusion.1), channel_id=1, source_target_pairs={{0,4},{4,8},{8,12},{12,0},{16,20},{20,24},{24,28},{28,16},{32,36},... | collective-permute-start | bytes 56 | tf_op jit(solution)/shard_map/ppermute | solution.py:429
  307.8 4.5 %collective-permute-start.7 = (f32[4]{0:T(128)S(1)}, f32[4]{0:T(128)S(1)}, u32[]{:S(2)}, u32[]{:S(2)}) collective-permute-start(f32[4]{0:T(128)S(1)} %add_add_fusion.2), channel_id=1, source_target_pairs={{0,48},{4,52},{8,56},{12,60},{16,0},{20,4},{24,8},{28,12},{32,16},... | collective-permute-start | bytes 56 | tf_op jit(solution)/shard_map/ppermute | solution.py:429
  310.5 5.1 %collective-permute-start.6 = (f32[4]{0:T(128)S(1)}, f32[4]{0:T(128)S(1)}, u32[]{:S(2)}, u32[]{:S(2)}) collective-permute-start(f32[4]{0:T(128)S(1)} %add_add_fusion.2), channel_id=1, source_target_pairs={{0,32},{4,36},{8,40},{12,44},{16,48},{20,52},{24,56},{28,60},{32,0... | collective-permute-start | bytes 56 | tf_op jit(solution)/shard_map/ppermute | solution.py:429
  311.4 4.8 %collective-permute-start.5 = (f32[4]{0:T(128)S(1)}, f32[4]{0:T(128)S(1)}, u32[]{:S(2)}, u32[]{:S(2)}) collective-permute-start(f32[4]{0:T(128)S(1)} %add_add_fusion.2), channel_id=1, source_target_pairs={{0,16},{4,20},{8,24},{12,28},{16,32},{20,36},{24,40},{28,44},{32,4... | collective-permute-start | bytes 56 | tf_op jit(solution)/shard_map/ppermute | solution.py:429
  316.2 5.2 %collective-permute-start.8 = (f32[4]{0:T(128)S(1)}, f32[4]{0:T(128)S(1)}, u32[]{:S(2)}, u32[]{:S(2)}) collective-permute-start(f32[4]{0:T(128)S(1)} %add_add_fusion.1), channel_id=1, source_target_pairs={{0,64},{4,68},{8,72},{12,76},{16,80},{20,84},{24,88},{28,92},{32,9... | collective-permute-start | bytes 56 | tf_op jit(solution)/shard_map/ppermute | solution.py:429
  (17 other events, 38.0 us)
Sparse Core Ops, SparseCore 0:
  31.5 89.9 all-gather.4
  124.5 81.4 all-gather.6
  208.6 41.3 all-reduce.2
